TPU v7x, 256 devices: a whole 4x4x8 slice. The times are simulated.
256 devices in a mesh: tile: 16 (over y, z_hi), spec: 16 (over x, z_lo, core).
Axes of the slice: x: 4, y: 4, z: 8 (z_hi: 4, z_lo: 2; z = z_hi * 2 + z_lo), core: 2. Of those that a mesh axis runs over, the one named last changes fastest.
Arguments:
- latent: bfloat16 [32, 4096, 1024], P(None, ('tile', 'spec')), may hold values from -6 to 6
- basis: bfloat16 [224, 32], replicated, may hold values from -1 to 1
- response: bfloat16 [8, 224], replicated, may hold values from -0.375 to 0.375
- hyper_obs: bfloat16 [224, 1024, 256], P('spec', 'tile'), may hold values from -6 to 6
- multi_obs: bfloat16 [8, 4096, 1024], P(None, ('tile', 'spec')), may hold values from -6 to 6
Outputs:
- z_next: bfloat16 [32, 4096, 1024], P(None, ('tile', 'spec'))
- hs_residual: bfloat16 [224, 1024, 256], P('spec', 'tile')
All inputs are finite; a program needn't handle non-finite values.
Results may differ from a plain program's by a relative error of at most 0.0054.
Values may be sent and summed in bfloat16 or wider, within the bound.
No kernel may reach another device: no remote copies, remote signals or barrier semaphores. Data moves between devices by JAX's collectives and lax.ppermute only.
A program may use at most 128 MiB of HBM per device.

v0:
```python
import jax
import jax.numpy as jnp
from jax import lax
from jax.sharding import PartitionSpec as P

DECIM = 4
HALO = 128


step_size = 0.3


def with_halo(cells, sides, width):
    for axis, dim in sides:
        count = lax.axis_size(axis)
        ends = count - 1
        head = lax.slice_in_dim(cells, 0, width, axis=dim)
        tail = lax.slice_in_dim(cells, cells.shape[dim] - width, cells.shape[dim], axis=dim)
        cells = jnp.concatenate(
            [
                lax.ppermute(tail, axis, [(i, (i + 1) % count) for i in range(ends)]),
                cells,
                lax.ppermute(head, axis, [((i + 1) % count, i) for i in range(ends)]),
            ],
            axis=dim,
        )
    return cells


def profile(where_at):
    narrow = DECIM / 2.0
    decay_len = 3.0 * HALO / 8.0
    ripple = jnp.cos(where_at * (jnp.pi / 7.0))
    return (
        jnp.exp(-where_at * where_at / (2.0 * narrow * narrow))
        + 0.5 * jnp.exp(-jnp.abs(where_at) / decay_len) * ripple * ripple
    )


def kernel_values(offsets):
    every_offset = jnp.arange(-HALO, HALO + 1).astype(jnp.float32)
    energy = jnp.sqrt(jnp.sum(profile(every_offset) ** 2))
    inside = jnp.abs(offsets) <= HALO
    return jnp.where(inside, profile(offsets.astype(jnp.float32)) / energy, 0.0).astype(
        jnp.bfloat16
    )


def column_matrix(fine_count, coarse_count):
    fine_cols = jnp.arange(fine_count)[:, None]
    coarse = jnp.arange(coarse_count)[None, :]
    return kernel_values(fine_cols - DECIM * coarse)


def row_matrix(rows_local):
    coarse = jnp.arange(rows_local // DECIM)[:, None]
    padded = jnp.arange(rows_local + 2 * HALO)[None, :]
    return kernel_values(padded - HALO - DECIM * coarse)


def back_matrix(rows_local):
    fine_rows = jnp.arange(rows_local)[:, None]
    coarse = jnp.arange(rows_local // DECIM + 2 * (HALO // DECIM))[None, :]
    return kernel_values(fine_rows - DECIM * coarse + HALO)


def shards(latent, basis, response, hyper_obs, multi_obs):
    highest = lax.Precision.HIGHEST
    rows_dev = hyper_obs.shape[1] * DECIM
    width_cols = latent.shape[2]
    spectra = jnp.einsum("bk,krc->brc", basis, latent, preferred_element_type=jnp.float32).astype(
        jnp.bfloat16
    )
    column_kernel = column_matrix(width_cols, width_cols // DECIM)
    column_wide = column_kernel.astype(jnp.float32)
    band_cube = lax.all_to_all(spectra, "spec", split_axis=0, concat_axis=1, tiled=True)
    padded = with_halo(band_cube, (("tile", 1),), HALO)
    rows_done = jnp.einsum(
        "ir,brc->bic", row_matrix(rows_dev), padded, preferred_element_type=jnp.float32
    )
    blurred = jnp.einsum("bic,cj->bij", rows_done, column_wide, precision=highest)
    hs_residual = (blurred - hyper_obs.astype(jnp.float32)).astype(jnp.bfloat16)
    coarse_padded = with_halo(hs_residual, (("tile", 1),), HALO // DECIM)
    rows_back = jnp.einsum(
        "rq,bqj->brj", back_matrix(rows_dev), coarse_padded, preferred_element_type=jnp.float32
    )
    multi_resid = (
        jnp.einsum("mb,brc->mrc", response, spectra, preferred_element_type=jnp.float32)
        - multi_obs.astype(jnp.float32)
    ).astype(jnp.bfloat16)
    spread = jnp.einsum("brj,cj->brc", rows_back, column_wide, precision=highest).astype(
        jnp.bfloat16
    )
    spread_pixel = lax.all_to_all(spread, "spec", split_axis=1, concat_axis=0, tiled=True)
    multi_back = jnp.einsum(
        "mb,mrc->brc", response, multi_resid, preferred_element_type=jnp.float32
    )
    spectral = (spread_pixel.astype(jnp.float32) + multi_back).astype(jnp.bfloat16)
    gradient = jnp.einsum("bk,brc->krc", basis, spectral, preferred_element_type=jnp.float32)
    z_next = (latent.astype(jnp.float32) - step_size * gradient).astype(jnp.bfloat16)
    return (z_next, hs_residual)


def solution(mesh):
    in_specs = (
        P(None, ("tile", "spec"), None),
        P(),
        P(),
        P("spec", "tile", None),
        P(None, ("tile", "spec"), None),
    )
    out_specs = (P(None, ("tile", "spec"), None), P("spec", "tile", None))
    return jax.shard_map(shards, mesh=mesh, in_specs=in_specs, out_specs=out_specs, check_vma=False)
```

profile of v0, /device:TPU:24, one launch (start us, length us, event | category | flops | bytes accessed | tf_op | source)
XLA Modules:
  0.0 483.7 jit_solution(12088717307099178395)
XLA Ops:
  1.4 3.3 convolution_convert_fusion.1
  4.7 7.1 %copy.30 = bf16[224,16,1024]{2,1,0:T(8,128)(2,1)} copy(bf16[224,16,1024]{2,0,1:T(8,128)(2,1)S(1)} %convolution_convert_fusion.1) | data formatting | bytes 14680064 | tf_op jit(solution)/shard_map/convert_element_type | solution.py:71
  11.8 89.8 %all_to_all.27 = bf16[224,16,1024]{2,1,0:T(8,128)(2,1)} all-to-all(bf16[224,16,1024]{2,1,0:T(8,128)(2,1)} %copy.30), channel_id=1, replica_groups=mesh['tile'=16,'spec'=16] {'spec'}, dimensions={0} | all-to-all | bytes 14680064 | tf_op jit(solution)/shard_map/all_to_all | solution.py:76
  101.6 4.7 copy.31
  106.3 4.8 fusion.119
  112.0 5.2 %collective-permute-start = (bf16[14,128,1024]{2,1,0:T(8,128)(2,1)}, bf16[14,128,1024]{2,1,0:T(8,128)(2,1)}, u32[]{:S(2)}, u32[]{:S(2)}) collective-permute-start(bf16[14,128,1024]{2,1,0:T(8,128)(2,1)} %get-tuple-element.10), channel_id=1, source_target_pairs={{0,16},{16,32},{32,48},{48,64},{64,80},{80,96},{96,112},{112,128},... | collective-permute-start | bytes 11010056 | tf_op jit(solution)/shard_map/ppermute | solution.py:21
  117.2 4.4 collective-permute-start.1
  123.0 76.3 %collective-permute-done = bf16[14,128,1024]{2,1,0:T(8,128)(2,1)} collective-permute-done((bf16[14,128,1024]{2,1,0:T(8,128)(2,1)}, bf16[14,128,1024]{2,1,0:T(8,128)(2,1)}, u32[]{:S(2)}, u32[]{:S(2)}) %collective-permute-start) | collective-permute-done | bytes 3670048 | tf_op jit(solution)/shard_map/ppermute | solution.py:21
  199.3 66.4 %collective-permute-done.1 = bf16[14,128,1024]{2,1,0:T(8,128)(2,1)} collective-permute-done((bf16[14,128,1024]{2,1,0:T(8,128)(2,1)}, bf16[14,128,1024]{2,1,0:T(8,128)(2,1)}, u32[]{:S(2)}, u32[]{:S(2)}) %collective-permute-start.1) | collective-permute-done | bytes 3670048 | tf_op jit(solution)/shard_map/ppermute | solution.py:23
  265.7 8.2 %fusion = f32[14,1024,64]{1,2,0:T(8,128)S(1)} fusion(bf16[14,128,1024]{2,1,0:T(8,128)(2,1)} %collective-permute-done.1, bf16[14,256,1024]{2,1,0:T(8,128)(2,1)} %bitcast.62, bf16[14,128,1024]{2,1,0:T(8,128)(2,1)} %collective-permute-done, f32[]{:T(128)S(6)} %sqrt.2, s32[64]{0:T(128)S(1)} %iota_multiply_fusion.2, s32[512]{0:T(512)S(1)} %iota_add_fusion), kind=kOutput, calls=%fused_computation | convolution fusion | flops 984154112 | bytes 18352388 | tf_op jit(solution)/shard_map/ir,brc->bic/dot_general | solution.py:78
  274.0 5.9 %fusion.15 = bf16[14,64,256]{2,1,0:T(8,128)(2,1)S(1)} fusion(f32[14,1024,64]{1,2,0:T(8,128)S(1)} %fusion, bf16[14,64,256]{2,1,0:T(8,128)(2,1)S(1)} %copy-done.7, f32[]{:T(128)S(6)} %sqrt.2, s32[256]{0:T(256)S(1)} %iota_multiply_fusion), kind=kOutput, calls=%fused_computation.20 | convolution fusion | flops 2823979008 | bytes 4588548 | tf_op jit(solution)/shard_map/bic,cj->bij/dot_general | solution.py:81
  279.9 13.9 %collective-permute-start.2 = (bf16[14,32,256]{2,1,0:T(8,128)(2,1)S(1)}, bf16[14,32,256]{2,1,0:T(8,128)(2,1)S(1)}, u32[]{:S(2)}, u32[]{:S(2)}) collective-permute-start(bf16[14,32,256]{2,1,0:T(8,128)(2,1)S(1)} %get-tuple-element.12), channel_id=1, source_target_pairs={{0,16},{16,32},{32,48},{48,64},{64,80},{80,96},{96,112},{112,128},... | collective-permute-start | bytes 688136 | tf_op jit(solution)/shard_map/ppermute | solution.py:21
  293.9 2.1 collective-permute-start.3
  297.4 7.0 %collective-permute-done.3 = bf16[14,32,256]{2,1,0:T(8,128)(2,1)S(1)} collective-permute-done((bf16[14,32,256]{2,1,0:T(8,128)(2,1)S(1)}, bf16[14,32,256]{2,1,0:T(8,128)(2,1)S(1)}, u32[]{:S(2)}, u32[]{:S(2)}) %collective-permute-start.3) | collective-permute-done | bytes 229408 | tf_op jit(solution)/shard_map/ppermute | solution.py:23
  305.6 16.4 %convolution_convert_fusion = bf16[14,256,1024]{2,1,0:T(8,128)(2,1)S(1)} fusion(f32[14,256,256]{2,1,0:T(8,128)S(1)} %fusion.27, f32[]{:T(128)S(6)} %sqrt.2, s32[256]{0:T(256)S(1)} %iota_multiply_fusion), kind=kOutput, calls=%fused_computation.9 | convolution fusion | flops 11282677760 | bytes 11011076 | tf_op jit(solution)/shard_map/brj,cj->brc/dot_general | solution.py:91
  322.0 7.5 %copy.34 = bf16[14,256,1024]{2,0,1:T(8,128)(2,1)} copy(bf16[14,256,1024]{2,1,0:T(8,128)(2,1)S(1)} %convolution_convert_fusion) | data formatting | bytes 14680064 | tf_op jit(solution)/shard_map/convert_element_type | solution.py:91
  329.5 12.4 %all-to-all-start.1 = ((bf16[14,256,1024]{2,0,1:T(8,128)(2,1)}), bf16[14,256,1024]{2,0,1:T(8,128)(2,1)}, u32[]{:S(2)}, u32[]{:S(2)}) async-start(bf16[14,256,1024]{2,0,1:T(8,128)(2,1)} %copy.34), calls=%async_computation.1 | async-start | bytes 16777216 | tf_op jit(solution)/shard_map/all_to_all | solution.py:94
  342.0 5.0 %fusion.19 = bf16[8,16,1024]{2,0,1:T(8,128)(2,1)S(1)} fusion(bf16[224,16,1024]{2,0,1:T(8,128)(2,1)} %copy-done.1, bf16[8,16,1024]{2,1,0:T(8,128)(2,1)S(1)} %copy-done.5, bf16[8,224]{1,0:T(8,128)(2,1)S(1)} %copy-done.6), kind=kOutput, calls=%fused_computation.23 | convolution fusion | flops 59113472 | bytes 7867904 | tf_op jit(solution)/shard_map/mb,brc->mrc/dot_general | solution.py:88
  346.9 89.9 %all-to-all-done.1 = bf16[14,256,1024]{2,0,1:T(8,128)(2,1)} async-done(((bf16[14,256,1024]{2,0,1:T(8,128)(2,1)}), bf16[14,256,1024]{2,0,1:T(8,128)(2,1)}, u32[]{:S(2)}, u32[]{:S(2)}) %all-to-all-start.1) | async-done | bytes 7340064 | tf_op jit(solution)/shard_map/all_to_all | solution.py:94
  436.9 7.5 %copy.35 = bf16[14,256,1024]{2,1,0:T(8,128)(2,1)S(1)} copy(bf16[14,256,1024]{2,0,1:T(8,128)(2,1)} %all-to-all-done.1) | data formatting | bytes 14680064 | tf_op jit(solution)/shard_map/all_to_all | solution.py:94
  444.4 7.1 %convert_bitcast_fusion = f32[16,14,16,1024]{3,2,0,1:T(8,128)} fusion(bf16[14,16,16,1024]{3,2,1,0:T(8,128)(2,1)S(1)} %bitcast.64), kind=kLoop, calls=%fused_computation.6 | loop fusion | flops 3670016 | bytes 22020096 | tf_op jit(solution)/shard_map/convert_element_type | solution.py:98
  451.5 13.7 %copy.36 = f32[16,14,16,1024]{3,2,1,0:T(8,128)} copy(f32[16,14,16,1024]{3,2,0,1:T(8,128)} %convert_bitcast_fusion) | data formatting | bytes 29360128 | tf_op jit(solution)/shard_map/convert_element_type | solution.py:98
  465.1 16.8 %fusion.11 = bf16[32,16,1024]{2,0,1:T(8,128)(2,1)S(1)} fusion(f32[224,16,1024]{2,1,0:T(8,128)} %bitcast.60, bf16[8,16,1024]{2,0,1:T(8,128)(2,1)S(1)} %fusion.19, bf16[32,16,1024]{2,1,0:T(8,128)(2,1)S(1)} %copy-done.3, bf16[224,32]{0,1:T(8,128)(2,1)S(1)} %copy-done, bf16[8,224]{1,0:T(8,128)(2,1)S(1)} %copy-done.6), kind=kOutput, calls=%fused_computation.16 | convolution fusion | flops 303038464 | bytes 17057280 | tf_op jit(solution)/shard_map/bk,brc->krc/dot_general | solution.py:99
  482.0 1.5 copy.39
  (24 shorter events, 4.8 us)
Async XLA Ops:
  0.6 0.7 copy-start
  4.7 7.1 %copy-start.1 = (bf16[224,16,1024]{2,0,1:T(8,128)(2,1)}, bf16[224,16,1024]{2,0,1:T(8,128)(2,1)S(1)}, u32[]{:S(2)}) copy-start(bf16[224,16,1024]{2,0,1:T(8,128)(2,1)S(1)} %convolution_convert_fusion.1) | copy-start | bytes 22020100
  106.3 5.7 %copy-start.2 = (bf16[14,16,16,1024]{3,2,1,0:T(8,128)(2,1)}, bf16[14,16,16,1024]{3,2,1,0:T(8,128)(2,1)S(1)}, u32[]{:S(2)}) copy-start(bf16[14,16,16,1024]{3,2,1,0:T(8,128)(2,1)S(1)} %copy.31) | copy-start | bytes 22020100
  112.0 87.3 %collective-permute-start = (bf16[14,128,1024]{2,1,0:T(8,128)(2,1)}, bf16[14,128,1024]{2,1,0:T(8,128)(2,1)}, u32[]{:S(2)}, u32[]{:S(2)}) collective-permute-start(bf16[14,128,1024]{2,1,0:T(8,128)(2,1)} %get-tuple-element.10), channel_id=1, source_target_pairs={{0,16},{16,32},{32,48},{48,64},{64,80},{80,96},{96,112},{112,128},... | collective-permute-start | bytes 11010056 | tf_op jit(solution)/shard_map/ppermute | solution.py:21
  117.2 148.6 %collective-permute-start.1 = (bf16[14,128,1024]{2,1,0:T(8,128)(2,1)}, bf16[14,128,1024]{2,1,0:T(8,128)(2,1)}, u32[]{:S(2)}, u32[]{:S(2)}) collective-permute-start(bf16[14,128,1024]{2,1,0:T(8,128)(2,1)} %get-tuple-element.11), channel_id=1, source_target_pairs={{16,0},{32,16},{48,32},{64,48},{80,64},{96,80},{112,96},{128,112},... | collective-permute-start | bytes 11010056 | tf_op jit(solution)/shard_map/ppermute | solution.py:23
  123.0 151.0 %copy-start.7 = (bf16[14,64,256]{2,1,0:T(8,128)(2,1)S(1)}, bf16[14,64,256]{2,1,0:T(8,128)(2,1)}, u32[]{:S(2)}) copy-start(bf16[14,64,256]{2,1,0:T(8,128)(2,1)} %param.8) | copy-start | bytes 1376260
  279.9 42.1 %copy-start.4 = (bf16[14,64,256]{2,1,0:T(8,128)(2,1)}, bf16[14,64,256]{2,1,0:T(8,128)(2,1)S(1)}, u32[]{:S(2)}) copy-start(bf16[14,64,256]{2,1,0:T(8,128)(2,1)S(1)} %fusion.15) | copy-start | bytes 1376260
  279.9 17.4 %collective-permute-start.2 = (bf16[14,32,256]{2,1,0:T(8,128)(2,1)S(1)}, bf16[14,32,256]{2,1,0:T(8,128)(2,1)S(1)}, u32[]{:S(2)}, u32[]{:S(2)}) collective-permute-start(bf16[14,32,256]{2,1,0:T(8,128)(2,1)S(1)} %get-tuple-element.12), channel_id=1, source_target_pairs={{0,16},{16,32},{32,48},{48,64},{64,80},{80,96},{96,112},{112,128},... | collective-permute-start | bytes 688136 | tf_op jit(solution)/shard_map/ppermute | solution.py:21
  293.9 10.5 %collective-permute-start.3 = (bf16[14,32,256]{2,1,0:T(8,128)(2,1)S(1)}, bf16[14,32,256]{2,1,0:T(8,128)(2,1)S(1)}, u32[]{:S(2)}, u32[]{:S(2)}) collective-permute-start(bf16[14,32,256]{2,1,0:T(8,128)(2,1)S(1)} %get-tuple-element.13), channel_id=1, source_target_pairs={{16,0},{32,16},{48,32},{64,48},{80,64},{96,80},{112,96},{128,112},... | collective-permute-start | bytes 688136 | tf_op jit(solution)/shard_map/ppermute | solution.py:23
  329.5 12.4 %copy-start.5 = (bf16[8,16,1024]{2,1,0:T(8,128)(2,1)S(1)}, bf16[8,16,1024]{2,1,0:T(8,128)(2,1)}, u32[]{:S(2)}) copy-start(bf16[8,16,1024]{2,1,0:T(8,128)(2,1)} %param.9) | copy-start | bytes 786436
  329.5 12.5 %copy-start.6 = (bf16[8,224]{1,0:T(8,128)(2,1)S(1)}, bf16[8,224]{1,0:T(8,128)(2,1)}, u32[]{:S(2)}) copy-start(bf16[8,224]{1,0:T(8,128)(2,1)} %param.7) | copy-start | bytes 10756
  329.5 107.4 %all-to-all-start.1 = ((bf16[14,256,1024]{2,0,1:T(8,128)(2,1)}), bf16[14,256,1024]{2,0,1:T(8,128)(2,1)}, u32[]{:S(2)}, u32[]{:S(2)}) async-start(bf16[14,256,1024]{2,0,1:T(8,128)(2,1)} %copy.34), calls=%async_computation.1 | async-start | bytes 16777216 | tf_op jit(solution)/shard_map/all_to_all | solution.py:94
  451.5 13.7 %copy-start.3 = (bf16[32,16,1024]{2,1,0:T(8,128)(2,1)S(1)}, bf16[32,16,1024]{2,1,0:T(8,128)(2,1)}, u32[]{:S(2)}) copy-start(bf16[32,16,1024]{2,1,0:T(8,128)(2,1)} %param.5) | copy-start | bytes 3145732
where the time goes:
time: 492 us; the launch traced here: 484 us
  waiting for transfers between devices  241 us (49%)
  blocking collectives  89.8 us (18%)
  matrix products  56.8 us (12%)
  local copies, waits for them, and re-layouts  48.5 us (10%)
  starting transfers between devices  38 us (8%)
  other arithmetic  7.76 us (2%)
    all_to_all x1, waiting for transfers between devices, shards(): lax.all_to_all(spread, 'spec', split_axis=1, concat_axis=0, tiled=True)  89.9 us
    all_to_all x1, blocking collectives, shards(): lax.all_to_all(spectra, 'spec', split_axis=0, concat_axis=1, tiled=True)  89.8 us
    ppermute x2, waiting for transfers between devices, with_halo(): lax.ppermute(tail, axis, [(i, (i + 1) % count) for i in range(ends)])  77.7 us
    ppermute x2, waiting for transfers between devices, with_halo(): lax.ppermute(head, axis, [((i + 1) % count, i) for i in range(ends)])  73.5 us
    ppermute x2, starting transfers between devices, with_halo(): lax.ppermute(tail, axis, [(i, (i + 1) % count) for i in range(ends)])  19.1 us
    dot_general x1, matrix products, shards(): jnp.einsum('bk,brc->krc', basis, spectral, preferred_element_type=jnp.flo...  16.8 us
    dot_general x1, matrix products, shards(): jnp.einsum('brj,cj->brc', rows_back, column_wide, precision=highest)  16.4 us
    convert_element_type x1, local copies, waits for them, and re-layouts, shards(): spread_pixel.astype(jnp.float32) + multi_back  13.7 us
  transfers between devices with their start and end apart: 5, of which 5 were waited for; matrix products, arithmetic and copies ran while one was open for 1% of the time, Pallas kernels for 0%

commit v1 on v0

--- a/solution.py
+++ b/solution.py
@@ -66,38 +66,45 @@
 
 def shards(latent, basis, response, hyper_obs, multi_obs):
     highest = lax.Precision.HIGHEST
+    f32 = jnp.float32
+    group = hyper_obs.shape[0]
     rows_dev = hyper_obs.shape[1] * DECIM
     width_cols = latent.shape[2]
-    spectra = jnp.einsum("bk,krc->brc", basis, latent, preferred_element_type=jnp.float32).astype(
-        jnp.bfloat16
+    spec_index = lax.axis_index("spec")
+    basis_wide = basis.astype(f32)
+    basis_own = lax.dynamic_slice_in_dim(basis_wide, spec_index * group, group, 0)
+    column_kernel = column_matrix(width_cols, width_cols // DECIM)
+    column_wide = column_kernel.astype(f32)
+
+    cols_done = jnp.einsum("qrc,cj->qrj", latent, column_kernel, preferred_element_type=f32)
+    coef_rows = lax.all_to_all(cols_done, "spec", split_axis=0, concat_axis=1, tiled=True)
+    padded = with_halo(coef_rows, (("tile", 1),), HALO)
+    coef_blurred = jnp.einsum(
+        "ir,qrj->qij", row_matrix(rows_dev).astype(f32), padded, precision=highest
     )
-    column_kernel = column_matrix(width_cols, width_cols // DECIM)
-    column_wide = column_kernel.astype(jnp.float32)
-    band_cube = lax.all_to_all(spectra, "spec", split_axis=0, concat_axis=1, tiled=True)
-    padded = with_halo(band_cube, (("tile", 1),), HALO)
-    rows_done = jnp.einsum(
-        "ir,brc->bic", row_matrix(rows_dev), padded, preferred_element_type=jnp.float32
+    coef_all = lax.all_gather(coef_blurred, "spec", axis=0, tiled=True)
+    blurred = jnp.einsum("bq,qij->bij", basis_own, coef_all, precision=highest)
+    hs_residual = (blurred - hyper_obs.astype(f32)).astype(jnp.bfloat16)
+
+    coef_part = jnp.einsum(
+        "bq,bij->qij", basis_own.astype(jnp.bfloat16), hs_residual, preferred_element_type=f32
     )
-    blurred = jnp.einsum("bic,cj->bij", rows_done, column_wide, precision=highest)
-    hs_residual = (blurred - hyper_obs.astype(jnp.float32)).astype(jnp.bfloat16)
-    coarse_padded = with_halo(hs_residual, (("tile", 1),), HALO // DECIM)
+    coef_resid = lax.psum_scatter(coef_part, "spec", scatter_dimension=0, tiled=True)
+    coarse_padded = with_halo(coef_resid, (("tile", 1),), HALO // DECIM)
     rows_back = jnp.einsum(
-        "rq,bqj->brj", back_matrix(rows_dev), coarse_padded, preferred_element_type=jnp.float32
+        "rq,cqj->crj", back_matrix(rows_dev).astype(f32), coarse_padded, precision=highest
     )
-    multi_resid = (
-        jnp.einsum("mb,brc->mrc", response, spectra, preferred_element_type=jnp.float32)
-        - multi_obs.astype(jnp.float32)
-    ).astype(jnp.bfloat16)
-    spread = jnp.einsum("brj,cj->brc", rows_back, column_wide, precision=highest).astype(
-        jnp.bfloat16
+    rows_pixel = lax.all_to_all(rows_back, "spec", split_axis=1, concat_axis=0, tiled=True)
+    grad_hs = jnp.einsum("qrj,cj->qrc", rows_pixel, column_wide, precision=highest)
+
+    resp_basis = jnp.dot(response.astype(f32), basis_wide, precision=highest)
+    multi_pred = jnp.einsum("mq,qrc->mrc", resp_basis, latent.astype(f32), precision=highest)
+    multi_resid = (multi_pred - multi_obs.astype(f32)).astype(jnp.bfloat16)
+    grad_ms = jnp.einsum(
+        "mq,mrc->qrc", resp_basis, multi_resid.astype(f32), precision=highest
     )
-    spread_pixel = lax.all_to_all(spread, "spec", split_axis=1, concat_axis=0, tiled=True)
-    multi_back = jnp.einsum(
-        "mb,mrc->brc", response, multi_resid, preferred_element_type=jnp.float32
-    )
-    spectral = (spread_pixel.astype(jnp.float32) + multi_back).astype(jnp.bfloat16)
-    gradient = jnp.einsum("bk,brc->krc", basis, spectral, preferred_element_type=jnp.float32)
-    z_next = (latent.astype(jnp.float32) - step_size * gradient).astype(jnp.bfloat16)
+    gradient = grad_hs + grad_ms
+    z_next = (latent.astype(f32) - step_size * gradient).astype(jnp.bfloat16)
     return (z_next, hs_residual)
 
 

time: 492 us -> 217 us (0.44); the launches traced: 484 us -> 215 us
  waiting for transfers between devices: 241 us -> 128 us
  blocking collectives: 89.8 us -> 16.4 us
  local copies, waits for them, and re-layouts: 48.5 us -> 7.24 us
  matrix products: 56.8 us -> 23 us
  between operations: 1.71 us -> 14.9 us
  starting transfers between devices: 38 us -> 24.9 us
  other arithmetic: 7.76 us -> 0.67 us
    all_to_all x1, waiting for transfers between devices: 89.9 us -> 7.2 us  [shards(): lax.all_to_all(rows_back, 'spec', split_axis=1, concat_axis=0, tiled=True)]
    all_to_all x1, blocking collectives: 89.8 us -> 16.4 us  [shards(): lax.all_to_all(cols_done, 'spec', split_axis=0, concat_axis=1, tiled=True)]
    ppermute x2, waiting for transfers between devices: 77.7 us -> 7.43 us  [with_halo(): lax.ppermute(tail, axis, [(i, (i + 1) % count) for i in range(ends)])]
    reduce_scatter x0 -> x1, waiting for transfers between devices: none -> 67.1 us  [shards(): lax.psum_scatter(coef_part, 'spec', scatter_dimension=0, tiled=True)]
    ppermute x2, waiting for transfers between devices: 73.5 us -> 10.5 us  [with_halo(): lax.ppermute(head, axis, [((i + 1) % count, i) for i in range(ends)])]
    all_gather x0 -> x1, waiting for transfers between devices: none -> 35.2 us  [shards(): coef_all = lax.all_gather(coef_blurred, 'spec', axis=0, tiled=True)]
    dot_general x7 -> x9, matrix products: 56.8 us -> 23 us  [the longest x1 7.25 us: shards(): jnp.einsum('qrj,cj->qrc', rows_pixel, column_wide, precision=highest)]
    convert_element_type x3 -> x0, local copies, waits for them, and re-layouts: 28.3 us -> none  [the longest x1 13.7 us: shards(): spread_pixel.astype(jnp.float32) + multi_back]
  transfers between devices with their start and end apart: 5 -> 7, of which waited for: 5 -> 7; matrix products, arithmetic and copies ran while one was open for 1% -> 2% of each run, Pallas kernels for 0% -> 0%
where the time goes in v1:
time: 217 us; the launch traced here: 215 us
  waiting for transfers between devices  128 us (59%)
  starting transfers between devices  24.9 us (11%)
  matrix products  23 us (11%)
  blocking collectives  16.4 us (8%)
  between operations  14.9 us (7%)
  local copies, waits for them, and re-layouts  7.24 us (3%)
    reduce_scatter x1, waiting for transfers between devices, shards(): lax.psum_scatter(coef_part, 'spec', scatter_dimension=0, tiled=True)  67.1 us
    all_gather x1, waiting for transfers between devices, shards(): coef_all = lax.all_gather(coef_blurred, 'spec', axis=0, tiled=True)  35.2 us
    all_to_all x1, blocking collectives, shards(): lax.all_to_all(cols_done, 'spec', split_axis=0, concat_axis=1, tiled=True)  16.4 us
    ppermute x2, waiting for transfers between devices, with_halo(): lax.ppermute(head, axis, [((i + 1) % count, i) for i in range(ends)])  10.5 us
    ppermute x2, starting transfers between devices, with_halo(): lax.ppermute(tail, axis, [(i, (i + 1) % count) for i in range(ends)])  9.98 us
    ppermute x2, starting transfers between devices, with_halo(): lax.ppermute(head, axis, [((i + 1) % count, i) for i in range(ends)])  8.73 us
    ppermute x2, waiting for transfers between devices, with_halo(): lax.ppermute(tail, axis, [(i, (i + 1) % count) for i in range(ends)])  7.43 us
    dot_general x1, matrix products, shards(): jnp.einsum('qrj,cj->qrc', rows_pixel, column_wide, precision=highest)  7.25 us
  transfers between devices with their start and end apart: 7, of which 7 were waited for; matrix products, arithmetic and copies ran while one was open for 2% of the time, Pallas kernels for 0%

profile of v1, /device:TPU:24, one launch (start us, length us, event | category | flops | bytes accessed | tf_op | source)
XLA Modules:
  0.0 214.6 jit_solution(12891729353502767403)
XLA Ops:
  8.6 6.0 %convolution_bitcast_fusion.1 = f32[32,16,256]{2,0,1:T(8,128)S(1)} fusion(bf16[32,16,1024]{2,1,0:T(8,128)(2,1)} %param.5, f32[]{:T(128)S(6)} %sqrt.2, s32[256]{0:T(256)S(1)} %iota_multiply_fusion), kind=kOutput, calls=%fused_computation.12 | convolution fusion | flops 273154048 | bytes 1573892 | tf_op jit(solution)/shard_map/qrc,cj->qrj/dot_general | solution.py:79
  14.9 16.4 %all_to_all.36 = f32[32,16,256]{2,1,0:T(8,128)S(1)} all-to-all(f32[32,16,256]{2,1,0:T(8,128)S(1)} %copy.64), channel_id=1, replica_groups=mesh['tile'=16,'spec'=16] {'spec'}, dimensions={0} | all-to-all | bytes 1048576 | tf_op jit(solution)/shard_map/all_to_all | solution.py:80
  31.4 5.3 %collective-permute-start = (f32[2,128,256]{2,1,0:T(8,128)S(1)}, f32[2,128,256]{2,1,0:T(8,128)S(1)}, u32[]{:S(2)}, u32[]{:S(2)}) collective-permute-start(f32[2,128,256]{2,1,0:T(8,128)S(1)} %get-tuple-element.12), channel_id=1, source_target_pairs={{0,16},{16,32},{32,48},{48,64},{64,80},{80,96},{96,112},{112,128},... | collective-permute-start | bytes 786440 | tf_op jit(solution)/shard_map/ppermute | solution.py:21
  36.7 4.2 %collective-permute-start.1 = (f32[2,128,256]{2,1,0:T(8,128)S(1)}, f32[2,128,256]{2,1,0:T(8,128)S(1)}, u32[]{:S(2)}, u32[]{:S(2)}) collective-permute-start(f32[2,128,256]{2,1,0:T(8,128)S(1)} %get-tuple-element.13), channel_id=1, source_target_pairs={{16,0},{32,16},{48,32},{64,48},{80,64},{96,80},{112,96},{128,112},... | collective-permute-start | bytes 786440 | tf_op jit(solution)/shard_map/ppermute | solution.py:23
  41.0 4.0 %collective-permute-done = f32[2,128,256]{2,1,0:T(8,128)S(1)} collective-permute-done((f32[2,128,256]{2,1,0:T(8,128)S(1)}, f32[2,128,256]{2,1,0:T(8,128)S(1)}, u32[]{:S(2)}, u32[]{:S(2)}) %collective-permute-start) | collective-permute-done | bytes 262176 | tf_op jit(solution)/shard_map/ppermute | solution.py:21
  45.0 7.5 %collective-permute-done.1 = f32[2,128,256]{2,1,0:T(8,128)S(1)} collective-permute-done((f32[2,128,256]{2,1,0:T(8,128)S(1)}, f32[2,128,256]{2,1,0:T(8,128)S(1)}, u32[]{:S(2)}, u32[]{:S(2)}) %collective-permute-start.1) | collective-permute-done | bytes 262176 | tf_op jit(solution)/shard_map/ppermute | solution.py:23
  52.5 1.7 convolution_bitcast_fusion.2
  54.3 35.2 %all-gather.2.cloned.1.call-done = f32[32,64,256]{2,1,0:T(8,128)} async-done(((f32[2,64,256]{2,1,0:T(8,128)}), f32[32,64,256]{2,1,0:T(8,128)}) %all-gather.2.cloned.1.call-update) | async-done | bytes 2097168 | tf_op jit(solution)/shard_map/all_gather | solution.py:85
  89.5 3.9 %fusion.8 = bf16[14,64,256]{2,0,1:T(8,128)(2,1)S(1)} fusion(f32[32,64,256]{2,1,0:T(8,128)} %all-gather.2.cloned.1.call-done, bf16[14,64,256]{2,1,0:T(8,128)(2,1)S(1)} %copy-done.3, bf16[224,32]{0,1:T(8,128)(2,1)S(1)} %copy-done.5, s32[]{:T(128)S(6)} %select_n.15), kind=kOutput, calls=%fused_computation.9 | convolution fusion | flops 88768512 | bytes 3022852 | tf_op jit(solution)/shard_map/bq,qij->bij/dot_general | solution.py:86
  93.9 2.6 %copy.69 = f32[32,64,256]{2,1,0:T(8,128)} copy(f32[32,64,256]{2,0,1:T(8,128)S(1)} %fusion.81) | data formatting | bytes 4194304 | tf_op jit(solution)/shard_map/bq,bij->qij/dot_general | solution.py:89
  96.5 67.1 %reduce-scatter.2.cloned.1.call-done = f32[2,64,256]{2,1,0:T(8,128)} async-done(((f32[32,64,256]{2,1,0:T(8,128)}), f32[2,64,256]{2,1,0:T(8,128)}) %reduce-scatter.2.cloned.1.call-update) | async-done | bytes 131088 | tf_op jit(solution)/shard_map/reduce_scatter | solution.py:92
  163.6 1.0 copy.70
  164.8 4.7 %collective-permute-start.2 = (f32[2,32,256]{1,2,0:T(8,128)S(1)}, f32[2,32,256]{1,2,0:T(8,128)S(1)}, u32[]{:S(2)}, u32[]{:S(2)}) collective-permute-start(f32[2,32,256]{1,2,0:T(8,128)S(1)} %get-tuple-element.14), channel_id=1, source_target_pairs={{0,16},{16,32},{32,48},{48,64},{64,80},{80,96},{96,112},{112,128},... | collective-permute-start | bytes 196616 | tf_op jit(solution)/shard_map/ppermute | solution.py:21
  169.5 4.5 %collective-permute-start.3 = (f32[2,32,256]{1,2,0:T(8,128)S(1)}, f32[2,32,256]{1,2,0:T(8,128)S(1)}, u32[]{:S(2)}, u32[]{:S(2)}) collective-permute-start(f32[2,32,256]{1,2,0:T(8,128)S(1)} %get-tuple-element.15), channel_id=1, source_target_pairs={{16,0},{32,16},{48,32},{64,48},{80,64},{96,80},{112,96},{128,112},... | collective-permute-start | bytes 196616 | tf_op jit(solution)/shard_map/ppermute | solution.py:23
  174.0 3.4 %collective-permute-done.2 = f32[2,32,256]{1,2,0:T(8,128)S(1)} collective-permute-done((f32[2,32,256]{1,2,0:T(8,128)S(1)}, f32[2,32,256]{1,2,0:T(8,128)S(1)}, u32[]{:S(2)}, u32[]{:S(2)}) %collective-permute-start.2) | collective-permute-done | bytes 65568 | tf_op jit(solution)/shard_map/ppermute | solution.py:21
  177.4 3.0 %collective-permute-done.3 = f32[2,32,256]{1,2,0:T(8,128)S(1)} collective-permute-done((f32[2,32,256]{1,2,0:T(8,128)S(1)}, f32[2,32,256]{1,2,0:T(8,128)S(1)}, u32[]{:S(2)}, u32[]{:S(2)}) %collective-permute-start.3) | collective-permute-done | bytes 65568 | tf_op jit(solution)/shard_map/ppermute | solution.py:23
  180.4 1.0 convolution_bitcast_fusion
  181.3 1.0 copy.73
  182.3 6.1 %all-to-all-start.1 = ((f32[2,256,256]{2,0,1:T(2,128)}), f32[2,256,256]{2,0,1:T(2,128)S(1)}, u32[]{:S(2)}, u32[]{:S(2)}) async-start(f32[2,256,256]{2,0,1:T(2,128)} %copy.73), calls=%async_computation.2 | async-start | bytes 1048576 | tf_op jit(solution)/shard_map/all_to_all | solution.py:97
  188.6 1.6 fusion.11
  190.2 1.0 fusion.121
  192.1 7.2 %all-to-all-done.1 = f32[2,256,256]{2,0,1:T(2,128)S(1)} async-done(((f32[2,256,256]{2,0,1:T(2,128)}), f32[2,256,256]{2,0,1:T(2,128)S(1)}, u32[]{:S(2)}, u32[]{:S(2)}) %all-to-all-start.1) | async-done | bytes 524320 | tf_op jit(solution)/shard_map/all_to_all | solution.py:97
  199.4 1.1 copy-done.2
  200.6 7.3 %fusion.2 = bf16[32,16,1024]{2,1,0:T(8,128)(2,1)} fusion(f32[32,16,1024]{2,0,1:T(8,128)S(1)} %fusion.121, bf16[32,16,1024]{2,1,0:T(8,128)(2,1)S(1)} %copy-done.2, f32[32,16,256]{2,1,0:T(8,128)S(1)} %bitcast.44, f32[]{:T(128)S(6)} %sqrt.2, s32[256]{0:T(256)S(1)} %iota_multiply_fusion), kind=kOutput, calls=%fused_computation.3 | convolution fusion | flops 1617952768 | bytes 4719620 | tf_op jit(solution)/shard_map/qrj,cj->qrc/dot_general | solution.py:98
  (29 shorter events, 2.9 us)
Async XLA Ops:
  7.2 181.3 %copy-start = (bf16[8,224]{1,0:T(8,128)(2,1)S(1)}, bf16[8,224]{1,0:T(8,128)(2,1)}, u32[]{:S(2)}) copy-start(bf16[8,224]{1,0:T(8,128)(2,1)} %param.7) | copy-start | bytes 10756
  7.2 82.3 %all-gather.2.cloned.1.call-start = ((), (), s32[]{:S(2)}) async-start(), calls=%async_computation.3 | async-start | bytes 2228224 | tf_op jit(solution)/shard_map/all_gather | solution.py:85
  31.3 58.2 %copy-start.3 = (bf16[14,64,256]{2,1,0:T(8,128)(2,1)S(1)}, bf16[14,64,256]{2,1,0:T(8,128)(2,1)}, u32[]{:S(2)}) copy-start(bf16[14,64,256]{2,1,0:T(8,128)(2,1)} %param.8) | copy-start | bytes 1376260
  31.3 58.2 %copy-start.5 = (bf16[224,32]{0,1:T(8,128)(2,1)S(1)}, bf16[224,32]{0,1:T(8,128)(2,1)}, u32[]{:S(2)}) copy-start(bf16[224,32]{0,1:T(8,128)(2,1)} %param.6) | copy-start | bytes 43012
  31.4 13.6 %collective-permute-start = (f32[2,128,256]{2,1,0:T(8,128)S(1)}, f32[2,128,256]{2,1,0:T(8,128)S(1)}, u32[]{:S(2)}, u32[]{:S(2)}) collective-permute-start(f32[2,128,256]{2,1,0:T(8,128)S(1)} %get-tuple-element.12), channel_id=1, source_target_pairs={{0,16},{16,32},{32,48},{48,64},{64,80},{80,96},{96,112},{112,128},... | collective-permute-start | bytes 786440 | tf_op jit(solution)/shard_map/ppermute | solution.py:21
  36.7 15.8 %collective-permute-start.1 = (f32[2,128,256]{2,1,0:T(8,128)S(1)}, f32[2,128,256]{2,1,0:T(8,128)S(1)}, u32[]{:S(2)}, u32[]{:S(2)}) collective-permute-start(f32[2,128,256]{2,1,0:T(8,128)S(1)} %get-tuple-element.13), channel_id=1, source_target_pairs={{16,0},{32,16},{48,32},{64,48},{80,64},{96,80},{112,96},{128,112},... | collective-permute-start | bytes 786440 | tf_op jit(solution)/shard_map/ppermute | solution.py:23
  54.3 109.3 %reduce-scatter.2.cloned.1.call-start = ((), (), s32[]{:S(2)}) async-start(), calls=%async_computation.4 | async-start | bytes 2228224 | tf_op jit(solution)/shard_map/reduce_scatter | solution.py:92
  164.6 24.0 %copy-start.1 = (bf16[32,16,1024]{2,1,0:T(8,128)(2,1)S(1)}, bf16[32,16,1024]{2,1,0:T(8,128)(2,1)}, u32[]{:S(2)}) copy-start(bf16[32,16,1024]{2,1,0:T(8,128)(2,1)} %param.5) | copy-start | bytes 3145732
  164.6 23.9 %copy-start.4 = (bf16[8,16,1024]{2,1,0:T(8,128)(2,1)S(1)}, bf16[8,16,1024]{2,1,0:T(8,128)(2,1)}, u32[]{:S(2)}) copy-start(bf16[8,16,1024]{2,1,0:T(8,128)(2,1)} %param.9) | copy-start | bytes 786436
  164.8 12.6 %collective-permute-start.2 = (f32[2,32,256]{1,2,0:T(8,128)S(1)}, f32[2,32,256]{1,2,0:T(8,128)S(1)}, u32[]{:S(2)}, u32[]{:S(2)}) collective-permute-start(f32[2,32,256]{1,2,0:T(8,128)S(1)} %get-tuple-element.14), channel_id=1, source_target_pairs={{0,16},{16,32},{32,48},{48,64},{64,80},{80,96},{96,112},{112,128},... | collective-permute-start | bytes 196616 | tf_op jit(solution)/shard_map/ppermute | solution.py:21
  169.5 10.9 %collective-permute-start.3 = (f32[2,32,256]{1,2,0:T(8,128)S(1)}, f32[2,32,256]{1,2,0:T(8,128)S(1)}, u32[]{:S(2)}, u32[]{:S(2)}) collective-permute-start(f32[2,32,256]{1,2,0:T(8,128)S(1)} %get-tuple-element.15), channel_id=1, source_target_pairs={{16,0},{32,16},{48,32},{64,48},{80,64},{96,80},{112,96},{128,112},... | collective-permute-start | bytes 196616 | tf_op jit(solution)/shard_map/ppermute | solution.py:23
  182.3 17.0 %all-to-all-start.1 = ((f32[2,256,256]{2,0,1:T(2,128)}), f32[2,256,256]{2,0,1:T(2,128)S(1)}, u32[]{:S(2)}, u32[]{:S(2)}) async-start(f32[2,256,256]{2,0,1:T(2,128)} %copy.73), calls=%async_computation.2 | async-start | bytes 1048576 | tf_op jit(solution)/shard_map/all_to_all | solution.py:97
  199.3 1.2 copy-start.2
Sparse Core Ops, SparseCore 0:
  54.4 35.0 all-gather.1
  96.6 66.9 reduce-scatter.1

commit v2 on v1

--- a/solution.py
+++ b/solution.py
@@ -67,34 +67,43 @@
 def shards(latent, basis, response, hyper_obs, multi_obs):
     highest = lax.Precision.HIGHEST
     f32 = jnp.float32
-    group = hyper_obs.shape[0]
-    rows_dev = hyper_obs.shape[1] * DECIM
-    width_cols = latent.shape[2]
-    spec_index = lax.axis_index("spec")
+    n_spec = lax.axis_size("spec")
+    group, coarse_rows, coarse_cols = hyper_obs.shape
+    rows_dev = coarse_rows * DECIM
+    subspace, rows_here, width_cols = latent.shape
+    chunk = coarse_cols // n_spec
     basis_wide = basis.astype(f32)
-    basis_own = lax.dynamic_slice_in_dim(basis_wide, spec_index * group, group, 0)
-    column_kernel = column_matrix(width_cols, width_cols // DECIM)
+    column_kernel = column_matrix(width_cols, coarse_cols)
     column_wide = column_kernel.astype(f32)
 
-    cols_done = jnp.einsum("qrc,cj->qrj", latent, column_kernel, preferred_element_type=f32)
-    coef_rows = lax.all_to_all(cols_done, "spec", split_axis=0, concat_axis=1, tiled=True)
-    padded = with_halo(coef_rows, (("tile", 1),), HALO)
+    cols_done = jnp.einsum(
+        "qrc,csj->sqjr",
+        latent,
+        column_kernel.reshape(width_cols, n_spec, chunk),
+        preferred_element_type=f32,
+    )
+    tile_rows = lax.all_to_all(cols_done, "spec", split_axis=0, concat_axis=3, tiled=True)[0]
+    padded = with_halo(tile_rows, (("tile", 2),), HALO)
     coef_blurred = jnp.einsum(
-        "ir,qrj->qij", row_matrix(rows_dev).astype(f32), padded, precision=highest
+        "qjr,ir->qji", padded, row_matrix(rows_dev).astype(f32), precision=highest
     )
-    coef_all = lax.all_gather(coef_blurred, "spec", axis=0, tiled=True)
-    blurred = jnp.einsum("bq,qij->bij", basis_own, coef_all, precision=highest)
-    hs_residual = (blurred - hyper_obs.astype(f32)).astype(jnp.bfloat16)
+    blurred = jnp.einsum("bq,qji->bji", basis_wide, coef_blurred, precision=highest)
 
-    coef_part = jnp.einsum(
-        "bq,bij->qij", basis_own.astype(jnp.bfloat16), hs_residual, preferred_element_type=f32
+    obs_split = hyper_obs.reshape(group, coarse_rows, n_spec, chunk).transpose(2, 0, 3, 1)
+    obs_cols = lax.all_to_all(obs_split, "spec", split_axis=0, concat_axis=1, tiled=True)[0]
+    resid_cols = (blurred - obs_cols.astype(f32)).astype(jnp.bfloat16)
+
+    resid_split = resid_cols.reshape(n_spec, group, chunk, coarse_rows)
+    resid_bands = lax.all_to_all(resid_split, "spec", split_axis=0, concat_axis=2, tiled=True)[0]
+    hs_residual = resid_bands.transpose(0, 2, 1)
+
+    coef_resid = jnp.einsum("bq,bji->qji", basis, resid_cols, preferred_element_type=f32)
+    coarse_padded = with_halo(coef_resid, (("tile", 2),), HALO // DECIM)
+    rows_back = jnp.einsum(
+        "qjk,rk->qjr", coarse_padded, back_matrix(rows_dev).astype(f32), precision=highest
     )
-    coef_resid = lax.psum_scatter(coef_part, "spec", scatter_dimension=0, tiled=True)
-    coarse_padded = with_halo(coef_resid, (("tile", 1),), HALO // DECIM)
-    rows_back = jnp.einsum(
-        "rq,cqj->crj", back_matrix(rows_dev).astype(f32), coarse_padded, precision=highest
-    )
-    rows_pixel = lax.all_to_all(rows_back, "spec", split_axis=1, concat_axis=0, tiled=True)
+    back_split = rows_back.reshape(subspace, chunk, n_spec, rows_here).transpose(2, 0, 3, 1)
+    rows_pixel = lax.all_to_all(back_split, "spec", split_axis=0, concat_axis=3, tiled=True)[0]
     grad_hs = jnp.einsum("qrj,cj->qrc", rows_pixel, column_wide, precision=highest)
 
     resp_basis = jnp.dot(response.astype(f32), basis_wide, precision=highest)

time: 217 us -> 129 us (0.59)
  waiting for transfers between devices: 128 us -> 35.7 us
  blocking collectives: 16.4 us -> 0 us
  starting transfers between devices: 24.9 us -> 40.6 us
  between operations: 14.9 us -> 1.62 us
  local copies, waits for them, and re-layouts: 7.24 us -> 18 us
  other arithmetic: 0.67 us -> 5.8 us
  matrix products: 23 us -> 25.5 us
    reduce_scatter x1 -> x0, waiting for transfers between devices: 67.1 us -> none  [shards(): lax.psum_scatter(coef_part, 'spec', scatter_dimension=0, tiled=True)]
    all_gather x1 -> x0, waiting for transfers between devices: 35.2 us -> none  [shards(): coef_all = lax.all_gather(coef_blurred, 'spec', axis=0, tiled=True)]
    all_to_all x1 -> x0, blocking collectives: 16.4 us -> none  [shards(): lax.all_to_all(cols_done, 'spec', split_axis=0, concat_axis=1, tiled=True)]
    all_to_all x1 -> x4, starting transfers between devices: 6.12 us -> 22.2 us  [the longest x1 7.1 us: shards(): lax.all_to_all(back_split, 'spec', split_axis=0, concat_axis=3, tiled=True)]
    unnamed x13 -> x22, local copies, waits for them, and re-layouts: 2.08 us -> 11 us
    ppermute x2, waiting for transfers between devices: 7.43 us -> 14.8 us  [with_halo(): lax.ppermute(tail, axis, [(i, (i + 1) % count) for i in range(ends)])]
    all_to_all x1 -> x4, waiting for transfers between devices: 7.2 us -> 13.2 us  [the longest x1 9.23 us: shards(): lax.all_to_all(cols_done, 'spec', split_axis=0, concat_axis=3, tiled=True)]
    all_to_all x0 -> x2, other arithmetic: none -> 3.84 us  [the longest x1 1.92 us: shards(): lax.all_to_all(back_split, 'spec', split_axis=0, concat_axis=3, tiled=True)]
  transfers between devices with their start and end apart: 7 -> 8, of which waited for: 7 -> 6; matrix products, arithmetic and copies ran while one was open for 2% -> 18% of each run, Pallas kernels for 0% -> 0%
where the time goes in v2:
time: 129 us; the launch traced here: 127 us
  starting transfers between devices  40.6 us (31%)
  waiting for transfers between devices  35.7 us (28%)
  matrix products  25.5 us (20%)
  local copies, waits for them, and re-layouts  18 us (14%)
  other arithmetic  5.8 us (4%)
  between operations  1.62 us (1%)
    ppermute x2, waiting for transfers between devices, with_halo(): lax.ppermute(tail, axis, [(i, (i + 1) % count) for i in range(ends)])  14.8 us
    unnamed x22, local copies, waits for them, and re-layouts  11 us
    ppermute x2, starting transfers between devices, with_halo(): lax.ppermute(tail, axis, [(i, (i + 1) % count) for i in range(ends)])  10.8 us
    all_to_all x1, waiting for transfers between devices, shards(): lax.all_to_all(cols_done, 'spec', split_axis=0, concat_axis=3, tiled=True)  9.23 us
    dot_general x1, matrix products, shards(): jnp.einsum('qrj,cj->qrc', rows_pixel, column_wide, precision=highest)  8.69 us
    ppermute x2, waiting for transfers between devices, with_halo(): lax.ppermute(head, axis, [((i + 1) % count, i) for i in range(ends)])  7.73 us
    ppermute x2, starting transfers between devices, with_halo(): lax.ppermute(head, axis, [((i + 1) % count, i) for i in range(ends)])  7.62 us
    all_to_all x1, starting transfers between devices, shards(): lax.all_to_all(back_split, 'spec', split_axis=0, concat_axis=3, tiled=True)  7.1 us
  transfers between devices with their start and end apart: 8, of which 6 were waited for; matrix products, arithmetic and copies ran while one was open for 18% of the time, Pallas kernels for 0%

profile of v2, /device:TPU:24, one launch (start us, length us, event | category | flops | bytes accessed | tf_op | source)
XLA Modules:
  0.0 127.2 jit_solution(10577256098781289085)
XLA Ops:
  3.5 5.8 %all-to-all-start.1 = ((bf16[16,2,7168]{2,1,0:T(2,128)(2,1)}), bf16[16,2,7168]{2,1,0:T(2,128)(2,1)S(1)}, u32[]{:S(2)}, u32[]{:S(2)}) async-start(bf16[16,2,7168]{2,1,0:T(2,128)(2,1)} %reshape.63), calls=%async_computation.1 | async-start | bytes 917504 | tf_op jit(solution)/shard_map/all_to_all | solution.py:93
  10.7 6.9 %fusion.130 = f32[16,16,16,32]{3,2,1,0:T(8,128)S(1)} fusion(bf16[32,16,1024]{2,1,0:T(8,128)(2,1)} %param.5, f32[]{:T(128)S(6)} %sqrt.2, s32[16,16]{1,0:T(8,128)S(1)} %add_multiply_fusion), kind=kOutput, calls=%fused_computation.154 | convolution fusion | flops 273154048 | bytes 1573892 | tf_op jit(solution)/shard_map/qrc,csj->sqjr/dot_general | solution.py:79
  17.5 1.7 %reshape.65 = f32[16,1,8192]{2,1,0:T(1,128)} reshape(f32[16,16,16,32]{3,2,1,0:T(8,128)S(1)} %fusion.130) | data formatting | bytes 1048576
  19.5 5.5 %all-to-all-start = ((f32[16,1,8192]{2,1,0:T(1,128)}), f32[16,1,8192]{2,1,0:T(1,128)S(1)}, u32[]{:S(2)}, u32[]{:S(2)}) async-start(f32[16,1,8192]{2,1,0:T(1,128)} %reshape.65), calls=%async_computation | async-start | bytes 1048576 | tf_op jit(solution)/shard_map/all_to_all | solution.py:85
  26.6 9.2 %all-to-all-done = f32[16,1,8192]{2,1,0:T(1,128)S(1)} async-done(((f32[16,1,8192]{2,1,0:T(1,128)}), f32[16,1,8192]{2,1,0:T(1,128)S(1)}, u32[]{:S(2)}, u32[]{:S(2)}) %all-to-all-start) | async-done | bytes 524320 | tf_op jit(solution)/shard_map/all_to_all | solution.py:85
  36.4 1.9 %reduce = f32[16,8192]{1,0:T(8,128)S(1)} reduce(f32[16,1,8192]{2,1,0:T(1,128)S(1)} %all-to-all-done, f32[]{:T(128)} %broadcast.81), dimensions={1}, to_apply=%all_to_all.40.reduce_sub_computation | reduce | bytes 1048580 | tf_op jit(solution)/shard_map/all_to_all | solution.py:85
  41.1 5.3 %collective-permute-start = (f32[32,16,128]{2,1,0:T(8,128)}, f32[32,16,128]{2,1,0:T(8,128)}, u32[]{:S(2)}, u32[]{:S(2)}) collective-permute-start(f32[32,16,128]{2,1,0:T(8,128)} %get-tuple-element.8), channel_id=1, source_target_pairs={{0,16},{16,32},{32,48},{48,64},{64,80},{80,96},{96,112},{112,128},... | collective-permute-start | bytes 786440 | tf_op jit(solution)/shard_map/ppermute | solution.py:21
  46.5 4.2 %collective-permute-start.1 = (f32[32,16,128]{2,1,0:T(8,128)}, f32[32,16,128]{2,1,0:T(8,128)}, u32[]{:S(2)}, u32[]{:S(2)}) collective-permute-start(f32[32,16,128]{2,1,0:T(8,128)} %get-tuple-element.9), channel_id=1, source_target_pairs={{16,0},{32,16},{48,32},{64,48},{80,64},{96,80},{112,96},{128,112},... | collective-permute-start | bytes 786440 | tf_op jit(solution)/shard_map/ppermute | solution.py:23
  51.8 3.0 %collective-permute-done = f32[32,16,128]{2,1,0:T(8,128)} collective-permute-done((f32[32,16,128]{2,1,0:T(8,128)}, f32[32,16,128]{2,1,0:T(8,128)}, u32[]{:S(2)}, u32[]{:S(2)}) %collective-permute-start) | collective-permute-done | bytes 262176 | tf_op jit(solution)/shard_map/ppermute | solution.py:21
  54.9 7.7 %collective-permute-done.1 = f32[32,16,128]{2,1,0:T(8,128)} collective-permute-done((f32[32,16,128]{2,1,0:T(8,128)}, f32[32,16,128]{2,1,0:T(8,128)}, u32[]{:S(2)}, u32[]{:S(2)}) %collective-permute-start.1) | collective-permute-done | bytes 262176 | tf_op jit(solution)/shard_map/ppermute | solution.py:23
  62.6 2.2 %fusion.16 = f32[32,16,64]{2,1,0:T(8,128)S(1)} fusion(f32[32,16,128]{2,1,0:T(8,128)} %collective-permute-done.1, f32[32,16,256]{2,1,0:T(8,128)S(1)} %copy.47, f32[32,16,128]{2,1,0:T(8,128)} %collective-permute-done, f32[]{:T(128)S(6)} %sqrt.2, s32[64]{0:T(128)S(1)} %copy-done.5, s32[512]{0:T(512)S(1)} %copy-done.4), kind=kOutput, calls=%fused_computation.26 | convolution fusion | flops 202440704 | bytes 1181956 | tf_op jit(solution)/shard_map/qjr,ir->qji/dot_general | solution.py:87
  67.6 3.8 %all-to-all-start.3 = ((bf16[16,2,7168]{2,1,0:T(2,128)(2,1)}), bf16[16,2,7168]{2,1,0:T(2,128)(2,1)S(1)}, u32[]{:S(2)}, u32[]{:S(2)}) async-start(bf16[16,2,7168]{2,1,0:T(2,128)(2,1)} %reshape.69), calls=%async_computation.3 | async-start | bytes 917504 | tf_op jit(solution)/shard_map/all_to_all | solution.py:97
  71.8 5.5 %collective-permute-start.2 = (f32[32,16,32]{2,0,1:T(8,128)S(1)}, f32[32,16,32]{2,0,1:T(8,128)S(1)}, u32[]{:S(2)}, u32[]{:S(2)}) collective-permute-start(f32[32,16,32]{2,0,1:T(8,128)S(1)} %get-tuple-element.10), channel_id=1, source_target_pairs={{0,16},{16,32},{32,48},{48,64},{64,80},{80,96},{96,112},{112,128},... | collective-permute-start | bytes 196616 | tf_op jit(solution)/shard_map/ppermute | solution.py:21
  77.3 3.4 %collective-permute-start.3 = (f32[32,16,32]{2,0,1:T(8,128)S(1)}, f32[32,16,32]{2,0,1:T(8,128)S(1)}, u32[]{:S(2)}, u32[]{:S(2)}) collective-permute-start(f32[32,16,32]{2,0,1:T(8,128)S(1)} %get-tuple-element.11), channel_id=1, source_target_pairs={{16,0},{32,16},{48,32},{64,48},{80,64},{96,80},{112,96},{128,112},... | collective-permute-start | bytes 196616 | tf_op jit(solution)/shard_map/ppermute | solution.py:23
  80.7 11.8 %collective-permute-done.2 = f32[32,16,32]{2,0,1:T(8,128)S(1)} collective-permute-done((f32[32,16,32]{2,0,1:T(8,128)S(1)}, f32[32,16,32]{2,0,1:T(8,128)S(1)}, u32[]{:S(2)}, u32[]{:S(2)}) %collective-permute-start.2) | collective-permute-done | bytes 65568 | tf_op jit(solution)/shard_map/ppermute | solution.py:21
  92.5 1.5 %fusion.47 = f32[32,16,256]{0,2,1:T(8,128)S(1)} fusion(f32[32,16,32]{2,0,1:T(8,128)S(1)} %collective-permute-done.3, f32[32,16,64]{2,0,1:T(8,128)S(1)} %convolution_bitcast_fusion.2, f32[32,16,32]{2,0,1:T(8,128)S(1)} %collective-permute-done.2, f32[]{:T(128)S(6)} %sqrt.2, s32[128]{0:T(128)S(1)} %iota_multiply_fusion.1), kind=kOutput, calls=%fused_computation.58 | convolution fusion | flops 202080256 | bytes 786948 | tf_op jit(solution)/shard_map/qjk,rk->qjr/dot_general | solution.py:102
  94.2 1.7 %reshape.67 = f32[16,1,8192]{2,1,0:T(1,128)} reshape(f32[16,16,16,32]{3,2,1,0:T(8,128)S(1)} %bitcast.82) | data formatting | bytes 1048576
  96.0 7.1 %all-to-all-start.2 = ((f32[16,1,8192]{2,1,0:T(1,128)}), f32[16,1,8192]{2,1,0:T(1,128)S(1)}, u32[]{:S(2)}, u32[]{:S(2)}) async-start(f32[16,1,8192]{2,1,0:T(1,128)} %reshape.67), calls=%async_computation.2 | async-start | bytes 1048576 | tf_op jit(solution)/shard_map/all_to_all | solution.py:106
  103.2 2.8 %fusion.5 = bf16[8,16,1024]{2,0,1:T(8,128)(2,1)S(1)} fusion(f32[8,32,1]{1,0,2:T(8,128)S(1)} %convolution_bitcast_fusion.3, bf16[32,16,1024]{2,1,0:T(8,128)(2,1)} %param.5, bf16[8,16,1024]{2,1,0:T(8,128)(2,1)S(1)} %copy-done.2), kind=kOutput, calls=%fused_computation.13 | convolution fusion | flops 50724864 | bytes 1573888 | tf_op jit(solution)/shard_map/mq,qrc->mrc/dot_general | solution.py:110
  106.0 2.3 %fusion.135 = f32[32,16,1024]{2,0,1:T(8,128)} fusion(f32[8,32,1]{1,0,2:T(8,128)S(1)} %convolution_bitcast_fusion.3, bf16[8,16,1024]{2,0,1:T(8,128)(2,1)S(1)} %fusion.5), kind=kOutput, calls=%fused_computation.155 | convolution fusion | flops 50331648 | bytes 2360320 | tf_op jit(solution)/shard_map/mq,mrc->qrc/dot_general | solution.py:112
  110.2 3.7 %all-to-all-done.2 = f32[16,1,8192]{2,1,0:T(1,128)S(1)} async-done(((f32[16,1,8192]{2,1,0:T(1,128)}), f32[16,1,8192]{2,1,0:T(1,128)S(1)}, u32[]{:S(2)}, u32[]{:S(2)}) %all-to-all-start.2) | async-done | bytes 524320 | tf_op jit(solution)/shard_map/all_to_all | solution.py:106
  113.9 1.9 %reduce.1 = f32[16,8192]{1,0:T(8,128)S(1)} reduce(f32[16,1,8192]{2,1,0:T(1,128)S(1)} %all-to-all-done.2, f32[]{:T(128)} %broadcast.81), dimensions={1}, to_apply=%all_to_all.44.reduce_sub_computation | reduce | bytes 1048580 | tf_op jit(solution)/shard_map/all_to_all | solution.py:106
  116.6 2.0 %copy.58 = f32[32,16,256]{2,1,0:T(8,128)} copy(f32[32,16,256]{0,1,2:T(8,128)S(1)} %bitcast.81) | data formatting | bytes 1048576 | tf_op jit(solution)/shard_map/squeeze | solution.py:106
  118.5 8.7 %fusion.2 = bf16[32,16,1024]{2,1,0:T(8,128)(2,1)} fusion(f32[32,16,1024]{2,0,1:T(8,128)} %fusion.135, bf16[32,16,1024]{2,1,0:T(8,128)(2,1)S(1)} %copy-done.1, f32[32,16,256]{2,1,0:T(8,128)} %copy.58, f32[]{:T(128)S(6)} %sqrt.2, s32[256]{0:T(256)S(1)} %iota_multiply_fusion), kind=kOutput, calls=%fused_computation.3 | convolution fusion | flops 1617952768 | bytes 4719620 | tf_op jit(solution)/shard_map/qrj,cj->qrc/dot_general | solution.py:107
  (42 shorter events, 15.8 us)
Async XLA Ops:
  0.6 64.2 %copy-start = (bf16[224,32]{0,1:T(8,128)(2,1)S(1)}, bf16[224,32]{0,1:T(8,128)(2,1)}, u32[]{:S(2)}) copy-start(bf16[224,32]{0,1:T(8,128)(2,1)} %param.6) | copy-start | bytes 43012
  3.5 15.9 %all-to-all-start.1 = ((bf16[16,2,7168]{2,1,0:T(2,128)(2,1)}), bf16[16,2,7168]{2,1,0:T(2,128)(2,1)S(1)}, u32[]{:S(2)}, u32[]{:S(2)}) async-start(bf16[16,2,7168]{2,1,0:T(2,128)(2,1)} %reshape.63), calls=%async_computation.1 | async-start | bytes 917504 | tf_op jit(solution)/shard_map/all_to_all | solution.py:93
  19.5 16.4 %all-to-all-start = ((f32[16,1,8192]{2,1,0:T(1,128)}), f32[16,1,8192]{2,1,0:T(1,128)S(1)}, u32[]{:S(2)}, u32[]{:S(2)}) async-start(f32[16,1,8192]{2,1,0:T(1,128)} %reshape.65), calls=%async_computation | async-start | bytes 1048576 | tf_op jit(solution)/shard_map/all_to_all | solution.py:85
  41.1 13.8 %collective-permute-start = (f32[32,16,128]{2,1,0:T(8,128)}, f32[32,16,128]{2,1,0:T(8,128)}, u32[]{:S(2)}, u32[]{:S(2)}) collective-permute-start(f32[32,16,128]{2,1,0:T(8,128)} %get-tuple-element.8), channel_id=1, source_target_pairs={{0,16},{16,32},{32,48},{48,64},{64,80},{80,96},{96,112},{112,128},... | collective-permute-start | bytes 786440 | tf_op jit(solution)/shard_map/ppermute | solution.py:21
  46.5 16.2 %collective-permute-start.1 = (f32[32,16,128]{2,1,0:T(8,128)}, f32[32,16,128]{2,1,0:T(8,128)}, u32[]{:S(2)}, u32[]{:S(2)}) collective-permute-start(f32[32,16,128]{2,1,0:T(8,128)} %get-tuple-element.9), channel_id=1, source_target_pairs={{16,0},{32,16},{48,32},{64,48},{80,64},{96,80},{112,96},{128,112},... | collective-permute-start | bytes 786440 | tf_op jit(solution)/shard_map/ppermute | solution.py:23
  50.9 11.7 %copy-start.4 = (s32[512]{0:T(512)S(1)}, s32[512]{0:T(512)}, u32[]{:S(2)}) copy-start(s32[512]{0:T(512)} %iota_add_fusion) | copy-start | bytes 6148
  50.9 11.7 %copy-start.5 = (s32[64]{0:T(128)S(1)}, s32[64]{0:T(128)}, u32[]{:S(2)}) copy-start(s32[64]{0:T(128)} %iota_multiply_fusion.2) | copy-start | bytes 772
  67.6 28.4 %all-to-all-start.3 = ((bf16[16,2,7168]{2,1,0:T(2,128)(2,1)}), bf16[16,2,7168]{2,1,0:T(2,128)(2,1)S(1)}, u32[]{:S(2)}, u32[]{:S(2)}) async-start(bf16[16,2,7168]{2,1,0:T(2,128)(2,1)} %reshape.69), calls=%async_computation.3 | async-start | bytes 917504 | tf_op jit(solution)/shard_map/all_to_all | solution.py:97
  71.8 20.6 %collective-permute-start.2 = (f32[32,16,32]{2,0,1:T(8,128)S(1)}, f32[32,16,32]{2,0,1:T(8,128)S(1)}, u32[]{:S(2)}, u32[]{:S(2)}) collective-permute-start(f32[32,16,32]{2,0,1:T(8,128)S(1)} %get-tuple-element.10), channel_id=1, source_target_pairs={{0,16},{16,32},{32,48},{48,64},{64,80},{80,96},{96,112},{112,128},... | collective-permute-start | bytes 196616 | tf_op jit(solution)/shard_map/ppermute | solution.py:21
  77.3 15.2 %collective-permute-start.3 = (f32[32,16,32]{2,0,1:T(8,128)S(1)}, f32[32,16,32]{2,0,1:T(8,128)S(1)}, u32[]{:S(2)}, u32[]{:S(2)}) collective-permute-start(f32[32,16,32]{2,0,1:T(8,128)S(1)} %get-tuple-element.11), channel_id=1, source_target_pairs={{16,0},{32,16},{48,32},{64,48},{80,64},{96,80},{112,96},{128,112},... | collective-permute-start | bytes 196616 | tf_op jit(solution)/shard_map/ppermute | solution.py:23
  94.2 8.9 %copy-start.3 = (bf16[8,224]{1,0:T(8,128)(2,1)S(1)}, bf16[8,224]{1,0:T(8,128)(2,1)}, u32[]{:S(2)}) copy-start(bf16[8,224]{1,0:T(8,128)(2,1)} %param.7) | copy-start | bytes 10756
  94.2 9.0 %copy-start.2 = (bf16[8,16,1024]{2,1,0:T(8,128)(2,1)S(1)}, bf16[8,16,1024]{2,1,0:T(8,128)(2,1)}, u32[]{:S(2)}) copy-start(bf16[8,16,1024]{2,1,0:T(8,128)(2,1)} %param.9) | copy-start | bytes 786436
  96.0 18.0 %all-to-all-start.2 = ((f32[16,1,8192]{2,1,0:T(1,128)}), f32[16,1,8192]{2,1,0:T(1,128)S(1)}, u32[]{:S(2)}, u32[]{:S(2)}) async-start(f32[16,1,8192]{2,1,0:T(1,128)} %reshape.67), calls=%async_computation.2 | async-start | bytes 1048576 | tf_op jit(solution)/shard_map/all_to_all | solution.py:106
  116.5 2.0 %copy-start.1 = (bf16[32,16,1024]{2,1,0:T(8,128)(2,1)S(1)}, bf16[32,16,1024]{2,1,0:T(8,128)(2,1)}, u32[]{:S(2)}) copy-start(bf16[32,16,1024]{2,1,0:T(8,128)(2,1)} %param.5) | copy-start | bytes 3145732

commit v3 on v2

--- a/solution.py
+++ b/solution.py
@@ -64,17 +64,41 @@
     return kernel_values(fine_rows - DECIM * coarse + HALO)
 
 
+def split_dot(spec, wide, narrow):
+    high_wide = lax.reduce_precision(wide, exponent_bits=8, mantissa_bits=7)
+    high = high_wide.astype(jnp.bfloat16)
+    low = (wide - high_wide).astype(jnp.bfloat16)
+    f32 = jnp.float32
+    return jnp.einsum(spec, high, narrow, preferred_element_type=f32) + jnp.einsum(
+        spec, low, narrow, preferred_element_type=f32
+    )
+
+
+def swap(chunks, axis):
+    count = chunks.shape[0]
+    rows = 8 if chunks.dtype == jnp.float32 else 16
+    flat = chunks.reshape(count, rows, -1)
+    flat = lax.all_to_all(flat, axis, split_axis=0, concat_axis=0, tiled=True)
+    return flat.reshape(chunks.shape)
+
+
 def shards(latent, basis, response, hyper_obs, multi_obs):
-    highest = lax.Precision.HIGHEST
     f32 = jnp.float32
     n_spec = lax.axis_size("spec")
+    n_tile = lax.axis_size("tile")
+    tile_index = lax.axis_index("tile")
     group, coarse_rows, coarse_cols = hyper_obs.shape
     rows_dev = coarse_rows * DECIM
+    rim = HALO // DECIM
     subspace, rows_here, width_cols = latent.shape
     chunk = coarse_cols // n_spec
-    basis_wide = basis.astype(f32)
-    column_kernel = column_matrix(width_cols, coarse_cols)
-    column_wide = column_kernel.astype(f32)
+    column_kernel, row_kernel, back_kernel = lax.optimization_barrier(
+        (
+            column_matrix(width_cols, coarse_cols),
+            row_matrix(rows_dev + 2 * (rows_dev - HALO)),
+            back_matrix(rows_dev),
+        )
+    )
 
     cols_done = jnp.einsum(
         "qrc,csj->sqjr",
@@ -82,36 +106,34 @@
         column_kernel.reshape(width_cols, n_spec, chunk),
         preferred_element_type=f32,
     )
-    tile_rows = lax.all_to_all(cols_done, "spec", split_axis=0, concat_axis=3, tiled=True)[0]
-    padded = with_halo(tile_rows, (("tile", 2),), HALO)
-    coef_blurred = jnp.einsum(
-        "qjr,ir->qji", padded, row_matrix(rows_dev).astype(f32), precision=highest
-    )
-    blurred = jnp.einsum("bq,qji->bji", basis_wide, coef_blurred, precision=highest)
+    got = swap(cols_done, "spec")
+    tile_rows = got.transpose(1, 2, 0, 3).reshape(subspace, chunk, rows_dev)
+    padded = with_halo(tile_rows, (("tile", 2),), rows_dev)
+    coef_blurred = split_dot("qjr,ir->qji", padded, row_kernel)
+    blurred = split_dot("qji,bq->bji", coef_blurred, basis)
 
     obs_split = hyper_obs.reshape(group, coarse_rows, n_spec, chunk).transpose(2, 0, 3, 1)
-    obs_cols = lax.all_to_all(obs_split, "spec", split_axis=0, concat_axis=1, tiled=True)[0]
-    resid_cols = (blurred - obs_cols.astype(f32)).astype(jnp.bfloat16)
+    obs_cols = swap(obs_split, "spec").reshape(group * n_spec, chunk, coarse_rows)
+    obs_wide = with_halo(obs_cols, (("tile", 2),), rim)
+    coarse_at = jnp.arange(coarse_rows + 2 * rim) + tile_index * coarse_rows - rim
+    inside = (coarse_at >= 0) & (coarse_at < n_tile * coarse_rows)
+    resid_wide = jnp.where(inside, blurred - obs_wide.astype(f32), 0.0).astype(jnp.bfloat16)
 
-    resid_split = resid_cols.reshape(n_spec, group, chunk, coarse_rows)
-    resid_bands = lax.all_to_all(resid_split, "spec", split_axis=0, concat_axis=2, tiled=True)[0]
-    hs_residual = resid_bands.transpose(0, 2, 1)
+    resid_cols = lax.slice_in_dim(resid_wide, rim, rim + coarse_rows, axis=2)
+    got_bands = swap(resid_cols.reshape(n_spec, group, chunk, coarse_rows), "spec")
+    hs_residual = got_bands.transpose(1, 3, 0, 2).reshape(group, coarse_rows, coarse_cols)
 
-    coef_resid = jnp.einsum("bq,bji->qji", basis, resid_cols, preferred_element_type=f32)
-    coarse_padded = with_halo(coef_resid, (("tile", 2),), HALO // DECIM)
-    rows_back = jnp.einsum(
-        "qjk,rk->qjr", coarse_padded, back_matrix(rows_dev).astype(f32), precision=highest
-    )
-    back_split = rows_back.reshape(subspace, chunk, n_spec, rows_here).transpose(2, 0, 3, 1)
-    rows_pixel = lax.all_to_all(back_split, "spec", split_axis=0, concat_axis=3, tiled=True)[0]
-    grad_hs = jnp.einsum("qrj,cj->qrc", rows_pixel, column_wide, precision=highest)
+    coef_resid = jnp.einsum("bq,bji->qji", basis, resid_wide, preferred_element_type=f32)
+    rows_back = split_dot("qjk,rk->qjr", coef_resid, back_kernel)
+    back_split = rows_back.reshape(subspace, chunk, n_spec, rows_here).transpose(2, 0, 1, 3)
+    got_rows = swap(back_split, "spec")
+    rows_pixel = got_rows.transpose(1, 3, 0, 2).reshape(subspace, rows_here, coarse_cols)
+    grad_hs = split_dot("qrj,cj->qrc", rows_pixel, column_kernel)
 
-    resp_basis = jnp.dot(response.astype(f32), basis_wide, precision=highest)
-    multi_pred = jnp.einsum("mq,qrc->mrc", resp_basis, latent.astype(f32), precision=highest)
+    resp_basis = jnp.dot(response, basis, preferred_element_type=f32)
+    multi_pred = split_dot("mq,qrc->mrc", resp_basis, latent)
     multi_resid = (multi_pred - multi_obs.astype(f32)).astype(jnp.bfloat16)
-    grad_ms = jnp.einsum(
-        "mq,mrc->qrc", resp_basis, multi_resid.astype(f32), precision=highest
-    )
+    grad_ms = split_dot("mq,mrc->qrc", resp_basis, multi_resid)
     gradient = grad_hs + grad_ms
     z_next = (latent.astype(f32) - step_size * gradient).astype(jnp.bfloat16)
     return (z_next, hs_residual)

time: 129 us -> 161 us (1.25)
  local copies, waits for them, and re-layouts: 18 us -> 59 us
  waiting for transfers between devices: 35.7 us -> 27.2 us
  matrix products: 25.5 us -> 20.7 us
  other arithmetic: 5.8 us -> 7.94 us
    reshape x0 -> x8, local copies, waits for them, and re-layouts: none -> 22.8 us  [the longest x3 12.2 us: swap(): flat = chunks.reshape(count, rows, -1)]
    transpose x1 -> x5, local copies, waits for them, and re-layouts: 0.2 us -> 17.3 us  [the longest x1 4.8 us: shards(): got_rows.transpose(1, 3, 0, 2).reshape(subspace, rows_here, coarse_cols)]
    convert_element_type x1 -> x3, other arithmetic: 0.19 us -> 7.27 us  [kernel_values(): jnp.where(inside, profile(offsets.astype(jnp.float32)) / energy, 0.0)]
    unnamed x22 -> x28, local copies, waits for them, and re-layouts: 11 us -> 4.25 us
    ppermute x2, waiting for transfers between devices: 14.8 us -> 8.55 us  [with_halo(): lax.ppermute(tail, axis, [(i, (i + 1) % count) for i in range(ends)])]
    ppermute x0 -> x2, local copies, waits for them, and re-layouts: none -> 4.42 us  [the longest x1 2.22 us: with_halo(): lax.ppermute(tail, axis, [(i, (i + 1) % count) for i in range(ends)])]
    dot_general x1, matrix products: 6.87 us -> 2.66 us  [shards(): jnp.einsum('qrc,csj->sqjr', latent, column_kernel.reshape(width_cols, n_s...]
    all_to_all x2 -> x0, other arithmetic: 3.84 us -> none  [the longest x1 1.92 us: shards(): lax.all_to_all(back_split, 'spec', split_axis=0, concat_axis=3, tiled=True)]
  transfers between devices with their start and end apart: 8 -> 8, of which waited for: 6 -> 4; matrix products, arithmetic and copies ran while one was open for 18% -> 26% of each run, Pallas kernels for 0% -> 0%
where the time goes in v3:
time: 161 us; the launch traced here: 158 us
  local copies, waits for them, and re-layouts  59 us (37%)
  starting transfers between devices  41.8 us (26%)
  waiting for transfers between devices  27.2 us (17%)
  matrix products  20.7 us (13%)
  other arithmetic  7.94 us (5%)
  between operations  1.68 us (1%)
    all_to_all x4, starting transfers between devices, swap(): flat = lax.all_to_all(flat, axis, split_axis=0, concat_axis=0, tiled=True)  23.4 us
    reshape x3, local copies, waits for them, and re-layouts, swap(): flat = chunks.reshape(count, rows, -1)  12.2 us
    all_to_all x4, waiting for transfers between devices, swap(): flat = lax.all_to_all(flat, axis, split_axis=0, concat_axis=0, tiled=True)  11.8 us
    dot_general x6, matrix products, split_dot(): jnp.einsum(spec, low, narrow, preferred_element_type=f32)  11.8 us
    ppermute x2, starting transfers between devices, with_halo(): lax.ppermute(head, axis, [((i + 1) % count, i) for i in range(ends)])  10.1 us
    ppermute x2, waiting for transfers between devices, with_halo(): lax.ppermute(tail, axis, [(i, (i + 1) % count) for i in range(ends)])  8.55 us
    ppermute x2, starting transfers between devices, with_halo(): lax.ppermute(tail, axis, [(i, (i + 1) % count) for i in range(ends)])  8.35 us
    convert_element_type x3, other arithmetic, kernel_values(): jnp.where(inside, profile(offsets.astype(jnp.float32)) / energy, 0.0)  7.27 us
  transfers between devices with their start and end apart: 8, of which 4 were waited for; matrix products, arithmetic and copies ran while one was open for 26% of the time, Pallas kernels for 0%

profile of v3, /device:TPU:24, one launch (start us, length us, event | category | flops | bytes accessed | tf_op | source)
XLA Modules:
  0.0 158.3 jit_solution(7802523919775438744)
XLA Ops:
  4.9 4.4 %fusion.15 = bf16[1024,256]{0,1:T(8,128)(2,1)S(1)} fusion(f32[]{:T(128)S(6)} %sqrt.2, s32[256]{0:T(256)S(1)} %iota_multiply_fusion), kind=kLoop, calls=%fused_computation.28 | loop fusion | flops 4718592 | bytes 525316 | tf_op jit(solution)/shard_map/convert_element_type | solution.py:44
  10.1 2.7 %convolution_bitcast_fusion = f32[16,32,16,16]{1,2,3,0:T(8,128)} fusion(bf16[1024,16,16,1]{0,2,3,1:T(8,128)(2,1)S(1)} %bitcast.85, bf16[32,16,1024]{2,1,0:T(8,128)(2,1)S(1)} %copy-done.1), kind=kOutput, calls=%fused_computation.10 | convolution fusion | flops 268435456 | bytes 2097152 | tf_op jit(solution)/shard_map/qrc,csj->sqjr/dot_general | solution.py:103
  12.8 4.4 %copy.49 = f32[16,32,16,16]{3,2,1,0:T(8,128)} copy(f32[16,32,16,16]{1,2,3,0:T(8,128)} %convolution_bitcast_fusion) | data formatting | bytes 1048576 | tf_op jit(solution)/shard_map/qrc,csj->sqjr/transpose | solution.py:103
  17.2 5.5 %reshape.61 = f32[16,8,1024]{2,1,0:T(8,128)} reshape(f32[16,32,16,16]{3,2,1,0:T(8,128)} %copy.49) | data formatting | bytes 1048576 | tf_op jit(solution)/shard_map/reshape | solution.py:80
  22.6 5.8 %all-to-all-start = ((f32[16,8,1024]{2,1,0:T(8,128)}), f32[16,8,1024]{2,1,0:T(8,128)S(1)}, u32[]{:S(2)}, u32[]{:S(2)}) async-start(f32[16,8,1024]{2,1,0:T(8,128)} %reshape.61), calls=%async_computation | async-start | bytes 1048576 | tf_op jit(solution)/shard_map/all_to_all | solution.py:81
  30.3 8.9 %all-to-all-done = f32[16,8,1024]{2,1,0:T(8,128)S(1)} async-done(((f32[16,8,1024]{2,1,0:T(8,128)}), f32[16,8,1024]{2,1,0:T(8,128)S(1)}, u32[]{:S(2)}, u32[]{:S(2)}) %all-to-all-start) | async-done | bytes 524320 | tf_op jit(solution)/shard_map/all_to_all | solution.py:81
  39.3 3.6 %all-to-all-start.1 = ((bf16[16,16,896]{2,1,0:T(8,128)(2,1)}), bf16[16,16,896]{2,1,0:T(8,128)(2,1)S(1)}, u32[]{:S(2)}, u32[]{:S(2)}) async-start(bf16[16,16,896]{2,1,0:T(8,128)(2,1)} %reshape.65), calls=%async_computation.1 | async-start | bytes 917504 | tf_op jit(solution)/shard_map/all_to_all | solution.py:81
  42.8 2.8 %reshape.62 = f32[16,32,16,16]{3,2,1,0:T(8,128)} reshape(f32[16,8,1024]{2,1,0:T(8,128)S(1)} %all-to-all-done) | data formatting | bytes 1048576 | tf_op jit(solution)/shard_map/reshape | solution.py:82
  45.6 3.8 %copy.50 = f32[32,16,16,16]{0,3,2,1:T(8,128)} copy(f32[32,16,16,16]{3,1,0,2:T(8,128)} %bitcast.77) | data formatting | bytes 1048576 | tf_op jit(solution)/shard_map/transpose | solution.py:110
  51.7 5.2 %collective-permute-start = (f32[32,16,256]{2,1,0:T(8,128)S(1)}, f32[32,16,256]{2,1,0:T(8,128)}, u32[]{:S(2)}, u32[]{:S(2)}) collective-permute-start(f32[32,16,256]{2,1,0:T(8,128)S(1)} %copy.51), channel_id=1, source_target_pairs={{0,16},{16,32},{32,48},{48,64},{64,80},{80,96},{96,112},{112,128},... | collective-permute-start | bytes 1572872 | tf_op jit(solution)/shard_map/ppermute | solution.py:21
  56.9 4.4 %collective-permute-start.1 = (f32[32,16,256]{2,1,0:T(8,128)S(1)}, f32[32,16,256]{2,1,0:T(8,128)}, u32[]{:S(2)}, u32[]{:S(2)}) collective-permute-start(f32[32,16,256]{2,1,0:T(8,128)S(1)} %copy.51), channel_id=1, source_target_pairs={{16,0},{32,16},{48,32},{64,48},{80,64},{96,80},{112,96},{128,112},... | collective-permute-start | bytes 1572872 | tf_op jit(solution)/shard_map/ppermute | solution.py:23
  63.2 2.5 %copy.58 = bf16[224,16,32]{0,2,1:T(8,128)(2,1)} copy(bf16[224,16,32]{2,1,0:T(8,128)(2,1)} %get-tuple-element.12) | data formatting | bytes 458752 | tf_op jit(solution)/shard_map/slice | solution.py:18
  65.7 3.2 %collective-permute-start.2 = (bf16[224,16,32]{0,2,1:T(8,128)(2,1)}, bf16[224,16,32]{0,2,1:T(8,128)(2,1)}, u32[]{:S(2)}, u32[]{:S(2)}) collective-permute-start(bf16[224,16,32]{0,2,1:T(8,128)(2,1)} %copy.58), channel_id=1, source_target_pairs={{0,16},{16,32},{32,48},{48,64},{64,80},{80,96},{96,112},{112,128},... | collective-permute-start | bytes 688136 | tf_op jit(solution)/shard_map/ppermute | solution.py:21
  70.4 5.7 %collective-permute-start.3 = (bf16[224,16,32]{0,2,1:T(8,128)(2,1)}, bf16[224,16,32]{0,2,1:T(8,128)(2,1)}, u32[]{:S(2)}, u32[]{:S(2)}) collective-permute-start(bf16[224,16,32]{0,2,1:T(8,128)(2,1)} %copy.59), channel_id=1, source_target_pairs={{16,0},{32,16},{48,32},{64,48},{80,64},{96,80},{112,96},{128,112},... | collective-permute-start | bytes 688136 | tf_op jit(solution)/shard_map/ppermute | solution.py:23
  76.3 8.6 %collective-permute-done.2 = bf16[224,16,32]{0,2,1:T(8,128)(2,1)} collective-permute-done((bf16[224,16,32]{0,2,1:T(8,128)(2,1)}, bf16[224,16,32]{0,2,1:T(8,128)(2,1)}, u32[]{:S(2)}, u32[]{:S(2)}) %collective-permute-start.2) | collective-permute-done | bytes 229408 | tf_op jit(solution)/shard_map/ppermute | solution.py:21
  87.1 6.8 %collective-permute-done.3 = bf16[224,16,32]{0,2,1:T(8,128)(2,1)} collective-permute-done((bf16[224,16,32]{0,2,1:T(8,128)(2,1)}, bf16[224,16,32]{0,2,1:T(8,128)(2,1)}, u32[]{:S(2)}, u32[]{:S(2)}) %collective-permute-start.3) | collective-permute-done | bytes 229408 | tf_op jit(solution)/shard_map/ppermute | solution.py:23
  103.0 8.4 %all-to-all-start.3 = ((bf16[16,16,896]{2,1,0:T(8,128)(2,1)}), bf16[16,16,896]{2,1,0:T(8,128)(2,1)S(1)}, u32[]{:S(2)}, u32[]{:S(2)}) async-start(bf16[16,16,896]{2,1,0:T(8,128)(2,1)} %reshape_reshape.7), calls=%async_computation.3 | async-start | bytes 917504 | tf_op jit(solution)/shard_map/all_to_all | solution.py:81
  114.3 4.0 %copy.66 = f32[16,32,16,16]{3,2,1,0:T(8,128)} copy(f32[16,32,16,16]{1,3,0,2:T(8,128)} %bitcast.80) | data formatting | bytes 1048576 | tf_op jit(solution)/shard_map/transpose | solution.py:128
  118.3 5.4 %reshape.67 = f32[16,8,1024]{2,1,0:T(8,128)} reshape(f32[16,32,16,16]{3,2,1,0:T(8,128)} %copy.66) | data formatting | bytes 1048576 | tf_op jit(solution)/shard_map/reshape | solution.py:80
  124.5 5.7 %all-to-all-start.2 = ((f32[16,8,1024]{2,1,0:T(8,128)}), f32[16,8,1024]{2,1,0:T(8,128)S(1)}, u32[]{:S(2)}, u32[]{:S(2)}) async-start(f32[16,8,1024]{2,1,0:T(8,128)} %reshape.67), calls=%async_computation.2 | async-start | bytes 1048576 | tf_op jit(solution)/shard_map/all_to_all | solution.py:81
  138.2 2.9 %all-to-all-done.2 = f32[16,8,1024]{2,1,0:T(8,128)S(1)} async-done(((f32[16,8,1024]{2,1,0:T(8,128)}), f32[16,8,1024]{2,1,0:T(8,128)S(1)}, u32[]{:S(2)}, u32[]{:S(2)}) %all-to-all-start.2) | async-done | bytes 524320 | tf_op jit(solution)/shard_map/all_to_all | solution.py:81
  141.1 2.7 %reshape.68 = f32[16,32,16,16]{3,2,1,0:T(8,128)} reshape(f32[16,8,1024]{2,1,0:T(8,128)S(1)} %all-to-all-done.2) | data formatting | bytes 1048576 | tf_op jit(solution)/shard_map/reshape | solution.py:82
  143.8 4.8 %copy.67 = f32[32,16,16,16]{0,3,2,1:T(8,128)} copy(f32[32,16,16,16]{1,3,0,2:T(8,128)} %bitcast.78) | data formatting | bytes 1048576 | tf_op jit(solution)/shard_map/transpose | solution.py:130
  152.6 5.7 %fusion.3 = bf16[32,16,1024]{2,1,0:T(8,128)(2,1)} fusion(f32[32,16,1024]{2,0,1:T(8,128)} %fusion.76, f32[32,16,1024]{2,0,1:T(8,128)S(1)} %copy-done.2, f32[32,16,1024]{2,1,0:T(8,128)S(1)} %fusion.26, bf16[32,16,1024]{2,1,0:T(8,128)(2,1)S(1)} %copy-done.1, bf16[1024,256]{0,1:T(8,128)(2,1)S(1)} %copy-done.6, f32[32,16,256]{2,1,0:T(8,128)S(1)} %copy.68), kind=kOutput, calls=%fused_computation.6 | convolution fusion | flops 272498688 | bytes 9437184 | tf_op jit(solution)/shard_map/qrj,cj->qrc/dot_general | solution.py:72
  (68 shorter events, 38.9 us)
Async XLA Ops:
  0.6 98.8 %copy-start = (bf16[224,32]{0,1:T(8,128)(2,1)S(1)}, bf16[224,32]{0,1:T(8,128)(2,1)}, u32[]{:S(2)}) copy-start(bf16[224,32]{0,1:T(8,128)(2,1)} %param.6) | copy-start | bytes 43012
  0.6 9.5 %copy-start.1 = (bf16[32,16,1024]{2,1,0:T(8,128)(2,1)S(1)}, bf16[32,16,1024]{2,1,0:T(8,128)(2,1)}, u32[]{:S(2)}) copy-start(bf16[32,16,1024]{2,1,0:T(8,128)(2,1)} %param.5) | copy-start | bytes 3145732
  9.3 0.8 copy-start.5
  17.2 11.2 %copy-start.9 = (bf16[14,64,256]{2,1,0:T(8,128)(2,1)S(1)}, bf16[14,64,256]{2,1,0:T(8,128)(2,1)}, u32[]{:S(2)}) copy-start(bf16[14,64,256]{2,1,0:T(8,128)(2,1)} %param.8) | copy-start | bytes 1376260
  22.6 16.6 %all-to-all-start = ((f32[16,8,1024]{2,1,0:T(8,128)}), f32[16,8,1024]{2,1,0:T(8,128)S(1)}, u32[]{:S(2)}, u32[]{:S(2)}) async-start(f32[16,8,1024]{2,1,0:T(8,128)} %reshape.61), calls=%async_computation | async-start | bytes 1048576 | tf_op jit(solution)/shard_map/all_to_all | solution.py:81
  39.3 22.1 %all-to-all-start.1 = ((bf16[16,16,896]{2,1,0:T(8,128)(2,1)}), bf16[16,16,896]{2,1,0:T(8,128)(2,1)S(1)}, u32[]{:S(2)}, u32[]{:S(2)}) async-start(bf16[16,16,896]{2,1,0:T(8,128)(2,1)} %reshape.65), calls=%async_computation.1 | async-start | bytes 917504 | tf_op jit(solution)/shard_map/all_to_all | solution.py:81
  51.7 44.4 %collective-permute-start = (f32[32,16,256]{2,1,0:T(8,128)S(1)}, f32[32,16,256]{2,1,0:T(8,128)}, u32[]{:S(2)}, u32[]{:S(2)}) collective-permute-start(f32[32,16,256]{2,1,0:T(8,128)S(1)} %copy.51), channel_id=1, source_target_pairs={{0,16},{16,32},{32,48},{48,64},{64,80},{80,96},{96,112},{112,128},... | collective-permute-start | bytes 1572872 | tf_op jit(solution)/shard_map/ppermute | solution.py:21
  56.9 39.2 %collective-permute-start.1 = (f32[32,16,256]{2,1,0:T(8,128)S(1)}, f32[32,16,256]{2,1,0:T(8,128)}, u32[]{:S(2)}, u32[]{:S(2)}) collective-permute-start(f32[32,16,256]{2,1,0:T(8,128)S(1)} %copy.51), channel_id=1, source_target_pairs={{16,0},{32,16},{48,32},{64,48},{80,64},{96,80},{112,96},{128,112},... | collective-permute-start | bytes 1572872 | tf_op jit(solution)/shard_map/ppermute | solution.py:23
  65.7 19.1 %collective-permute-start.2 = (bf16[224,16,32]{0,2,1:T(8,128)(2,1)}, bf16[224,16,32]{0,2,1:T(8,128)(2,1)}, u32[]{:S(2)}, u32[]{:S(2)}) collective-permute-start(bf16[224,16,32]{0,2,1:T(8,128)(2,1)} %copy.58), channel_id=1, source_target_pairs={{0,16},{16,32},{32,48},{48,64},{64,80},{80,96},{96,112},{112,128},... | collective-permute-start | bytes 688136 | tf_op jit(solution)/shard_map/ppermute | solution.py:21
  70.4 23.5 %collective-permute-start.3 = (bf16[224,16,32]{0,2,1:T(8,128)(2,1)}, bf16[224,16,32]{0,2,1:T(8,128)(2,1)}, u32[]{:S(2)}, u32[]{:S(2)}) collective-permute-start(bf16[224,16,32]{0,2,1:T(8,128)(2,1)} %copy.59), channel_id=1, source_target_pairs={{16,0},{32,16},{48,32},{64,48},{80,64},{96,80},{112,96},{128,112},... | collective-permute-start | bytes 688136 | tf_op jit(solution)/shard_map/ppermute | solution.py:23
  76.3 19.8 %copy-start.12 = (bf16[128,768]{1,0:T(8,128)(2,1)S(1)}, bf16[128,768]{1,0:T(8,128)(2,1)}, u32[]{:S(2)}) copy-start(bf16[128,768]{1,0:T(8,128)(2,1)} %fusion.39) | copy-start | bytes 589828
  97.7 2.2 %copy-start.3 = (bf16[224,16,32]{2,0,1:T(8,128)(2,1)S(1)}, bf16[224,16,32]{2,0,1:T(8,128)(2,1)}, u32[]{:S(2)}) copy-start(bf16[224,16,32]{2,0,1:T(8,128)(2,1)} %copy.60) | copy-start | bytes 688132
  97.7 2.2 %copy-start.4 = (bf16[224,16,32]{2,0,1:T(8,128)(2,1)S(1)}, bf16[224,16,32]{2,0,1:T(8,128)(2,1)}, u32[]{:S(2)}) copy-start(bf16[224,16,32]{2,0,1:T(8,128)(2,1)} %copy.62) | copy-start | bytes 688132
  101.3 10.1 %copy-start.11 = (bf16[8,224]{1,0:T(8,128)(2,1)S(1)}, bf16[8,224]{1,0:T(8,128)(2,1)}, u32[]{:S(2)}) copy-start(bf16[8,224]{1,0:T(8,128)(2,1)} %param.7) | copy-start | bytes 10756
  103.0 20.7 %all-to-all-start.3 = ((bf16[16,16,896]{2,1,0:T(8,128)(2,1)}), bf16[16,16,896]{2,1,0:T(8,128)(2,1)S(1)}, u32[]{:S(2)}, u32[]{:S(2)}) async-start(bf16[16,16,896]{2,1,0:T(8,128)(2,1)} %reshape_reshape.7), calls=%async_computation.3 | async-start | bytes 917504 | tf_op jit(solution)/shard_map/all_to_all | solution.py:81
  123.7 7.7 %copy-start.10 = (bf16[8,16,1024]{2,1,0:T(8,128)(2,1)S(1)}, bf16[8,16,1024]{2,1,0:T(8,128)(2,1)}, u32[]{:S(2)}) copy-start(bf16[8,16,1024]{2,1,0:T(8,128)(2,1)} %param.9) | copy-start | bytes 786436
  123.7 0.8 copy-start.7
  124.5 16.6 %all-to-all-start.2 = ((f32[16,8,1024]{2,1,0:T(8,128)}), f32[16,8,1024]{2,1,0:T(8,128)S(1)}, u32[]{:S(2)}, u32[]{:S(2)}) async-start(f32[16,8,1024]{2,1,0:T(8,128)} %reshape.67), calls=%async_computation.2 | async-start | bytes 1048576 | tf_op jit(solution)/shard_map/all_to_all | solution.py:81
  132.7 3.7 %copy-start.8 = (bf16[16,16,896]{2,1,0:T(8,128)(2,1)S(1)}, bf16[16,16,896]{2,1,0:T(8,128)(2,1)}, u32[]{:S(2)}) copy-start(bf16[16,16,896]{2,1,0:T(8,128)(2,1)} %copy-done.7) | copy-start | bytes 1376260
  148.6 2.3 %copy-start.6 = (bf16[1024,256]{0,1:T(8,128)(2,1)S(1)}, bf16[1024,256]{0,1:T(8,128)(2,1)}, u32[]{:S(2)}) copy-start(bf16[1024,256]{0,1:T(8,128)(2,1)} %copy-done.5) | copy-start | bytes 1572868
  151.0 1.6 %copy-start.2 = (f32[32,16,1024]{2,0,1:T(8,128)S(1)}, f32[32,16,1024]{2,0,1:T(8,128)}, u32[]{:S(2)}) copy-start(f32[32,16,1024]{2,0,1:T(8,128)} %fusion.73) | copy-start | bytes 6291460

commit v4 on v2

--- a/solution.py
+++ b/solution.py
@@ -64,56 +64,91 @@
     return kernel_values(fine_rows - DECIM * coarse + HALO)
 
 
+def split_dot(spec, wide, narrow):
+    high_wide = lax.reduce_precision(wide, exponent_bits=8, mantissa_bits=7)
+    high = high_wide.astype(jnp.bfloat16)
+    low = (wide - high_wide).astype(jnp.bfloat16)
+    f32 = jnp.float32
+    return jnp.einsum(spec, high, narrow, preferred_element_type=f32) + jnp.einsum(
+        spec, low, narrow, preferred_element_type=f32
+    )
+
+
+def neighbours(parts, axis):
+    count = lax.axis_size(axis)
+    ends = count - 1
+    flat = jnp.concatenate([p.reshape(-1) for p in parts])
+    from_prev = lax.ppermute(flat, axis, [(i, i + 1) for i in range(ends)])
+    from_next = lax.ppermute(flat, axis, [(i + 1, i) for i in range(ends)])
+    out = []
+    for got in (from_prev, from_next):
+        pieces, at = [], 0
+        for p in parts:
+            pieces.append(got[at : at + p.size].reshape(p.shape))
+            at += p.size
+        out.append(pieces)
+    return out
+
+
 def shards(latent, basis, response, hyper_obs, multi_obs):
     highest = lax.Precision.HIGHEST
     f32 = jnp.float32
+    bf16 = jnp.bfloat16
     n_spec = lax.axis_size("spec")
+    n_tile = lax.axis_size("tile")
+    tile_index = lax.axis_index("tile")
     group, coarse_rows, coarse_cols = hyper_obs.shape
     rows_dev = coarse_rows * DECIM
+    rim = HALO // DECIM
     subspace, rows_here, width_cols = latent.shape
     chunk = coarse_cols // n_spec
     basis_wide = basis.astype(f32)
     column_kernel = column_matrix(width_cols, coarse_cols)
-    column_wide = column_kernel.astype(f32)
 
     cols_done = jnp.einsum(
         "qrc,csj->sqjr",
         latent,
         column_kernel.reshape(width_cols, n_spec, chunk),
         preferred_element_type=f32,
-    )
+    ).astype(bf16)
     tile_rows = lax.all_to_all(cols_done, "spec", split_axis=0, concat_axis=3, tiled=True)[0]
-    padded = with_halo(tile_rows, (("tile", 2),), HALO)
-    coef_blurred = jnp.einsum(
-        "qjr,ir->qji", padded, row_matrix(rows_dev).astype(f32), precision=highest
-    )
-    blurred = jnp.einsum("bq,qji->bji", basis_wide, coef_blurred, precision=highest)
 
     obs_split = hyper_obs.reshape(group, coarse_rows, n_spec, chunk).transpose(2, 0, 3, 1)
     obs_cols = lax.all_to_all(obs_split, "spec", split_axis=0, concat_axis=1, tiled=True)[0]
-    resid_cols = (blurred - obs_cols.astype(f32)).astype(jnp.bfloat16)
 
+    obs_head = lax.slice_in_dim(obs_cols, 0, rim, axis=2)
+    obs_tail = lax.slice_in_dim(obs_cols, coarse_rows - rim, coarse_rows, axis=2)
+    (prev_rows, prev_tail, _), (next_rows, _, next_head) = neighbours(
+        (tile_rows, obs_tail, obs_head), "tile"
+    )
+    padded = jnp.concatenate([prev_rows, tile_rows, next_rows], axis=2)
+    obs_wide = jnp.concatenate([prev_tail, obs_cols, next_head], axis=2)
+    row_kernel = row_matrix(rows_dev + 2 * (rows_dev - HALO))
+    coef_blurred = jnp.einsum("qjr,ir->qji", padded, row_kernel, preferred_element_type=f32)
+    blurred = split_dot("qji,bq->bji", coef_blurred, basis)
+    coarse_at = jnp.arange(coarse_rows + 2 * rim) + tile_index * coarse_rows - rim
+    inside = (coarse_at >= 0) & (coarse_at < n_tile * coarse_rows)
+    resid_wide = jnp.where(inside, blurred - obs_wide.astype(f32), 0.0).astype(bf16)
+
+    resid_cols = lax.slice_in_dim(resid_wide, rim, rim + coarse_rows, axis=2)
     resid_split = resid_cols.reshape(n_spec, group, chunk, coarse_rows)
     resid_bands = lax.all_to_all(resid_split, "spec", split_axis=0, concat_axis=2, tiled=True)[0]
     hs_residual = resid_bands.transpose(0, 2, 1)
 
-    coef_resid = jnp.einsum("bq,bji->qji", basis, resid_cols, preferred_element_type=f32)
-    coarse_padded = with_halo(coef_resid, (("tile", 2),), HALO // DECIM)
-    rows_back = jnp.einsum(
-        "qjk,rk->qjr", coarse_padded, back_matrix(rows_dev).astype(f32), precision=highest
-    )
+    coef_resid = jnp.einsum("bq,bji->qji", basis, resid_wide, preferred_element_type=f32)
+    rows_back = split_dot("qjk,rk->qjr", coef_resid, back_matrix(rows_dev))
     back_split = rows_back.reshape(subspace, chunk, n_spec, rows_here).transpose(2, 0, 3, 1)
     rows_pixel = lax.all_to_all(back_split, "spec", split_axis=0, concat_axis=3, tiled=True)[0]
-    grad_hs = jnp.einsum("qrj,cj->qrc", rows_pixel, column_wide, precision=highest)
+    grad_hs = split_dot("qrj,cj->qrc", rows_pixel, column_kernel)
 
     resp_basis = jnp.dot(response.astype(f32), basis_wide, precision=highest)
     multi_pred = jnp.einsum("mq,qrc->mrc", resp_basis, latent.astype(f32), precision=highest)
-    multi_resid = (multi_pred - multi_obs.astype(f32)).astype(jnp.bfloat16)
+    multi_resid = (multi_pred - multi_obs.astype(f32)).astype(bf16)
     grad_ms = jnp.einsum(
         "mq,mrc->qrc", resp_basis, multi_resid.astype(f32), precision=highest
     )
     gradient = grad_hs + grad_ms
-    z_next = (latent.astype(f32) - step_size * gradient).astype(jnp.bfloat16)
+    z_next = (latent.astype(f32) - step_size * gradient).astype(bf16)
     return (z_next, hs_residual)
 
 

time: 129 us -> 146 us (1.13)
  local copies, waits for them, and re-layouts: 18 us -> 38.8 us
  starting transfers between devices: 40.6 us -> 28.9 us
  waiting for transfers between devices: 35.7 us -> 43.9 us
  matrix products: 25.5 us -> 29.1 us
  other arithmetic: 5.8 us -> 2.56 us
    ppermute x4 -> x2, starting transfers between devices: 18.4 us -> 9.58 us  [the longest x1 5.17 us: neighbours(): from_prev = lax.ppermute(flat, axis, [(i, i + 1) for i in range(ends)])]
    slice x2 -> x9, local copies, waits for them, and re-layouts: 0.98 us -> 7.44 us  [the longest x6 5.43 us: neighbours(): pieces.append(got[at:at + p.size].reshape(p.shape))]
    ppermute x4 -> x2, waiting for transfers between devices: 22.5 us -> 28.4 us  [the longest x1 15.7 us: neighbours(): from_next = lax.ppermute(flat, axis, [(i + 1, i) for i in range(ends)])]
    all_to_all x1 -> x2, local copies, waits for them, and re-layouts: 0.58 us -> 5.95 us  [shards(): lax.all_to_all(cols_done, 'spec', split_axis=0, concat_axis=3, tiled=True)]
    dot_general x5 -> x8, matrix products: 13.4 us -> 17.3 us  [the longest x3 8.44 us: split_dot(): jnp.einsum(spec, low, narrow, preferred_element_type=f32)]
    reshape x0 -> x6, local copies, waits for them, and re-layouts: none -> 3.5 us  [the longest x2 2.3 us: neighbours(): flat = jnp.concatenate([p.reshape(-1) for p in parts])]
    all_to_all x1, starting transfers between devices: 7.1 us -> 3.79 us  [shards(): lax.all_to_all(back_split, 'spec', split_axis=0, concat_axis=3, tiled=True)]
    unnamed x22 -> x26, local copies, waits for them, and re-layouts: 11 us -> 14.2 us
  transfers between devices with their start and end apart: 8 -> 6, of which waited for: 6 -> 6; matrix products, arithmetic and copies ran while one was open for 18% -> 18% of each run, Pallas kernels for 0% -> 0%
where the time goes in v4:
time: 146 us; the launch traced here: 145 us
  waiting for transfers between devices  43.9 us (30%)
  local copies, waits for them, and re-layouts  38.8 us (27%)
  matrix products  29.1 us (20%)
  starting transfers between devices  28.9 us (20%)
  other arithmetic  2.56 us (2%)
  between operations  1.71 us (1%)
    ppermute x1, waiting for transfers between devices, neighbours(): from_next = lax.ppermute(flat, axis, [(i + 1, i) for i in range(ends)])  15.7 us
    unnamed x26, local copies, waits for them, and re-layouts  14.2 us
    ppermute x1, waiting for transfers between devices, neighbours(): from_prev = lax.ppermute(flat, axis, [(i, i + 1) for i in range(ends)])  12.7 us
    dot_general x3, matrix products, split_dot(): jnp.einsum(spec, low, narrow, preferred_element_type=f32)  8.44 us
    dot_general x1, matrix products, shards(): jnp.einsum('qrc,csj->sqjr', latent, column_kernel.reshape(width_cols, n_s...  7.78 us
    all_to_all x1, waiting for transfers between devices, shards(): lax.all_to_all(cols_done, 'spec', split_axis=0, concat_axis=3, tiled=True)  6.16 us
    all_to_all x2, local copies, waits for them, and re-layouts, shards(): lax.all_to_all(cols_done, 'spec', split_axis=0, concat_axis=3, tiled=True)  5.95 us
    all_to_all x1, starting transfers between devices, shards(): lax.all_to_all(cols_done, 'spec', split_axis=0, concat_axis=3, tiled=True)  5.76 us
  transfers between devices with their start and end apart: 6, of which 6 were waited for; matrix products, arithmetic and copies ran while one was open for 18% of the time, Pallas kernels for 0%

profile of v4, /device:TPU:24, one launch (start us, length us, event | category | flops | bytes accessed | tf_op | source)
XLA Modules:
  0.0 145.0 jit_solution(18397049891015588113)
XLA Ops:
  2.0 7.8 %fusion.147 = bf16[16,16,16,32]{3,2,1,0:T(8,128)(2,1)S(1)} fusion(bf16[32,16,1024]{2,1,0:T(8,128)(2,1)} %param.5, f32[]{:T(128)S(6)} %sqrt.2, s32[16,16]{1,0:T(8,128)S(1)} %add_multiply_fusion), kind=kOutput, calls=%fused_computation.175 | convolution fusion | flops 273285120 | bytes 1311748 | tf_op jit(solution)/shard_map/qrc,csj->sqjr/dot_general | solution.py:108
  9.8 1.7 %reshape.111 = bf16[16,2,4096]{2,1,0:T(2,128)(2,1)} reshape(bf16[16,16,16,32]{3,2,1,0:T(8,128)(2,1)S(1)} %fusion.147) | data formatting | bytes 524288
  11.5 5.8 %all-to-all-start = ((bf16[16,2,4096]{2,1,0:T(2,128)(2,1)}), bf16[16,2,4096]{2,1,0:T(2,128)(2,1)S(1)}, u32[]{:S(2)}, u32[]{:S(2)}) async-start(bf16[16,2,4096]{2,1,0:T(2,128)(2,1)} %reshape.111), calls=%async_computation | async-start | bytes 524288 | tf_op jit(solution)/shard_map/all_to_all | solution.py:114
  19.1 6.2 %all-to-all-done = bf16[16,2,4096]{2,1,0:T(2,128)(2,1)S(1)} async-done(((bf16[16,2,4096]{2,1,0:T(2,128)(2,1)}), bf16[16,2,4096]{2,1,0:T(2,128)(2,1)S(1)}, u32[]{:S(2)}, u32[]{:S(2)}) %all-to-all-start) | async-done | bytes 262176 | tf_op jit(solution)/shard_map/all_to_all | solution.py:114
  25.3 4.2 %all-to-all-start.1 = ((bf16[16,2,7168]{2,1,0:T(2,128)(2,1)}), bf16[16,2,7168]{2,1,0:T(2,128)(2,1)}, u32[]{:S(2)}, u32[]{:S(2)}) async-start(bf16[16,2,7168]{2,1,0:T(2,128)(2,1)} %reshape.113), calls=%async_computation.1 | async-start | bytes 917504 | tf_op jit(solution)/shard_map/all_to_all | solution.py:117
  31.2 4.8 %copy.40 = bf16[1,32,16,16,16]{4,3,2,1,0:T(8,128)(2,1)S(1)} copy(bf16[1,32,16,16,16]{1,2,4,3,0:T(8,128)(2,1)} %bitcast_bitcast_fusion) | data formatting | bytes 524288 | tf_op jit(solution)/shard_map/all_to_all | solution.py:114
  38.0 1.7 %all-to-all-done.1 = bf16[16,2,7168]{2,1,0:T(2,128)(2,1)} async-done(((bf16[16,2,7168]{2,1,0:T(2,128)(2,1)}), bf16[16,2,7168]{2,1,0:T(2,128)(2,1)}, u32[]{:S(2)}, u32[]{:S(2)}) %all-to-all-start.1) | async-done | bytes 458784 | tf_op jit(solution)/shard_map/all_to_all | solution.py:117
  39.7 2.1 %reshape.114 = bf16[16,14,16,64]{3,2,1,0:T(8,128)(2,1)S(1)} reshape(bf16[16,2,7168]{2,1,0:T(2,128)(2,1)} %all-to-all-done.1) | data formatting | bytes 917504
  43.1 1.9 %reshape.98 = bf16[114688]{0:T(1024)(128)(2,1)S(1)} reshape(bf16[224,16,32]{2,1,0:T(8,128)(2,1)} %get-tuple-element.7) | data formatting | bytes 458752 | tf_op jit(solution)/shard_map/reshape | solution.py:80
  46.9 5.2 %collective-permute-start = (bf16[360448]{0:T(1024)(128)(2,1)}, bf16[360448]{0:T(1024)(128)(2,1)}, u32[]{:S(2)}, u32[]{:S(2)}) collective-permute-start(bf16[360448]{0:T(1024)(128)(2,1)} %constant_dynamic-update-slice_fusion), channel_id=1, source_target_pairs={{0,16},{16,32},{32,48},{48,64},{64,80},{80,96},{96,112},{112,128},... | collective-permute-start | bytes 2162696 | tf_op jit(solution)/shard_map/ppermute | solution.py:81
  52.0 4.4 %collective-permute-start.1 = (bf16[360448]{0:T(1024)(128)(2,1)}, bf16[360448]{0:T(1024)(128)(2,1)}, u32[]{:S(2)}, u32[]{:S(2)}) collective-permute-start(bf16[360448]{0:T(1024)(128)(2,1)} %constant_dynamic-update-slice_fusion), channel_id=1, source_target_pairs={{16,0},{32,16},{48,32},{64,48},{80,64},{96,80},{112,96},{128,112},... | collective-permute-start | bytes 2162696 | tf_op jit(solution)/shard_map/ppermute | solution.py:82
  57.8 12.7 %collective-permute-done = bf16[360448]{0:T(1024)(128)(2,1)} collective-permute-done((bf16[360448]{0:T(1024)(128)(2,1)}, bf16[360448]{0:T(1024)(128)(2,1)}, u32[]{:S(2)}, u32[]{:S(2)}) %collective-permute-start) | collective-permute-done | bytes 720928 | tf_op jit(solution)/shard_map/ppermute | solution.py:81
  72.3 15.7 %collective-permute-done.1 = bf16[360448]{0:T(1024)(128)(2,1)} collective-permute-done((bf16[360448]{0:T(1024)(128)(2,1)}, bf16[360448]{0:T(1024)(128)(2,1)}, u32[]{:S(2)}, u32[]{:S(2)}) %collective-permute-start.1) | collective-permute-done | bytes 720928 | tf_op jit(solution)/shard_map/ppermute | solution.py:82
  92.9 2.9 %fusion.63 = (bf16[32,16,128]{2,1,0:T(8,128)(2,1)S(1)}, bf16[32,16,128]{2,1,0:T(8,128)(2,1)S(1)}) fusion(f32[]{:T(128)S(6)} %sqrt.2, s32[128]{0:T(128)S(1)} %iota_multiply_fusion.1, s32[768]{0:T(1024)S(1)} %iota_add_fusion, bf16[32,16,256]{2,1,0:T(8,128)(2,1)} %slice.62, bf16[32,16,256]{2,1,0:T(8,128)(2,1)S(1)} %copy.43, bf16[32,16,256]{2,1,0:T(8,128)(2,1)} %slice.60), kind=kOutput, calls=%fused_computation.83 | convolution fusion | flops 105054208 | bytes 1052164 | tf_op jit(solution)/shard_map/qjr,ir->qji/dot_general | solution.py:127
  99.4 5.6 %all-to-all-start.3 = ((bf16[16,2,7168]{2,1,0:T(2,128)(2,1)}), bf16[16,2,7168]{2,1,0:T(2,128)(2,1)S(1)}, u32[]{:S(2)}, u32[]{:S(2)}) async-start(bf16[16,2,7168]{2,1,0:T(2,128)(2,1)} %reshape.117), calls=%async_computation.3 | async-start | bytes 917504 | tf_op jit(solution)/shard_map/all_to_all | solution.py:135
  107.4 1.6 %copy.92 = f32[16,32,16,16]{1,2,3,0:T(8,128)} copy(f32[16,32,16,16]{1,2,0,3:T(8,128)S(1)} %bitcast.95) | data formatting | bytes 1048576 | tf_op jit(solution)/shard_map/transpose | solution.py:140
  109.0 3.2 %reshape.115 = f32[16,1,8192]{2,1,0:T(1,128)} reshape(f32[16,16,16,32]{3,2,1,0:T(8,128)} %bitcast.96) | data formatting | bytes 1048576
  112.2 3.0 %all-to-all-done.3 = bf16[16,2,7168]{2,1,0:T(2,128)(2,1)S(1)} async-done(((bf16[16,2,7168]{2,1,0:T(2,128)(2,1)}), bf16[16,2,7168]{2,1,0:T(2,128)(2,1)S(1)}, u32[]{:S(2)}, u32[]{:S(2)}) %all-to-all-start.3) | async-done | bytes 458784 | tf_op jit(solution)/shard_map/all_to_all | solution.py:135
  115.1 3.8 %all-to-all-start.2 = ((f32[16,1,8192]{2,1,0:T(1,128)}), f32[16,1,8192]{2,1,0:T(1,128)S(1)}, u32[]{:S(2)}, u32[]{:S(2)}) async-start(f32[16,1,8192]{2,1,0:T(1,128)} %reshape.115), calls=%async_computation.2 | async-start | bytes 1048576 | tf_op jit(solution)/shard_map/all_to_all | solution.py:141
  120.7 2.4 %fusion.152 = f32[32,16,1024]{2,0,1:T(8,128)} fusion(f32[8,32,1]{1,0,2:T(8,128)S(1)} %convolution_bitcast_fusion.1, bf16[8,16,1024]{2,0,1:T(8,128)(2,1)S(1)} %fusion.6), kind=kOutput, calls=%fused_computation.177 | convolution fusion | flops 50331648 | bytes 2360320 | tf_op jit(solution)/shard_map/mq,mrc->qrc/dot_general | solution.py:147
  124.9 4.7 %all-to-all-done.2 = f32[16,1,8192]{2,1,0:T(1,128)S(1)} async-done(((f32[16,1,8192]{2,1,0:T(1,128)}), f32[16,1,8192]{2,1,0:T(1,128)S(1)}, u32[]{:S(2)}, u32[]{:S(2)}) %all-to-all-start.2) | async-done | bytes 524320 | tf_op jit(solution)/shard_map/all_to_all | solution.py:141
  130.1 1.9 %reduce = f32[16,8192]{1,0:T(8,128)S(1)} reduce(f32[16,1,8192]{2,1,0:T(1,128)S(1)} %all-to-all-done.2, f32[]{:T(128)} %broadcast.90), dimensions={1}, to_apply=%all_to_all.44.reduce_sub_computation | reduce | bytes 1048580 | tf_op jit(solution)/shard_map/all_to_all | solution.py:141
  133.9 4.5 %fusion.35 = f32[32,16,1024]{2,1,0:T(8,128)S(1)} fusion(f32[]{:T(128)S(6)} %sqrt.2, s32[256]{0:T(256)S(1)} %iota_multiply_fusion, f32[32,16,256]{2,1,0:T(8,128)S(1)} %copy.54), kind=kOutput, calls=%fused_computation.52 | convolution fusion | flops 273416192 | bytes 2622468 | tf_op jit(solution)/shard_map/qrj,cj->qrc/dot_general | solution.py:72
  138.4 6.6 %fusion.2 = bf16[32,16,1024]{2,1,0:T(8,128)(2,1)} fusion(f32[32,16,1024]{2,0,1:T(8,128)S(1)} %copy-done.1, f32[32,16,1024]{2,1,0:T(8,128)S(1)} %fusion.35, bf16[32,16,1024]{2,1,0:T(8,128)(2,1)S(1)} %copy-done.3, f32[]{:T(128)S(6)} %sqrt.2, s32[256]{0:T(256)S(1)} %iota_multiply_fusion, f32[32,16,256]{2,1,0:T(8,128)S(1)} %copy.54), kind=kOutput, calls=%fused_computation.3 | convolution fusion | flops 276692992 | bytes 6816772 | tf_op jit(solution)/shard_map/qrj,cj->qrc/dot_general | solution.py:72
  (60 shorter events, 29.2 us)
Async XLA Ops:
  0.6 95.2 %copy-start = (bf16[224,32]{0,1:T(8,128)(2,1)S(1)}, bf16[224,32]{0,1:T(8,128)(2,1)}, u32[]{:S(2)}) copy-start(bf16[224,32]{0,1:T(8,128)(2,1)} %param.6) | copy-start | bytes 43012
  9.8 7.5 %copy-start.4 = (bf16[14,64,256]{2,1,0:T(8,128)(2,1)S(1)}, bf16[14,64,256]{2,1,0:T(8,128)(2,1)}, u32[]{:S(2)}) copy-start(bf16[14,64,256]{2,1,0:T(8,128)(2,1)} %param.8) | copy-start | bytes 1376260
  11.5 13.8 %all-to-all-start = ((bf16[16,2,4096]{2,1,0:T(2,128)(2,1)}), bf16[16,2,4096]{2,1,0:T(2,128)(2,1)S(1)}, u32[]{:S(2)}, u32[]{:S(2)}) async-start(bf16[16,2,4096]{2,1,0:T(2,128)(2,1)} %reshape.111), calls=%async_computation | async-start | bytes 524288 | tf_op jit(solution)/shard_map/all_to_all | solution.py:114
  25.3 14.4 %all-to-all-start.1 = ((bf16[16,2,7168]{2,1,0:T(2,128)(2,1)}), bf16[16,2,7168]{2,1,0:T(2,128)(2,1)}, u32[]{:S(2)}, u32[]{:S(2)}) async-start(bf16[16,2,7168]{2,1,0:T(2,128)(2,1)} %reshape.113), calls=%async_computation.1 | async-start | bytes 917504 | tf_op jit(solution)/shard_map/all_to_all | solution.py:117
  46.9 23.7 %collective-permute-start = (bf16[360448]{0:T(1024)(128)(2,1)}, bf16[360448]{0:T(1024)(128)(2,1)}, u32[]{:S(2)}, u32[]{:S(2)}) collective-permute-start(bf16[360448]{0:T(1024)(128)(2,1)} %constant_dynamic-update-slice_fusion), channel_id=1, source_target_pairs={{0,16},{16,32},{32,48},{48,64},{64,80},{80,96},{96,112},{112,128},... | collective-permute-start | bytes 2162696 | tf_op jit(solution)/shard_map/ppermute | solution.py:81
  52.0 36.0 %collective-permute-start.1 = (bf16[360448]{0:T(1024)(128)(2,1)}, bf16[360448]{0:T(1024)(128)(2,1)}, u32[]{:S(2)}, u32[]{:S(2)}) collective-permute-start(bf16[360448]{0:T(1024)(128)(2,1)} %constant_dynamic-update-slice_fusion), channel_id=1, source_target_pairs={{16,0},{32,16},{48,32},{64,48},{80,64},{96,80},{112,96},{128,112},... | collective-permute-start | bytes 2162696 | tf_op jit(solution)/shard_map/ppermute | solution.py:82
  99.4 15.7 %all-to-all-start.3 = ((bf16[16,2,7168]{2,1,0:T(2,128)(2,1)}), bf16[16,2,7168]{2,1,0:T(2,128)(2,1)S(1)}, u32[]{:S(2)}, u32[]{:S(2)}) async-start(bf16[16,2,7168]{2,1,0:T(2,128)(2,1)} %reshape.117), calls=%async_computation.3 | async-start | bytes 917504 | tf_op jit(solution)/shard_map/all_to_all | solution.py:135
  109.0 10.0 %copy-start.6 = (bf16[8,224]{1,0:T(8,128)(2,1)S(1)}, bf16[8,224]{1,0:T(8,128)(2,1)}, u32[]{:S(2)}) copy-start(bf16[8,224]{1,0:T(8,128)(2,1)} %param.7) | copy-start | bytes 10756
  109.0 10.1 %copy-start.2 = (bf16[32,16,1024]{2,1,0:T(8,128)(2,1)S(1)}, bf16[32,16,1024]{2,1,0:T(8,128)(2,1)}, u32[]{:S(2)}) copy-start(bf16[32,16,1024]{2,1,0:T(8,128)(2,1)} %param.5) | copy-start | bytes 3145732
  109.0 10.1 %copy-start.5 = (bf16[8,16,1024]{2,1,0:T(8,128)(2,1)S(1)}, bf16[8,16,1024]{2,1,0:T(8,128)(2,1)}, u32[]{:S(2)}) copy-start(bf16[8,16,1024]{2,1,0:T(8,128)(2,1)} %param.9) | copy-start | bytes 786436
  115.1 14.4 %all-to-all-start.2 = ((f32[16,1,8192]{2,1,0:T(1,128)}), f32[16,1,8192]{2,1,0:T(1,128)S(1)}, u32[]{:S(2)}, u32[]{:S(2)}) async-start(f32[16,1,8192]{2,1,0:T(1,128)} %reshape.115), calls=%async_computation.2 | async-start | bytes 1048576 | tf_op jit(solution)/shard_map/all_to_all | solution.py:141
  133.9 4.5 %copy-start.1 = (f32[32,16,1024]{2,0,1:T(8,128)S(1)}, f32[32,16,1024]{2,0,1:T(8,128)}, u32[]{:S(2)}) copy-start(f32[32,16,1024]{2,0,1:T(8,128)} %fusion.152) | copy-start | bytes 6291460
  133.9 4.5 %copy-start.3 = (bf16[32,16,1024]{2,1,0:T(8,128)(2,1)S(1)}, bf16[32,16,1024]{2,1,0:T(8,128)(2,1)}, u32[]{:S(2)}) copy-start(bf16[32,16,1024]{2,1,0:T(8,128)(2,1)} %param.5) | copy-start | bytes 3145732

commit v5 on v4

--- a/solution.py
+++ b/solution.py
@@ -46,22 +46,13 @@
     )
 
 
-def column_matrix(fine_count, coarse_count):
-    fine_cols = jnp.arange(fine_count)[:, None]
-    coarse = jnp.arange(coarse_count)[None, :]
-    return kernel_values(fine_cols - DECIM * coarse)
-
-
-def row_matrix(rows_local):
-    coarse = jnp.arange(rows_local // DECIM)[:, None]
-    padded = jnp.arange(rows_local + 2 * HALO)[None, :]
-    return kernel_values(padded - HALO - DECIM * coarse)
-
-
-def back_matrix(rows_local):
-    fine_rows = jnp.arange(rows_local)[:, None]
-    coarse = jnp.arange(rows_local // DECIM + 2 * (HALO // DECIM))[None, :]
-    return kernel_values(fine_rows - DECIM * coarse + HALO)
+def banded(count, width, stride, shift):
+    period = width + stride * count
+    at = jnp.arange(period)
+    offsets = jnp.where(at < width, at, at - period) + shift
+    period_values = kernel_values(offsets)
+    rows = jnp.tile(period_values, count)[: count * (period - stride)]
+    return rows.reshape(count, period - stride)[:, :width]
 
 
 def split_dot(spec, wide, narrow):
@@ -72,22 +63,6 @@
     return jnp.einsum(spec, high, narrow, preferred_element_type=f32) + jnp.einsum(
         spec, low, narrow, preferred_element_type=f32
     )
-
-
-def neighbours(parts, axis):
-    count = lax.axis_size(axis)
-    ends = count - 1
-    flat = jnp.concatenate([p.reshape(-1) for p in parts])
-    from_prev = lax.ppermute(flat, axis, [(i, i + 1) for i in range(ends)])
-    from_next = lax.ppermute(flat, axis, [(i + 1, i) for i in range(ends)])
-    out = []
-    for got in (from_prev, from_next):
-        pieces, at = [], 0
-        for p in parts:
-            pieces.append(got[at : at + p.size].reshape(p.shape))
-            at += p.size
-        out.append(pieces)
-    return out
 
 
 def shards(latent, basis, response, hyper_obs, multi_obs):
@@ -102,31 +77,39 @@
     rim = HALO // DECIM
     subspace, rows_here, width_cols = latent.shape
     chunk = coarse_cols // n_spec
+    wide_rows = coarse_rows + 2 * rim
     basis_wide = basis.astype(f32)
-    column_kernel = column_matrix(width_cols, coarse_cols)
+    column_t = banded(coarse_cols, width_cols, DECIM, 0)
+    own_rows = banded(wide_rows, rows_dev, DECIM, HALO)
 
     cols_done = jnp.einsum(
-        "qrc,csj->sqjr",
+        "qrc,sjc->sqjr",
         latent,
-        column_kernel.reshape(width_cols, n_spec, chunk),
+        column_t.reshape(n_spec, chunk, width_cols),
         preferred_element_type=f32,
     ).astype(bf16)
     tile_rows = lax.all_to_all(cols_done, "spec", split_axis=0, concat_axis=3, tiled=True)[0]
 
-    obs_split = hyper_obs.reshape(group, coarse_rows, n_spec, chunk).transpose(2, 0, 3, 1)
-    obs_cols = lax.all_to_all(obs_split, "spec", split_axis=0, concat_axis=1, tiled=True)[0]
+    obs_wide_bands = with_halo(hyper_obs, (("tile", 1),), rim)
+    obs_split = obs_wide_bands.reshape(group, wide_rows, n_spec, chunk).transpose(2, 0, 3, 1)
+    obs_wide = lax.all_to_all(obs_split, "spec", split_axis=0, concat_axis=1, tiled=True)[0]
 
-    obs_head = lax.slice_in_dim(obs_cols, 0, rim, axis=2)
-    obs_tail = lax.slice_in_dim(obs_cols, coarse_rows - rim, coarse_rows, axis=2)
-    (prev_rows, prev_tail, _), (next_rows, _, next_head) = neighbours(
-        (tile_rows, obs_tail, obs_head), "tile"
+    own_part = jnp.einsum("qjr,er->qje", tile_rows, own_rows, preferred_element_type=f32)
+    half = wide_rows // 2
+    ends = n_tile - 1
+    from_prev = lax.ppermute(
+        lax.slice_in_dim(own_part, half, wide_rows, axis=2),
+        "tile",
+        [(i, i + 1) for i in range(ends)],
     )
-    padded = jnp.concatenate([prev_rows, tile_rows, next_rows], axis=2)
-    obs_wide = jnp.concatenate([prev_tail, obs_cols, next_head], axis=2)
-    row_kernel = row_matrix(rows_dev + 2 * (rows_dev - HALO))
-    coef_blurred = jnp.einsum("qjr,ir->qji", padded, row_kernel, preferred_element_type=f32)
+    from_next = lax.ppermute(
+        lax.slice_in_dim(own_part, 0, half, axis=2),
+        "tile",
+        [(i + 1, i) for i in range(ends)],
+    )
+    coef_blurred = own_part + jnp.concatenate([from_prev, from_next], axis=2)
     blurred = split_dot("qji,bq->bji", coef_blurred, basis)
-    coarse_at = jnp.arange(coarse_rows + 2 * rim) + tile_index * coarse_rows - rim
+    coarse_at = jnp.arange(wide_rows) + tile_index * coarse_rows - rim
     inside = (coarse_at >= 0) & (coarse_at < n_tile * coarse_rows)
     resid_wide = jnp.where(inside, blurred - obs_wide.astype(f32), 0.0).astype(bf16)
 
@@ -136,10 +119,12 @@
     hs_residual = resid_bands.transpose(0, 2, 1)
 
     coef_resid = jnp.einsum("bq,bji->qji", basis, resid_wide, preferred_element_type=f32)
-    rows_back = split_dot("qjk,rk->qjr", coef_resid, back_matrix(rows_dev))
+    rows_back = split_dot("qjk,kr->qjr", coef_resid, own_rows)
     back_split = rows_back.reshape(subspace, chunk, n_spec, rows_here).transpose(2, 0, 3, 1)
     rows_pixel = lax.all_to_all(back_split, "spec", split_axis=0, concat_axis=3, tiled=True)[0]
-    grad_hs = split_dot("qrj,cj->qrc", rows_pixel, column_kernel)
+    grad_hs = jnp.einsum(
+        "qrj,jc->qrc", rows_pixel, column_t.astype(f32), precision=highest
+    )
 
     resp_basis = jnp.dot(response.astype(f32), basis_wide, precision=highest)
     multi_pred = jnp.einsum("mq,qrc->mrc", resp_basis, latent.astype(f32), precision=highest)

time: 146 us -> 117 us (0.80)
  matrix products: 29.1 us -> 12.8 us
  local copies, waits for them, and re-layouts: 38.8 us -> 22.9 us
  waiting for transfers between devices: 43.9 us -> 34.4 us
  starting transfers between devices: 28.9 us -> 38.2 us
  other arithmetic: 2.56 us -> 5.76 us
    ppermute x2 -> x4, starting transfers between devices: 9.58 us -> 18.5 us  [the longest x1 5.72 us: shards(): lax.ppermute(lax.slice_in_dim(own_part, half, wide_rows, axis=2), 'tile',...]
    dot_general x3 -> x2, matrix products: 8.44 us -> 1.24 us  [split_dot(): jnp.einsum(spec, low, narrow, preferred_element_type=f32)]
    slice x7 -> x4, local copies, waits for them, and re-layouts: 6.77 us -> 0.27 us  [the longest x1 0.13 us: shards(): lax.slice_in_dim(own_part, half, wide_rows, axis=2)]
    all_to_all x1, waiting for transfers between devices: 6.16 us -> 0.01 us  [shards(): lax.all_to_all(cols_done, 'spec', split_axis=0, concat_axis=3, tiled=True)]
    all_to_all x2 -> x0, local copies, waits for them, and re-layouts: 5.95 us -> none  [shards(): lax.all_to_all(cols_done, 'spec', split_axis=0, concat_axis=3, tiled=True)]
    dot_general x3 -> x2, matrix products: 5.64 us -> 0.64 us  [split_dot(): jnp.einsum(spec, high, narrow, preferred_element_type=f32)]
    dot_general x2 -> x3, matrix products: 10.7 us -> 6.58 us  [the longest x1 4.96 us: shards(): jnp.einsum('qrj,jc->qrc', rows_pixel, column_t.astype(f32), precision=hig...]
    ppermute x2 -> x4, waiting for transfers between devices: 28.4 us -> 25.5 us  [the longest x1 14.5 us: shards(): lax.ppermute(lax.slice_in_dim(own_part, half, wide_rows, axis=2), 'tile',...]
  transfers between devices with their start and end apart: 6 -> 8, of which waited for: 6 -> 5; matrix products, arithmetic and copies ran while one was open for 18% -> 16% of each run, Pallas kernels for 0% -> 0%
where the time goes in v5:
time: 117 us; the launch traced here: 116 us
  starting transfers between devices  38.2 us (33%)
  waiting for transfers between devices  34.4 us (29%)
  local copies, waits for them, and re-layouts  22.9 us (20%)
  matrix products  12.8 us (11%)
  other arithmetic  5.76 us (5%)
  between operations  1.71 us (1%)
    ppermute x1, waiting for transfers between devices, shards(): lax.ppermute(lax.slice_in_dim(own_part, half, wide_rows, axis=2), 'tile',...  14.5 us
    unnamed x28, local copies, waits for them, and re-layouts  11.7 us
    ppermute x1, waiting for transfers between devices, with_halo(): lax.ppermute(tail, axis, [(i, (i + 1) % count) for i in range(ends)])  5.95 us
    all_to_all x1, starting transfers between devices, shards(): lax.all_to_all(cols_done, 'spec', split_axis=0, concat_axis=3, tiled=True)  5.76 us
    ppermute x1, starting transfers between devices, shards(): lax.ppermute(lax.slice_in_dim(own_part, half, wide_rows, axis=2), 'tile',...  5.72 us
    all_to_all x1, starting transfers between devices, shards(): lax.all_to_all(resid_split, 'spec', split_axis=0, concat_axis=2, tiled=True)  5.48 us
    ppermute x1, starting transfers between devices, with_halo(): lax.ppermute(tail, axis, [(i, (i + 1) % count) for i in range(ends)])  5.18 us
    ppermute x1, waiting for transfers between devices, with_halo(): lax.ppermute(head, axis, [((i + 1) % count, i) for i in range(ends)])  5.01 us
  transfers between devices with their start and end apart: 8, of which 5 were waited for; matrix products, arithmetic and copies ran while one was open for 16% of the time, Pallas kernels for 0%

profile of v5, /device:TPU:24, one launch (start us, length us, event | category | flops | bytes accessed | tf_op | source)
XLA Modules:
  0.0 115.7 jit_solution(6756125784169917975)
XLA Ops:
  2.6 1.7 %reshape.88 = bf16[256,2044]{1,0:T(8,128)(2,1)S(1)} reshape(bf16[523264]{0:T(1024)(128)(2,1)S(1)} %slice.36) | data formatting | bytes 2093056 | tf_op jit(solution)/shard_map/reshape | solution.py:55
  4.3 1.4 %fusion.44 = bf16[16,16,16,32]{3,2,1,0:T(8,128)(2,1)S(1)} fusion(bf16[16,16,1024,1]{2,1,3,0:T(8,128)(2,1)S(1)} %bitcast.97, bf16[32,16,1024]{2,1,0:T(8,128)(2,1)S(1)} %copy-done.1), kind=kOutput, calls=%fused_computation.72 | convolution fusion | flops 268566528 | bytes 1835008 | tf_op jit(solution)/shard_map/qrc,sjc->sqjr/dot_general | solution.py:85
  5.8 1.7 %reshape.101 = bf16[16,2,4096]{2,1,0:T(2,128)(2,1)} reshape(bf16[16,16,16,32]{3,2,1,0:T(8,128)(2,1)S(1)} %fusion.44) | data formatting | bytes 524288
  7.5 5.8 %all-to-all-start = ((bf16[16,2,4096]{2,1,0:T(2,128)(2,1)}), bf16[16,2,4096]{2,1,0:T(2,128)(2,1)S(1)}, u32[]{:S(2)}, u32[]{:S(2)}) async-start(bf16[16,2,4096]{2,1,0:T(2,128)(2,1)} %reshape.101), calls=%async_computation | async-start | bytes 524288 | tf_op jit(solution)/shard_map/all_to_all | solution.py:91
  13.3 5.2 %collective-permute-start.2 = (bf16[14,32,256]{2,1,0:T(8,128)(2,1)S(1)}, bf16[14,32,256]{2,1,0:T(8,128)(2,1)S(1)}, u32[]{:S(2)}, u32[]{:S(2)}) collective-permute-start(bf16[14,32,256]{2,1,0:T(8,128)(2,1)S(1)} %get-tuple-element.8), channel_id=1, source_target_pairs={{0,16},{16,32},{32,48},{48,64},{64,80},{80,96},{96,112},{112,128},... | collective-permute-start | bytes 688136 | tf_op jit(solution)/shard_map/ppermute | solution.py:21
  18.5 4.2 %collective-permute-start.3 = (bf16[14,32,256]{2,1,0:T(8,128)(2,1)S(1)}, bf16[14,32,256]{2,1,0:T(8,128)(2,1)S(1)}, u32[]{:S(2)}, u32[]{:S(2)}) collective-permute-start(bf16[14,32,256]{2,1,0:T(8,128)(2,1)S(1)} %get-tuple-element.9), channel_id=1, source_target_pairs={{16,0},{32,16},{48,32},{64,48},{80,64},{96,80},{112,96},{128,112},... | collective-permute-start | bytes 688136 | tf_op jit(solution)/shard_map/ppermute | solution.py:23
  23.1 5.9 %collective-permute-done.2 = bf16[14,32,256]{2,1,0:T(8,128)(2,1)S(1)} collective-permute-done((bf16[14,32,256]{2,1,0:T(8,128)(2,1)S(1)}, bf16[14,32,256]{2,1,0:T(8,128)(2,1)S(1)}, u32[]{:S(2)}, u32[]{:S(2)}) %collective-permute-start.2) | collective-permute-done | bytes 229408 | tf_op jit(solution)/shard_map/ppermute | solution.py:21
  29.5 5.0 %collective-permute-done.3 = bf16[14,32,256]{2,1,0:T(8,128)(2,1)S(1)} collective-permute-done((bf16[14,32,256]{2,1,0:T(8,128)(2,1)S(1)}, bf16[14,32,256]{2,1,0:T(8,128)(2,1)S(1)}, u32[]{:S(2)}, u32[]{:S(2)}) %collective-permute-start.3) | collective-permute-done | bytes 229408 | tf_op jit(solution)/shard_map/ppermute | solution.py:23
  36.9 4.9 %all-to-all-start.1 = ((bf16[16,14,16,128]{3,2,1,0:T(8,128)(2,1)}), bf16[16,14,16,128]{3,2,1,0:T(8,128)(2,1)}, u32[]{:S(2)}, u32[]{:S(2)}) async-start(bf16[16,14,16,128]{3,2,1,0:T(8,128)(2,1)} %copy.44), calls=%async_computation.1 | async-start | bytes 1835008 | tf_op jit(solution)/shard_map/all_to_all | solution.py:95
  44.5 5.7 %collective-permute-start = (f32[32,16,64]{2,1,0:T(8,128)S(1)}, f32[32,16,64]{2,1,0:T(8,128)S(1)}, u32[]{:S(2)}, u32[]{:S(2)}) collective-permute-start(f32[32,16,64]{2,1,0:T(8,128)S(1)} %get-tuple-element.12), channel_id=1, source_target_pairs={{0,16},{16,32},{32,48},{48,64},{64,80},{80,96},{96,112},{112,128},... | collective-permute-start | bytes 393224 | tf_op jit(solution)/shard_map/ppermute | solution.py:100
  50.2 3.3 %collective-permute-start.1 = (f32[32,16,64]{2,1,0:T(8,128)S(1)}, f32[32,16,64]{2,1,0:T(8,128)S(1)}, u32[]{:S(2)}, u32[]{:S(2)}) collective-permute-start(f32[32,16,64]{2,1,0:T(8,128)S(1)} %get-tuple-element.13), channel_id=1, source_target_pairs={{16,0},{32,16},{48,32},{64,48},{80,64},{96,80},{112,96},{128,112},... | collective-permute-start | bytes 393224 | tf_op jit(solution)/shard_map/ppermute | solution.py:105
  53.6 14.5 %collective-permute-done = f32[32,16,64]{2,1,0:T(8,128)S(1)} collective-permute-done((f32[32,16,64]{2,1,0:T(8,128)S(1)}, f32[32,16,64]{2,1,0:T(8,128)S(1)}, u32[]{:S(2)}, u32[]{:S(2)}) %collective-permute-start) | collective-permute-done | bytes 131104 | tf_op jit(solution)/shard_map/ppermute | solution.py:100
  73.0 5.5 %all-to-all-start.3 = ((bf16[16,2,7168]{2,1,0:T(2,128)(2,1)}), bf16[16,2,7168]{2,1,0:T(2,128)(2,1)S(1)}, u32[]{:S(2)}, u32[]{:S(2)}) async-start(bf16[16,2,7168]{2,1,0:T(2,128)(2,1)} %reshape.105), calls=%async_computation.3 | async-start | bytes 917504 | tf_op jit(solution)/shard_map/all_to_all | solution.py:118
  79.9 1.6 %copy.88 = f32[16,32,16,16]{1,2,3,0:T(8,128)} copy(f32[16,32,16,16]{1,2,0,3:T(8,128)S(1)} %bitcast.88) | data formatting | bytes 1048576 | tf_op jit(solution)/shard_map/transpose | solution.py:123
  81.4 3.2 %reshape.103 = f32[16,1,8192]{2,1,0:T(1,128)} reshape(f32[16,16,16,32]{3,2,1,0:T(8,128)} %bitcast.89) | data formatting | bytes 1048576
  84.7 4.0 %all-to-all-done.3 = bf16[16,2,7168]{2,1,0:T(2,128)(2,1)S(1)} async-done(((bf16[16,2,7168]{2,1,0:T(2,128)(2,1)}), bf16[16,2,7168]{2,1,0:T(2,128)(2,1)S(1)}, u32[]{:S(2)}, u32[]{:S(2)}) %all-to-all-start.3) | async-done | bytes 458784 | tf_op jit(solution)/shard_map/all_to_all | solution.py:118
  89.4 3.6 %all-to-all-start.2 = ((f32[16,1,8192]{2,1,0:T(1,128)}), f32[16,1,8192]{2,1,0:T(1,128)S(1)}, u32[]{:S(2)}, u32[]{:S(2)}) async-start(f32[16,1,8192]{2,1,0:T(1,128)} %reshape.103), calls=%async_computation.2 | async-start | bytes 1048576 | tf_op jit(solution)/shard_map/all_to_all | solution.py:124
  93.1 1.6 %fusion.6 = bf16[8,16,1024]{2,0,1:T(8,128)(2,1)S(1)} fusion(f32[8,32,1]{1,0,2:T(8,128)S(1)} %convolution_bitcast_fusion.1, bf16[32,16,1024]{2,1,0:T(8,128)(2,1)S(1)} %copy-done.2, bf16[8,16,1024]{2,1,0:T(8,128)(2,1)S(1)} %copy-done.7), kind=kOutput, calls=%fused_computation.11 | convolution fusion | flops 50724864 | bytes 1573888 | tf_op jit(solution)/shard_map/mq,qrc->mrc/dot_general | solution.py:130
  94.7 2.4 %fusion.47 = f32[32,16,1024]{2,0,1:T(8,128)} fusion(f32[8,32,1]{1,0,2:T(8,128)S(1)} %convolution_bitcast_fusion.1, bf16[8,16,1024]{2,0,1:T(8,128)(2,1)S(1)} %fusion.6), kind=kOutput, calls=%fused_computation.73 | convolution fusion | flops 50331648 | bytes 2360320 | tf_op jit(solution)/shard_map/mq,mrc->qrc/dot_general | solution.py:132
  98.9 4.9 %all-to-all-done.2 = f32[16,1,8192]{2,1,0:T(1,128)S(1)} async-done(((f32[16,1,8192]{2,1,0:T(1,128)}), f32[16,1,8192]{2,1,0:T(1,128)S(1)}, u32[]{:S(2)}, u32[]{:S(2)}) %all-to-all-start.2) | async-done | bytes 524320 | tf_op jit(solution)/shard_map/all_to_all | solution.py:124
  104.3 2.7 %reduce = f32[16,8192]{1,0:T(8,128)} reduce(f32[16,1,8192]{2,1,0:T(1,128)S(1)} %all-to-all-done.2, f32[]{:T(128)} %broadcast.127), dimensions={1}, to_apply=%all_to_all.44.reduce_sub_computation | reduce | bytes 1048580 | tf_op jit(solution)/shard_map/all_to_all | solution.py:124
  107.0 1.7 %reshape.104 = f32[16,16,16,32]{3,2,1,0:T(8,128)S(1)} reshape(f32[16,8192]{1,0:T(8,128)} %reduce) | data formatting | bytes 1048576
  108.8 2.0 %copy.51 = f32[32,16,256]{2,1,0:T(8,128)} copy(f32[32,16,256]{0,1,2:T(8,128)S(1)} %bitcast.87) | data formatting | bytes 1048576 | tf_op jit(solution)/shard_map/squeeze | solution.py:124
  110.7 5.0 %fusion.2 = bf16[32,16,1024]{2,1,0:T(8,128)(2,1)} fusion(f32[32,16,1024]{2,0,1:T(8,128)} %fusion.47, bf16[32,16,1024]{2,1,0:T(8,128)(2,1)S(1)} %copy-done.2, f32[32,16,256]{2,1,0:T(8,128)} %copy.51, bf16[256,2044]{1,0:T(8,128)(2,1)} %copy-done.3), kind=kOutput, calls=%fused_computation.3 | convolution fusion | flops 1613234176 | bytes 5242880 | tf_op jit(solution)/shard_map/qrj,jc->qrc/dot_general | solution.py:125
  (58 shorter events, 16.7 us)
Async XLA Ops:
  0.6 67.6 %copy-start = (bf16[224,32]{0,1:T(8,128)(2,1)S(1)}, bf16[224,32]{0,1:T(8,128)(2,1)}, u32[]{:S(2)}) copy-start(bf16[224,32]{0,1:T(8,128)(2,1)} %param.6) | copy-start | bytes 43012
  2.6 1.7 %copy-start.1 = (bf16[32,16,1024]{2,1,0:T(8,128)(2,1)S(1)}, bf16[32,16,1024]{2,1,0:T(8,128)(2,1)}, u32[]{:S(2)}) copy-start(bf16[32,16,1024]{2,1,0:T(8,128)(2,1)} %param.5) | copy-start | bytes 3145732
  4.3 1.5 %copy-start.3 = (bf16[256,2044]{1,0:T(8,128)(2,1)}, bf16[256,2044]{1,0:T(8,128)(2,1)S(1)}, u32[]{:S(2)}) copy-start(bf16[256,2044]{1,0:T(8,128)(2,1)S(1)} %reshape.88) | copy-start | bytes 3139588
  5.8 7.5 %copy-start.4 = (bf16[14,64,256]{2,1,0:T(8,128)(2,1)S(1)}, bf16[14,64,256]{2,1,0:T(8,128)(2,1)}, u32[]{:S(2)}) copy-start(bf16[14,64,256]{2,1,0:T(8,128)(2,1)} %param.8) | copy-start | bytes 1376260
  7.5 29.4 %all-to-all-start = ((bf16[16,2,4096]{2,1,0:T(2,128)(2,1)}), bf16[16,2,4096]{2,1,0:T(2,128)(2,1)S(1)}, u32[]{:S(2)}, u32[]{:S(2)}) async-start(bf16[16,2,4096]{2,1,0:T(2,128)(2,1)} %reshape.101), calls=%async_computation | async-start | bytes 524288 | tf_op jit(solution)/shard_map/all_to_all | solution.py:91
  13.3 15.8 %collective-permute-start.2 = (bf16[14,32,256]{2,1,0:T(8,128)(2,1)S(1)}, bf16[14,32,256]{2,1,0:T(8,128)(2,1)S(1)}, u32[]{:S(2)}, u32[]{:S(2)}) collective-permute-start(bf16[14,32,256]{2,1,0:T(8,128)(2,1)S(1)} %get-tuple-element.8), channel_id=1, source_target_pairs={{0,16},{16,32},{32,48},{48,64},{64,80},{80,96},{96,112},{112,128},... | collective-permute-start | bytes 688136 | tf_op jit(solution)/shard_map/ppermute | solution.py:21
  18.5 16.1 %collective-permute-start.3 = (bf16[14,32,256]{2,1,0:T(8,128)(2,1)S(1)}, bf16[14,32,256]{2,1,0:T(8,128)(2,1)S(1)}, u32[]{:S(2)}, u32[]{:S(2)}) collective-permute-start(bf16[14,32,256]{2,1,0:T(8,128)(2,1)S(1)} %get-tuple-element.9), channel_id=1, source_target_pairs={{16,0},{32,16},{48,32},{64,48},{80,64},{96,80},{112,96},{128,112},... | collective-permute-start | bytes 688136 | tf_op jit(solution)/shard_map/ppermute | solution.py:23
  36.9 31.8 %all-to-all-start.1 = ((bf16[16,14,16,128]{3,2,1,0:T(8,128)(2,1)}), bf16[16,14,16,128]{3,2,1,0:T(8,128)(2,1)}, u32[]{:S(2)}, u32[]{:S(2)}) async-start(bf16[16,14,16,128]{3,2,1,0:T(8,128)(2,1)} %copy.44), calls=%async_computation.1 | async-start | bytes 1835008 | tf_op jit(solution)/shard_map/all_to_all | solution.py:95
  44.5 23.6 %collective-permute-start = (f32[32,16,64]{2,1,0:T(8,128)S(1)}, f32[32,16,64]{2,1,0:T(8,128)S(1)}, u32[]{:S(2)}, u32[]{:S(2)}) collective-permute-start(f32[32,16,64]{2,1,0:T(8,128)S(1)} %get-tuple-element.12), channel_id=1, source_target_pairs={{0,16},{16,32},{32,48},{48,64},{64,80},{80,96},{96,112},{112,128},... | collective-permute-start | bytes 393224 | tf_op jit(solution)/shard_map/ppermute | solution.py:100
  50.2 17.9 %collective-permute-start.1 = (f32[32,16,64]{2,1,0:T(8,128)S(1)}, f32[32,16,64]{2,1,0:T(8,128)S(1)}, u32[]{:S(2)}, u32[]{:S(2)}) collective-permute-start(f32[32,16,64]{2,1,0:T(8,128)S(1)} %get-tuple-element.13), channel_id=1, source_target_pairs={{16,0},{32,16},{48,32},{64,48},{80,64},{96,80},{112,96},{128,112},... | collective-permute-start | bytes 393224 | tf_op jit(solution)/shard_map/ppermute | solution.py:105
  73.0 15.6 %all-to-all-start.3 = ((bf16[16,2,7168]{2,1,0:T(2,128)(2,1)}), bf16[16,2,7168]{2,1,0:T(2,128)(2,1)S(1)}, u32[]{:S(2)}, u32[]{:S(2)}) async-start(bf16[16,2,7168]{2,1,0:T(2,128)(2,1)} %reshape.105), calls=%async_computation.3 | async-start | bytes 917504 | tf_op jit(solution)/shard_map/all_to_all | solution.py:118
  81.4 11.6 %copy-start.8 = (bf16[8,224]{1,0:T(8,128)(2,1)S(1)}, bf16[8,224]{1,0:T(8,128)(2,1)}, u32[]{:S(2)}) copy-start(bf16[8,224]{1,0:T(8,128)(2,1)} %param.7) | copy-start | bytes 10756
  81.4 11.7 %copy-start.2 = (bf16[32,16,1024]{2,1,0:T(8,128)(2,1)S(1)}, bf16[32,16,1024]{2,1,0:T(8,128)(2,1)}, u32[]{:S(2)}) copy-start(bf16[32,16,1024]{2,1,0:T(8,128)(2,1)} %param.5) | copy-start | bytes 3145732
  81.4 11.7 %copy-start.7 = (bf16[8,16,1024]{2,1,0:T(8,128)(2,1)S(1)}, bf16[8,16,1024]{2,1,0:T(8,128)(2,1)}, u32[]{:S(2)}) copy-start(bf16[8,16,1024]{2,1,0:T(8,128)(2,1)} %param.9) | copy-start | bytes 786436
  88.6 0.8 copy-start.5
  89.4 14.4 %all-to-all-start.2 = ((f32[16,1,8192]{2,1,0:T(1,128)}), f32[16,1,8192]{2,1,0:T(1,128)S(1)}, u32[]{:S(2)}, u32[]{:S(2)}) async-start(f32[16,1,8192]{2,1,0:T(1,128)} %reshape.103), calls=%async_computation.2 | async-start | bytes 1048576 | tf_op jit(solution)/shard_map/all_to_all | solution.py:124
  93.1 3.9 %copy-start.6 = (bf16[16,2,7168]{2,1,0:T(2,128)(2,1)S(1)}, bf16[16,2,7168]{2,1,0:T(2,128)(2,1)}, u32[]{:S(2)}) copy-start(bf16[16,2,7168]{2,1,0:T(2,128)(2,1)} %copy-done.5) | copy-start | bytes 1376260

commit v6 on v5

--- a/solution.py
+++ b/solution.py
@@ -65,6 +65,23 @@
     )
 
 
+def halves(wide):
+    high_wide = lax.reduce_precision(wide, exponent_bits=8, mantissa_bits=7)
+    return high_wide.astype(jnp.bfloat16), (wide - high_wide).astype(jnp.bfloat16)
+
+
+def packed_swap(parts, axis):
+    count = parts[0].shape[0]
+    flat = jnp.concatenate([p.reshape(count, -1) for p in parts], axis=1)
+    got = lax.all_to_all(flat, axis, split_axis=0, concat_axis=0, tiled=True)
+    out, at = [], 0
+    for p in parts:
+        size = p.size // count
+        out.append(got[:, at : at + size].reshape(p.shape))
+        at += size
+    return out
+
+
 def shards(latent, basis, response, hyper_obs, multi_obs):
     highest = lax.Precision.HIGHEST
     f32 = jnp.float32
@@ -78,6 +95,7 @@
     subspace, rows_here, width_cols = latent.shape
     chunk = coarse_cols // n_spec
     wide_rows = coarse_rows + 2 * rim
+    half = wide_rows // 2
     basis_wide = basis.astype(f32)
     column_t = banded(coarse_cols, width_cols, DECIM, 0)
     own_rows = banded(wide_rows, rows_dev, DECIM, HALO)
@@ -88,43 +106,48 @@
         column_t.reshape(n_spec, chunk, width_cols),
         preferred_element_type=f32,
     ).astype(bf16)
-    tile_rows = lax.all_to_all(cols_done, "spec", split_axis=0, concat_axis=3, tiled=True)[0]
-
-    obs_wide_bands = with_halo(hyper_obs, (("tile", 1),), rim)
-    obs_split = obs_wide_bands.reshape(group, wide_rows, n_spec, chunk).transpose(2, 0, 3, 1)
-    obs_wide = lax.all_to_all(obs_split, "spec", split_axis=0, concat_axis=1, tiled=True)[0]
+    obs_split = hyper_obs.reshape(group, coarse_rows, n_spec, chunk).transpose(2, 0, 3, 1)
+    rows_got, obs_got = packed_swap((cols_done, obs_split), "spec")
+    tile_rows = rows_got.transpose(1, 2, 0, 3).reshape(subspace, chunk, rows_dev)
+    obs_cols = obs_got.reshape(group * n_spec, chunk, coarse_rows)
 
     own_part = jnp.einsum("qjr,er->qje", tile_rows, own_rows, preferred_element_type=f32)
-    half = wide_rows // 2
     ends = n_tile - 1
-    from_prev = lax.ppermute(
+
+    def payload(part, obs_rim):
+        high, low = halves(part)
+        return jnp.concatenate([high.reshape(-1), low.reshape(-1), obs_rim.reshape(-1)])
+
+    def unpack(got):
+        size = subspace * chunk * half
+        part = got[:size].astype(f32) + got[size : 2 * size].astype(f32)
+        return part.reshape(subspace, chunk, half), got[2 * size :].reshape(-1, chunk, rim)
+
+    to_next = payload(
         lax.slice_in_dim(own_part, half, wide_rows, axis=2),
-        "tile",
-        [(i, i + 1) for i in range(ends)],
+        lax.slice_in_dim(obs_cols, coarse_rows - rim, coarse_rows, axis=2),
     )
-    from_next = lax.ppermute(
-        lax.slice_in_dim(own_part, 0, half, axis=2),
-        "tile",
-        [(i + 1, i) for i in range(ends)],
+    to_prev = payload(
+        lax.slice_in_dim(own_part, 0, half, axis=2), lax.slice_in_dim(obs_cols, 0, rim, axis=2)
     )
-    coef_blurred = own_part + jnp.concatenate([from_prev, from_next], axis=2)
+    part_prev, rim_prev = unpack(lax.ppermute(to_next, "tile", [(i, i + 1) for i in range(ends)]))
+    part_next, rim_next = unpack(lax.ppermute(to_prev, "tile", [(i + 1, i) for i in range(ends)]))
+    coef_blurred = own_part + jnp.concatenate([part_prev, part_next], axis=2)
+    obs_wide = jnp.concatenate([rim_prev, obs_cols, rim_next], axis=2)
     blurred = split_dot("qji,bq->bji", coef_blurred, basis)
     coarse_at = jnp.arange(wide_rows) + tile_index * coarse_rows - rim
     inside = (coarse_at >= 0) & (coarse_at < n_tile * coarse_rows)
     resid_wide = jnp.where(inside, blurred - obs_wide.astype(f32), 0.0).astype(bf16)
 
+    coef_resid = jnp.einsum("bq,bji->qji", basis, resid_wide, preferred_element_type=f32)
+    rows_back = split_dot("qjk,kr->qjr", coef_resid, own_rows).astype(bf16)
+    back_split = rows_back.reshape(subspace, chunk, n_spec, rows_here).transpose(2, 0, 1, 3)
     resid_cols = lax.slice_in_dim(resid_wide, rim, rim + coarse_rows, axis=2)
     resid_split = resid_cols.reshape(n_spec, group, chunk, coarse_rows)
-    resid_bands = lax.all_to_all(resid_split, "spec", split_axis=0, concat_axis=2, tiled=True)[0]
-    hs_residual = resid_bands.transpose(0, 2, 1)
-
-    coef_resid = jnp.einsum("bq,bji->qji", basis, resid_wide, preferred_element_type=f32)
-    rows_back = split_dot("qjk,kr->qjr", coef_resid, own_rows)
-    back_split = rows_back.reshape(subspace, chunk, n_spec, rows_here).transpose(2, 0, 3, 1)
-    rows_pixel = lax.all_to_all(back_split, "spec", split_axis=0, concat_axis=3, tiled=True)[0]
-    grad_hs = jnp.einsum(
-        "qrj,jc->qrc", rows_pixel, column_t.astype(f32), precision=highest
-    )
+    back_got, resid_got = packed_swap((back_split, resid_split), "spec")
+    rows_pixel = back_got.transpose(1, 3, 0, 2).reshape(subspace, rows_here, coarse_cols)
+    hs_residual = resid_got.transpose(1, 3, 0, 2).reshape(group, coarse_rows, coarse_cols)
+    grad_hs = jnp.einsum("qrj,jc->qrc", rows_pixel, column_t, preferred_element_type=f32)
 
     resp_basis = jnp.dot(response.astype(f32), basis_wide, precision=highest)
     multi_pred = jnp.einsum("mq,qrc->mrc", resp_basis, latent.astype(f32), precision=highest)

time: 117 us -> 128 us (1.094)
  local copies, waits for them, and re-layouts: 22.9 us -> 51.6 us
  starting transfers between devices: 38.2 us -> 19.3 us
  waiting for transfers between devices: 34.4 us -> 36.9 us
    reshape x0 -> x17, local copies, waits for them, and re-layouts: none -> 19.6 us  [the longest x3 7.91 us: packed_swap(): flat = jnp.concatenate([p.reshape(count, -1) for p in parts], axis=1)]
    all_to_all x4 -> x2, waiting for transfers between devices: 8.92 us -> 20.4 us  [packed_swap(): got = lax.all_to_all(flat, axis, split_axis=0, concat_axis=0, tiled=True)]
    all_to_all x4 -> x2, starting transfers between devices: 19.7 us -> 9.63 us  [packed_swap(): got = lax.all_to_all(flat, axis, split_axis=0, concat_axis=0, tiled=True)]
    ppermute x4 -> x2, waiting for transfers between devices: 25.5 us -> 16.5 us  [the longest x1 10 us: shards(): lax.ppermute(to_prev, 'tile', [(i + 1, i) for i in range(ends)])]
    ppermute x4 -> x2, starting transfers between devices: 18.5 us -> 9.62 us  [the longest x1 5.17 us: shards(): lax.ppermute(to_next, 'tile', [(i, i + 1) for i in range(ends)])]
    transpose x2 -> x5, local copies, waits for them, and re-layouts: 2.66 us -> 8.73 us  [the longest x1 2.58 us: shards(): back_got.transpose(1, 3, 0, 2).reshape(subspace, rows_here, coarse_cols)]
    slice x2 -> x7, local copies, waits for them, and re-layouts: 0.17 us -> 3.71 us  [the longest x2 1.66 us: unpack(): got[2 * size:].reshape(-1, chunk, rim)]
    squeeze x2 -> x0, local copies, waits for them, and re-layouts: 3.04 us -> none  [the longest x1 1.96 us: shards(): lax.all_to_all(back_split, 'spec', split_axis=0, concat_axis=3, tiled=True)]
  transfers between devices with their start and end apart: 8 -> 4, of which waited for: 5 -> 4; matrix products, arithmetic and copies ran while one was open for 16% -> 5% of each run, Pallas kernels for 0% -> 0%
where the time goes in v6:
time: 128 us; the launch traced here: 127 us
  local copies, waits for them, and re-layouts  51.6 us (40%)
  waiting for transfers between devices  36.9 us (29%)
  starting transfers between devices  19.3 us (15%)
  matrix products  11.7 us (9%)
  other arithmetic  5.81 us (5%)
  between operations  1.97 us (2%)
    all_to_all x2, waiting for transfers between devices, packed_swap(): got = lax.all_to_all(flat, axis, split_axis=0, concat_axis=0, tiled=True)  20.4 us
    ppermute x1, waiting for transfers between devices, shards(): lax.ppermute(to_prev, 'tile', [(i + 1, i) for i in range(ends)])  10 us
    all_to_all x2, starting transfers between devices, packed_swap(): got = lax.all_to_all(flat, axis, split_axis=0, concat_axis=0, tiled=True)  9.63 us
    unnamed x40, local copies, waits for them, and re-layouts  9.62 us
    reshape x3, local copies, waits for them, and re-layouts, packed_swap(): flat = jnp.concatenate([p.reshape(count, -1) for p in parts], axis=1)  7.91 us
    ppermute x1, waiting for transfers between devices, shards(): lax.ppermute(to_next, 'tile', [(i, i + 1) for i in range(ends)])  6.44 us
    reshape x3, local copies, waits for them, and re-layouts, packed_swap(): out.append(got[:, at:at + size].reshape(p.shape))  6.19 us
    ppermute x1, starting transfers between devices, shards(): lax.ppermute(to_next, 'tile', [(i, i + 1) for i in range(ends)])  5.17 us
  transfers between devices with their start and end apart: 4, of which 4 were waited for; matrix products, arithmetic and copies ran while one was open for 5% of the time, Pallas kernels for 0%

profile of v6, /device:TPU:24, one launch (start us, length us, event | category | flops | bytes accessed | tf_op | source)
XLA Modules:
  0.0 127.2 jit_solution(18446601196099993664)
XLA Ops:
  2.6 1.7 %reshape.187 = bf16[256,2044]{1,0:T(8,128)(2,1)S(1)} reshape(bf16[523264]{0:T(1024)(128)(2,1)S(1)} %slice.124) | data formatting | bytes 2093056 | tf_op jit(solution)/shard_map/reshape | solution.py:55
  6.7 2.3 %copy.60 = bf16[16,32,16,16]{3,2,1,0:T(8,128)(2,1)S(1)} copy(bf16[16,32,16,16]{1,2,3,0:T(8,128)(2,1)S(1)} %fusion.5) | data formatting | bytes 524288 | tf_op jit(solution)/shard_map/convert_element_type | solution.py:108
  9.0 3.6 %reshape.189 = bf16[16,8192]{1,0:T(8,128)(2,1)S(1)} reshape(bf16[16,32,16,16]{3,2,1,0:T(8,128)(2,1)S(1)} %copy.60) | data formatting | bytes 524288 | tf_op jit(solution)/shard_map/reshape | solution.py:75
  17.2 5.8 %all-to-all-start = ((bf16[16,2,11264]{2,1,0:T(2,128)(2,1)}), bf16[16,2,11264]{2,1,0:T(2,128)(2,1)S(1)}, u32[]{:S(2)}, u32[]{:S(2)}) async-start(bf16[16,2,11264]{2,1,0:T(2,128)(2,1)} %reshape.215), calls=%async_computation | async-start | bytes 1441792 | tf_op jit(solution)/shard_map/all_to_all | solution.py:76
  24.3 11.7 %all-to-all-done = bf16[16,2,11264]{2,1,0:T(2,128)(2,1)S(1)} async-done(((bf16[16,2,11264]{2,1,0:T(2,128)(2,1)}), bf16[16,2,11264]{2,1,0:T(2,128)(2,1)S(1)}, u32[]{:S(2)}, u32[]{:S(2)}) %all-to-all-start) | async-done | bytes 720928 | tf_op jit(solution)/shard_map/all_to_all | solution.py:76
  37.8 1.7 %reshape.192 = bf16[16,32,16,16]{3,2,1,0:T(8,128)(2,1)S(1)} reshape(bf16[16,8192]{1,0:T(8,128)(2,1)S(1)} %slice.126) | data formatting | bytes 524288 | tf_op jit(solution)/shard_map/reshape | solution.py:80
  39.5 1.8 %copy.64 = bf16[32,16,16,16]{0,3,2,1:T(8,128)(2,1)S(1)} copy(bf16[32,16,16,16]{3,1,0,2:T(8,128)(2,1)S(1)} %bitcast.78) | data formatting | bytes 524288 | tf_op jit(solution)/shard_map/transpose | solution.py:111
  45.3 1.6 %pad_maximum_fusion = bf16[180224]{0:T(1024)(128)(2,1)} fusion(bf16[114688]{0:T(1024)(128)(2,1)S(1)} %reshape.197, bf16[32768]{0:T(1024)(128)(2,1)} %reshape.196, bf16[32768]{0:T(1024)(128)(2,1)} %reshape.195), kind=kLoop, calls=%fused_computation.32 | loop fusion | flops 1081344 | bytes 720896 | tf_op jit(solution)/shard_map/concatenate | solution.py:119
  47.0 5.2 %collective-permute-start = (bf16[180224]{0:T(1024)(128)(2,1)}, bf16[180224]{0:T(1024)(128)(2,1)S(1)}, u32[]{:S(2)}, u32[]{:S(2)}) collective-permute-start(bf16[180224]{0:T(1024)(128)(2,1)} %pad_maximum_fusion), channel_id=1, source_target_pairs={{0,16},{16,32},{32,48},{48,64},{64,80},{80,96},{96,112},{112,128},... | collective-permute-start | bytes 1081352 | tf_op jit(solution)/shard_map/ppermute | solution.py:133
  53.2 4.5 %collective-permute-start.1 = (bf16[180224]{0:T(1024)(128)(2,1)S(1)}, bf16[180224]{0:T(1024)(128)(2,1)S(1)}, u32[]{:S(2)}, u32[]{:S(2)}) collective-permute-start(bf16[180224]{0:T(1024)(128)(2,1)S(1)} %pad_maximum_fusion.1), channel_id=1, source_target_pairs={{16,0},{32,16},{48,32},{64,48},{80,64},{96,80},{112,96},{128,112},... | collective-permute-start | bytes 1081352 | tf_op jit(solution)/shard_map/ppermute | solution.py:134
  57.7 6.4 %collective-permute-done = bf16[180224]{0:T(1024)(128)(2,1)S(1)} collective-permute-done((bf16[180224]{0:T(1024)(128)(2,1)}, bf16[180224]{0:T(1024)(128)(2,1)S(1)}, u32[]{:S(2)}, u32[]{:S(2)}) %collective-permute-start) | collective-permute-done | bytes 360480 | tf_op jit(solution)/shard_map/ppermute | solution.py:133
  64.3 10.0 %collective-permute-done.1 = bf16[180224]{0:T(1024)(128)(2,1)S(1)} collective-permute-done((bf16[180224]{0:T(1024)(128)(2,1)S(1)}, bf16[180224]{0:T(1024)(128)(2,1)S(1)}, u32[]{:S(2)}, u32[]{:S(2)}) %collective-permute-start.1) | collective-permute-done | bytes 360480 | tf_op jit(solution)/shard_map/ppermute | solution.py:134
  76.0 1.6 %slice.139 = bf16[114688]{0:T(1024)(128)(2,1)} slice(bf16[180224]{0:T(1024)(128)(2,1)} %copy-done.11), slice={[65536:180224]} | slice | bytes 458752 | tf_op jit(solution)/shard_map/slice | solution.py:124
  83.7 1.7 %copy.78 = bf16[16,32,16,16]{3,2,1,0:T(8,128)(2,1)S(1)} copy(bf16[16,32,16,16]{1,3,0,2:T(8,128)(2,1)S(1)} %bitcast.80) | data formatting | bytes 524288 | tf_op jit(solution)/shard_map/transpose | solution.py:144
  85.4 3.6 %reshape.204 = bf16[16,8192]{1,0:T(8,128)(2,1)S(1)} reshape(bf16[16,32,16,16]{3,2,1,0:T(8,128)(2,1)S(1)} %copy.78) | data formatting | bytes 524288 | tf_op jit(solution)/shard_map/reshape | solution.py:75
  92.9 3.9 %all-to-all-start.1 = ((bf16[16,2,11264]{2,1,0:T(2,128)(2,1)}), bf16[16,2,11264]{2,1,0:T(2,128)(2,1)S(1)}, u32[]{:S(2)}, u32[]{:S(2)}) async-start(bf16[16,2,11264]{2,1,0:T(2,128)(2,1)} %reshape.217), calls=%async_computation.1 | async-start | bytes 1441792 | tf_op jit(solution)/shard_map/all_to_all | solution.py:76
  98.5 2.3 %fusion.48 = f32[32,16,1024]{2,0,1:T(8,128)} fusion(f32[8,32,1]{1,0,2:T(8,128)S(1)} %convolution_bitcast_fusion.1, bf16[8,16,1024]{2,0,1:T(8,128)(2,1)S(1)} %fusion.7), kind=kOutput, calls=%fused_computation.82 | convolution fusion | flops 50331648 | bytes 2360320 | tf_op jit(solution)/shard_map/mq,mrc->qrc/dot_general | solution.py:155
  100.9 8.7 %all-to-all-done.1 = bf16[16,2,11264]{2,1,0:T(2,128)(2,1)S(1)} async-done(((bf16[16,2,11264]{2,1,0:T(2,128)(2,1)}), bf16[16,2,11264]{2,1,0:T(2,128)(2,1)S(1)}, u32[]{:S(2)}, u32[]{:S(2)}) %all-to-all-start.1) | async-done | bytes 720928 | tf_op jit(solution)/shard_map/all_to_all | solution.py:76
  111.4 1.7 %reshape.205 = bf16[16,32,16,16]{3,2,1,0:T(8,128)(2,1)S(1)} reshape(bf16[16,8192]{1,0:T(8,128)(2,1)S(1)} %slice.141) | data formatting | bytes 524288 | tf_op jit(solution)/shard_map/reshape | solution.py:80
  113.1 2.6 %copy.81 = bf16[32,16,16,16]{0,3,2,1:T(8,128)(2,1)S(1)} copy(bf16[32,16,16,16]{1,3,0,2:T(8,128)(2,1)S(1)} %bitcast.79) | data formatting | bytes 524288 | tf_op jit(solution)/shard_map/transpose | solution.py:148
  116.2 2.8 %reshape.207 = bf16[16,14,16,64]{3,2,1,0:T(8,128)(2,1)} reshape(bf16[16,14336]{1,0:T(8,128)(2,1)} %slice.142) | data formatting | bytes 917504 | tf_op jit(solution)/shard_map/reshape | solution.py:80
  119.0 2.5 %copy.86 = bf16[14,64,16,16]{1,3,2,0:T(8,128)(2,1)} copy(bf16[14,64,16,16]{1,3,0,2:T(8,128)(2,1)} %bitcast.84) | data formatting | bytes 917504 | tf_op jit(solution)/shard_map/transpose | solution.py:149
  121.5 2.2 %copy.87 = bf16[14,64,256]{2,1,0:T(8,128)(2,1)} copy(bf16[14,64,256]{1,2,0:T(8,128)(2,1)} %bitcast.85) | data formatting | bytes 917504
  123.7 3.4 %fusion.2 = bf16[32,16,1024]{2,1,0:T(8,128)(2,1)} fusion(f32[32,16,1024]{2,0,1:T(8,128)S(1)} %copy-done.1, bf16[32,16,1024]{2,1,0:T(8,128)(2,1)S(1)} %copy-done.4, bf16[32,16,256]{2,1,0:T(8,128)(2,1)S(1)} %copy.82, bf16[256,2044]{1,0:T(8,128)(2,1)} %copy-done.5), kind=kOutput, calls=%fused_computation.3 | convolution fusion | flops 271056896 | bytes 4980736 | tf_op jit(solution)/shard_map/qrj,jc->qrc/dot_general | solution.py:150
  (99 shorter events, 31.9 us)
Async XLA Ops:
  0.6 78.8 %copy-start = (bf16[224,32]{0,1:T(8,128)(2,1)S(1)}, bf16[224,32]{0,1:T(8,128)(2,1)}, u32[]{:S(2)}) copy-start(bf16[224,32]{0,1:T(8,128)(2,1)} %param.6) | copy-start | bytes 43012
  2.6 2.6 %copy-start.2 = (bf16[32,16,1024]{2,1,0:T(8,128)(2,1)S(1)}, bf16[32,16,1024]{2,1,0:T(8,128)(2,1)}, u32[]{:S(2)}) copy-start(bf16[32,16,1024]{2,1,0:T(8,128)(2,1)} %param.5) | copy-start | bytes 3145732
  4.3 1.0 copy-start.5
  9.0 3.6 %copy-start.10 = (bf16[14,64,256]{2,1,0:T(8,128)(2,1)S(1)}, bf16[14,64,256]{2,1,0:T(8,128)(2,1)}, u32[]{:S(2)}) copy-start(bf16[14,64,256]{2,1,0:T(8,128)(2,1)} %param.8) | copy-start | bytes 1376260
  17.2 18.8 %all-to-all-start = ((bf16[16,2,11264]{2,1,0:T(2,128)(2,1)}), bf16[16,2,11264]{2,1,0:T(2,128)(2,1)S(1)}, u32[]{:S(2)}, u32[]{:S(2)}) async-start(bf16[16,2,11264]{2,1,0:T(2,128)(2,1)} %reshape.215), calls=%async_computation | async-start | bytes 1441792 | tf_op jit(solution)/shard_map/all_to_all | solution.py:76
  23.7 17.6 %copy-start.8 = (bf16[128,764]{1,0:T(8,128)(2,1)}, bf16[128,764]{1,0:T(8,128)(2,1)S(1)}, u32[]{:S(2)}) copy-start(bf16[128,764]{1,0:T(8,128)(2,1)S(1)} %reshape.194) | copy-start | bytes 586756
  41.3 2.2 %copy-start.7 = (bf16[16,14336]{1,0:T(8,128)(2,1)S(1)}, bf16[16,14336]{1,0:T(8,128)(2,1)}, u32[]{:S(2)}) copy-start(bf16[16,14336]{1,0:T(8,128)(2,1)} %slice.130) | copy-start | bytes 1376260
  47.0 17.2 %collective-permute-start = (bf16[180224]{0:T(1024)(128)(2,1)}, bf16[180224]{0:T(1024)(128)(2,1)S(1)}, u32[]{:S(2)}, u32[]{:S(2)}) collective-permute-start(bf16[180224]{0:T(1024)(128)(2,1)} %pad_maximum_fusion), channel_id=1, source_target_pairs={{0,16},{16,32},{32,48},{48,64},{64,80},{80,96},{96,112},{112,128},... | collective-permute-start | bytes 1081352 | tf_op jit(solution)/shard_map/ppermute | solution.py:133
  53.2 21.1 %collective-permute-start.1 = (bf16[180224]{0:T(1024)(128)(2,1)S(1)}, bf16[180224]{0:T(1024)(128)(2,1)S(1)}, u32[]{:S(2)}, u32[]{:S(2)}) collective-permute-start(bf16[180224]{0:T(1024)(128)(2,1)S(1)} %pad_maximum_fusion.1), channel_id=1, source_target_pairs={{16,0},{32,16},{48,32},{64,48},{80,64},{96,80},{112,96},{128,112},... | collective-permute-start | bytes 1081352 | tf_op jit(solution)/shard_map/ppermute | solution.py:134
  74.4 0.7 copy-start.11
  79.2 0.8 copy-start.14
  81.2 1.5 %copy-start.9 = (bf16[128,764]{1,0:T(8,128)(2,1)S(1)}, bf16[128,764]{1,0:T(8,128)(2,1)}, u32[]{:S(2)}) copy-start(bf16[128,764]{1,0:T(8,128)(2,1)} %copy-done.8) | copy-start | bytes 586756
  85.4 3.6 %copy-start.6 = (bf16[224,16,64]{2,0,1:T(8,128)(2,1)S(1)}, bf16[224,16,64]{2,0,1:T(8,128)(2,1)}, u32[]{:S(2)}) copy-start(bf16[224,16,64]{2,0,1:T(8,128)(2,1)} %slice.140) | copy-start | bytes 1376260
  90.2 6.6 %copy-start.13 = (bf16[8,224]{1,0:T(8,128)(2,1)S(1)}, bf16[8,224]{1,0:T(8,128)(2,1)}, u32[]{:S(2)}) copy-start(bf16[8,224]{1,0:T(8,128)(2,1)} %param.7) | copy-start | bytes 10756
  90.2 6.7 %copy-start.3 = (bf16[32,16,1024]{2,1,0:T(8,128)(2,1)S(1)}, bf16[32,16,1024]{2,1,0:T(8,128)(2,1)}, u32[]{:S(2)}) copy-start(bf16[32,16,1024]{2,1,0:T(8,128)(2,1)} %param.5) | copy-start | bytes 3145732
  90.2 6.7 %copy-start.12 = (bf16[8,16,1024]{2,1,0:T(8,128)(2,1)S(1)}, bf16[8,16,1024]{2,1,0:T(8,128)(2,1)}, u32[]{:S(2)}) copy-start(bf16[8,16,1024]{2,1,0:T(8,128)(2,1)} %param.9) | copy-start | bytes 786436
  92.9 16.6 %all-to-all-start.1 = ((bf16[16,2,11264]{2,1,0:T(2,128)(2,1)}), bf16[16,2,11264]{2,1,0:T(2,128)(2,1)S(1)}, u32[]{:S(2)}, u32[]{:S(2)}) async-start(bf16[16,2,11264]{2,1,0:T(2,128)(2,1)} %reshape.217), calls=%async_computation.1 | async-start | bytes 1441792 | tf_op jit(solution)/shard_map/all_to_all | solution.py:76
  119.0 4.7 %copy-start.1 = (f32[32,16,1024]{2,0,1:T(8,128)S(1)}, f32[32,16,1024]{2,0,1:T(8,128)}, u32[]{:S(2)}) copy-start(f32[32,16,1024]{2,0,1:T(8,128)} %fusion.48) | copy-start | bytes 6291460
  119.0 4.7 %copy-start.4 = (bf16[32,16,1024]{2,1,0:T(8,128)(2,1)S(1)}, bf16[32,16,1024]{2,1,0:T(8,128)(2,1)}, u32[]{:S(2)}) copy-start(bf16[32,16,1024]{2,1,0:T(8,128)(2,1)} %param.5) | copy-start | bytes 3145732

commit v7 on v5

--- a/solution.py
+++ b/solution.py
@@ -113,18 +113,17 @@
     inside = (coarse_at >= 0) & (coarse_at < n_tile * coarse_rows)
     resid_wide = jnp.where(inside, blurred - obs_wide.astype(f32), 0.0).astype(bf16)
 
+    coef_resid = jnp.einsum("bq,bji->qji", basis, resid_wide, preferred_element_type=f32)
+    rows_back = split_dot("qjk,kr->qjr", coef_resid, own_rows).astype(bf16)
+    back_split = rows_back.reshape(subspace, chunk, n_spec, rows_here).transpose(2, 0, 3, 1)
+    rows_pixel = lax.all_to_all(back_split, "spec", split_axis=0, concat_axis=3, tiled=True)[0]
+    grad_hs = jnp.einsum("qrj,jc->qrc", rows_pixel, column_t, preferred_element_type=f32)
+
     resid_cols = lax.slice_in_dim(resid_wide, rim, rim + coarse_rows, axis=2)
     resid_split = resid_cols.reshape(n_spec, group, chunk, coarse_rows)
+    resid_split, _ = lax.optimization_barrier((resid_split, rows_pixel))
     resid_bands = lax.all_to_all(resid_split, "spec", split_axis=0, concat_axis=2, tiled=True)[0]
     hs_residual = resid_bands.transpose(0, 2, 1)
-
-    coef_resid = jnp.einsum("bq,bji->qji", basis, resid_wide, preferred_element_type=f32)
-    rows_back = split_dot("qjk,kr->qjr", coef_resid, own_rows)
-    back_split = rows_back.reshape(subspace, chunk, n_spec, rows_here).transpose(2, 0, 3, 1)
-    rows_pixel = lax.all_to_all(back_split, "spec", split_axis=0, concat_axis=3, tiled=True)[0]
-    grad_hs = jnp.einsum(
-        "qrj,jc->qrc", rows_pixel, column_t.astype(f32), precision=highest
-    )
 
     resp_basis = jnp.dot(response.astype(f32), basis_wide, precision=highest)
     multi_pred = jnp.einsum("mq,qrc->mrc", resp_basis, latent.astype(f32), precision=highest)

time: 117 us -> 107 us (0.915)
  waiting for transfers between devices: 34.4 us -> 31.4 us
  matrix products: 12.8 us -> 9.9 us
  other arithmetic: 5.76 us -> 3.07 us
  local copies, waits for them, and re-layouts: 22.9 us -> 20.4 us
    all_to_all x1, waiting for transfers between devices: 3.99 us -> 0.02 us  [shards(): lax.all_to_all(resid_split, 'spec', split_axis=0, concat_axis=2, tiled=True)]
    all_to_all x1 -> x0, other arithmetic: 2.69 us -> none  [shards(): lax.all_to_all(back_split, 'spec', split_axis=0, concat_axis=3, tiled=True)]
    all_to_all x1, starting transfers between devices: 3.57 us -> 5.48 us  [shards(): lax.all_to_all(back_split, 'spec', split_axis=0, concat_axis=3, tiled=True)]
    dot_general x1, matrix products: 4.96 us -> 3.44 us  [shards(): jnp.einsum('qrj,jc->qrc', rows_pixel, column_t, preferred_element_type=f32)]
    dot_general x1, matrix products: 2.36 us -> 1.01 us  [shards(): jnp.einsum('mq,mrc->qrc', resp_basis, multi_resid.astype(f32), precision=...]
    transpose x1, local copies, waits for them, and re-layouts: 1.58 us -> 0.27 us  [shards(): rows_back.reshape(subspace, chunk, n_spec, rows_here).transpose(2, 0, 3, 1)]
    unnamed x28 -> x24, local copies, waits for them, and re-layouts: 11.7 us -> 10.7 us
  transfers between devices with their start and end apart: 8 -> 8, of which waited for: 5 -> 4; matrix products, arithmetic and copies ran while one was open for 16% -> 17% of each run, Pallas kernels for 0% -> 0%
where the time goes in v7:
time: 107 us; the launch traced here: 106 us
  starting transfers between devices  39 us (36%)
  waiting for transfers between devices  31.4 us (29%)
  local copies, waits for them, and re-layouts  20.4 us (19%)
  matrix products  9.9 us (9%)
  other arithmetic  3.07 us (3%)
  between operations  1.76 us (2%)
    ppermute x1, waiting for transfers between devices, shards(): lax.ppermute(lax.slice_in_dim(own_part, half, wide_rows, axis=2), 'tile',...  14.5 us
    unnamed x24, local copies, waits for them, and re-layouts  10.7 us
    ppermute x1, waiting for transfers between devices, with_halo(): lax.ppermute(tail, axis, [(i, (i + 1) % count) for i in range(ends)])  5.95 us
    all_to_all x1, waiting for transfers between devices, shards(): lax.all_to_all(back_split, 'spec', split_axis=0, concat_axis=3, tiled=True)  5.92 us
    all_to_all x1, starting transfers between devices, shards(): lax.all_to_all(cols_done, 'spec', split_axis=0, concat_axis=3, tiled=True)  5.76 us
    ppermute x1, starting transfers between devices, shards(): lax.ppermute(lax.slice_in_dim(own_part, half, wide_rows, axis=2), 'tile',...  5.72 us
    all_to_all x1, starting transfers between devices, shards(): lax.all_to_all(back_split, 'spec', split_axis=0, concat_axis=3, tiled=True)  5.48 us
    ppermute x1, starting transfers between devices, with_halo(): lax.ppermute(tail, axis, [(i, (i + 1) % count) for i in range(ends)])  5.18 us
  transfers between devices with their start and end apart: 8, of which 4 were waited for; matrix products, arithmetic and copies ran while one was open for 17% of the time, Pallas kernels for 0%

profile of v7, /device:TPU:24, one launch (start us, length us, event | category | flops | bytes accessed | tf_op | source)
XLA Modules:
  0.0 105.6 jit_solution(5554229399589716740)
XLA Ops:
  2.6 1.7 %reshape.88 = bf16[256,2044]{1,0:T(8,128)(2,1)S(1)} reshape(bf16[523264]{0:T(1024)(128)(2,1)S(1)} %slice.36) | data formatting | bytes 2093056 | tf_op jit(solution)/shard_map/reshape | solution.py:55
  4.3 1.4 %fusion.45 = bf16[16,16,16,32]{3,2,1,0:T(8,128)(2,1)S(1)} fusion(bf16[16,16,1024,1]{2,1,3,0:T(8,128)(2,1)S(1)} %bitcast.98, bf16[32,16,1024]{2,1,0:T(8,128)(2,1)S(1)} %copy-done.1), kind=kOutput, calls=%fused_computation.72 | convolution fusion | flops 268566528 | bytes 1835008 | tf_op jit(solution)/shard_map/qrc,sjc->sqjr/dot_general | solution.py:85
  5.8 1.7 %reshape.101 = bf16[16,2,4096]{2,1,0:T(2,128)(2,1)} reshape(bf16[16,16,16,32]{3,2,1,0:T(8,128)(2,1)S(1)} %fusion.45) | data formatting | bytes 524288
  7.5 5.8 %all-to-all-start = ((bf16[16,2,4096]{2,1,0:T(2,128)(2,1)}), bf16[16,2,4096]{2,1,0:T(2,128)(2,1)S(1)}, u32[]{:S(2)}, u32[]{:S(2)}) async-start(bf16[16,2,4096]{2,1,0:T(2,128)(2,1)} %reshape.101), calls=%async_computation | async-start | bytes 524288 | tf_op jit(solution)/shard_map/all_to_all | solution.py:91
  13.3 5.2 %collective-permute-start.2 = (bf16[14,32,256]{2,1,0:T(8,128)(2,1)S(1)}, bf16[14,32,256]{2,1,0:T(8,128)(2,1)S(1)}, u32[]{:S(2)}, u32[]{:S(2)}) collective-permute-start(bf16[14,32,256]{2,1,0:T(8,128)(2,1)S(1)} %get-tuple-element.10), channel_id=1, source_target_pairs={{0,16},{16,32},{32,48},{48,64},{64,80},{80,96},{96,112},{112,128},... | collective-permute-start | bytes 688136 | tf_op jit(solution)/shard_map/ppermute | solution.py:21
  18.5 4.2 %collective-permute-start.3 = (bf16[14,32,256]{2,1,0:T(8,128)(2,1)S(1)}, bf16[14,32,256]{2,1,0:T(8,128)(2,1)S(1)}, u32[]{:S(2)}, u32[]{:S(2)}) collective-permute-start(bf16[14,32,256]{2,1,0:T(8,128)(2,1)S(1)} %get-tuple-element.11), channel_id=1, source_target_pairs={{16,0},{32,16},{48,32},{64,48},{80,64},{96,80},{112,96},{128,112},... | collective-permute-start | bytes 688136 | tf_op jit(solution)/shard_map/ppermute | solution.py:23
  23.1 5.9 %collective-permute-done.2 = bf16[14,32,256]{2,1,0:T(8,128)(2,1)S(1)} collective-permute-done((bf16[14,32,256]{2,1,0:T(8,128)(2,1)S(1)}, bf16[14,32,256]{2,1,0:T(8,128)(2,1)S(1)}, u32[]{:S(2)}, u32[]{:S(2)}) %collective-permute-start.2) | collective-permute-done | bytes 229408 | tf_op jit(solution)/shard_map/ppermute | solution.py:21
  29.5 5.0 %collective-permute-done.3 = bf16[14,32,256]{2,1,0:T(8,128)(2,1)S(1)} collective-permute-done((bf16[14,32,256]{2,1,0:T(8,128)(2,1)S(1)}, bf16[14,32,256]{2,1,0:T(8,128)(2,1)S(1)}, u32[]{:S(2)}, u32[]{:S(2)}) %collective-permute-start.3) | collective-permute-done | bytes 229408 | tf_op jit(solution)/shard_map/ppermute | solution.py:23
  35.8 1.1 %copy.44 = bf16[16,14,16,128]{3,2,1,0:T(8,128)(2,1)} copy(bf16[16,14,16,128]{3,2,0,1:T(8,128)(2,1)S(1)} %bitcast.93) | data formatting | bytes 1835008 | tf_op jit(solution)/shard_map/transpose | solution.py:94
  36.9 4.9 %all-to-all-start.1 = ((bf16[16,14,16,128]{3,2,1,0:T(8,128)(2,1)}), bf16[16,14,16,128]{3,2,1,0:T(8,128)(2,1)}, u32[]{:S(2)}, u32[]{:S(2)}) async-start(bf16[16,14,16,128]{3,2,1,0:T(8,128)(2,1)} %copy.44), calls=%async_computation.1 | async-start | bytes 1835008 | tf_op jit(solution)/shard_map/all_to_all | solution.py:95
  44.5 5.7 %collective-permute-start = (f32[32,16,64]{2,1,0:T(8,128)S(1)}, f32[32,16,64]{2,1,0:T(8,128)S(1)}, u32[]{:S(2)}, u32[]{:S(2)}) collective-permute-start(f32[32,16,64]{2,1,0:T(8,128)S(1)} %get-tuple-element.14), channel_id=1, source_target_pairs={{0,16},{16,32},{32,48},{48,64},{64,80},{80,96},{96,112},{112,128},... | collective-permute-start | bytes 393224 | tf_op jit(solution)/shard_map/ppermute | solution.py:100
  50.2 3.3 %collective-permute-start.1 = (f32[32,16,64]{2,1,0:T(8,128)S(1)}, f32[32,16,64]{2,1,0:T(8,128)S(1)}, u32[]{:S(2)}, u32[]{:S(2)}) collective-permute-start(f32[32,16,64]{2,1,0:T(8,128)S(1)} %get-tuple-element.15), channel_id=1, source_target_pairs={{16,0},{32,16},{48,32},{64,48},{80,64},{96,80},{112,96},{128,112},... | collective-permute-start | bytes 393224 | tf_op jit(solution)/shard_map/ppermute | solution.py:105
  53.6 14.5 %collective-permute-done = f32[32,16,64]{2,1,0:T(8,128)S(1)} collective-permute-done((f32[32,16,64]{2,1,0:T(8,128)S(1)}, f32[32,16,64]{2,1,0:T(8,128)S(1)}, u32[]{:S(2)}, u32[]{:S(2)}) %collective-permute-start) | collective-permute-done | bytes 131104 | tf_op jit(solution)/shard_map/ppermute | solution.py:100
  68.7 1.3 %bitcast_convert_fusion = f32[224,16,128]{2,1,0:T(8,128)S(1)} fusion(bf16[16,14,16,128]{3,2,1,0:T(8,128)(2,1)} %all-to-all-done.1), kind=kLoop, calls=%fused_computation.19 | loop fusion | flops 458752 | bytes 2752512 | tf_op jit(solution)/shard_map/convert_element_type | solution.py:114
  72.6 1.7 %reshape.103 = bf16[16,2,4096]{2,1,0:T(2,128)(2,1)} reshape(bf16[16,16,16,32]{3,2,1,0:T(8,128)(2,1)S(1)} %bitcast.91) | data formatting | bytes 524288
  74.2 5.5 %all-to-all-start.2 = ((bf16[16,2,4096]{2,1,0:T(2,128)(2,1)}), bf16[16,2,4096]{2,1,0:T(2,128)(2,1)S(1)}, u32[]{:S(2)}, u32[]{:S(2)}) async-start(bf16[16,2,4096]{2,1,0:T(2,128)(2,1)} %reshape.103), calls=%async_computation.2 | async-start | bytes 524288 | tf_op jit(solution)/shard_map/all_to_all | solution.py:119
  80.6 1.3 %reshape.105 = bf16[16,2,7168]{2,1,0:T(2,128)(2,1)} reshape(bf16[16,14,16,64]{3,2,1,0:T(8,128)(2,1)S(1)} %bitcast.94) | data formatting | bytes 917504
  81.9 5.9 %all-to-all-done.2 = bf16[16,2,4096]{2,1,0:T(2,128)(2,1)S(1)} async-done(((bf16[16,2,4096]{2,1,0:T(2,128)(2,1)}), bf16[16,2,4096]{2,1,0:T(2,128)(2,1)S(1)}, u32[]{:S(2)}, u32[]{:S(2)}) %all-to-all-start.2) | async-done | bytes 262176 | tf_op jit(solution)/shard_map/all_to_all | solution.py:119
  87.8 4.5 %all-to-all-start.3 = ((bf16[16,2,7168]{2,1,0:T(2,128)(2,1)}), bf16[16,2,7168]{2,1,0:T(2,128)(2,1)}, u32[]{:S(2)}, u32[]{:S(2)}) async-start(bf16[16,2,7168]{2,1,0:T(2,128)(2,1)} %reshape.105), calls=%async_computation.3 | async-start | bytes 917504 | tf_op jit(solution)/shard_map/all_to_all | solution.py:125
  92.3 1.6 %fusion.7 = bf16[8,16,1024]{2,0,1:T(8,128)(2,1)S(1)} fusion(f32[8,32,1]{1,0,2:T(8,128)S(1)} %convolution_bitcast_fusion.1, bf16[32,16,1024]{2,1,0:T(8,128)(2,1)S(1)} %copy-done.2, bf16[8,16,1024]{2,1,0:T(8,128)(2,1)S(1)} %copy-done.5), kind=kOutput, calls=%fused_computation.12 | convolution fusion | flops 50724864 | bytes 1573888 | tf_op jit(solution)/shard_map/mq,qrc->mrc/dot_general | solution.py:129
  94.9 1.5 %reshape.104 = bf16[16,16,16,32]{3,2,1,0:T(8,128)(2,1)} reshape(bf16[16,2,4096]{2,1,0:T(2,128)(2,1)S(1)} %all-to-all-done.2) | data formatting | bytes 524288
  96.3 2.4 %copy.51 = bf16[32,16,256]{2,1,0:T(8,128)(2,1)S(1)} copy(bf16[32,16,256]{0,1,2:T(8,128)(2,1)} %bitcast.89) | data formatting | bytes 524288 | tf_op jit(solution)/shard_map/squeeze | solution.py:119
  98.7 3.4 %fusion.2 = bf16[32,16,1024]{2,1,0:T(8,128)(2,1)} fusion(f32[32,16,1024]{2,0,1:T(8,128)S(1)} %fusion.48, bf16[32,16,1024]{2,1,0:T(8,128)(2,1)S(1)} %copy-done.2, bf16[32,16,256]{2,1,0:T(8,128)(2,1)S(1)} %copy.51, bf16[256,2044]{1,0:T(8,128)(2,1)} %copy-done.3), kind=kOutput, calls=%fused_computation.3 | convolution fusion | flops 271056896 | bytes 4980736 | tf_op jit(solution)/shard_map/qrj,jc->qrc/dot_general | solution.py:120
  102.2 2.1 %reshape.106 = bf16[16,14,16,64]{3,2,1,0:T(8,128)(2,1)S(1)} reshape(bf16[16,2,7168]{2,1,0:T(2,128)(2,1)} %all-to-all-done.3) | data formatting | bytes 917504
  (52 shorter events, 12.3 us)
Async XLA Ops:
  0.6 67.6 %copy-start = (bf16[224,32]{0,1:T(8,128)(2,1)S(1)}, bf16[224,32]{0,1:T(8,128)(2,1)}, u32[]{:S(2)}) copy-start(bf16[224,32]{0,1:T(8,128)(2,1)} %param.6) | copy-start | bytes 43012
  2.6 1.7 %copy-start.1 = (bf16[32,16,1024]{2,1,0:T(8,128)(2,1)S(1)}, bf16[32,16,1024]{2,1,0:T(8,128)(2,1)}, u32[]{:S(2)}) copy-start(bf16[32,16,1024]{2,1,0:T(8,128)(2,1)} %param.5) | copy-start | bytes 3145732
  4.3 1.5 %copy-start.3 = (bf16[256,2044]{1,0:T(8,128)(2,1)}, bf16[256,2044]{1,0:T(8,128)(2,1)S(1)}, u32[]{:S(2)}) copy-start(bf16[256,2044]{1,0:T(8,128)(2,1)S(1)} %reshape.88) | copy-start | bytes 3139588
  5.8 7.5 %copy-start.4 = (bf16[14,64,256]{2,1,0:T(8,128)(2,1)S(1)}, bf16[14,64,256]{2,1,0:T(8,128)(2,1)}, u32[]{:S(2)}) copy-start(bf16[14,64,256]{2,1,0:T(8,128)(2,1)} %param.8) | copy-start | bytes 1376260
  7.5 29.4 %all-to-all-start = ((bf16[16,2,4096]{2,1,0:T(2,128)(2,1)}), bf16[16,2,4096]{2,1,0:T(2,128)(2,1)S(1)}, u32[]{:S(2)}, u32[]{:S(2)}) async-start(bf16[16,2,4096]{2,1,0:T(2,128)(2,1)} %reshape.101), calls=%async_computation | async-start | bytes 524288 | tf_op jit(solution)/shard_map/all_to_all | solution.py:91
  13.3 15.8 %collective-permute-start.2 = (bf16[14,32,256]{2,1,0:T(8,128)(2,1)S(1)}, bf16[14,32,256]{2,1,0:T(8,128)(2,1)S(1)}, u32[]{:S(2)}, u32[]{:S(2)}) collective-permute-start(bf16[14,32,256]{2,1,0:T(8,128)(2,1)S(1)} %get-tuple-element.10), channel_id=1, source_target_pairs={{0,16},{16,32},{32,48},{48,64},{64,80},{80,96},{96,112},{112,128},... | collective-permute-start | bytes 688136 | tf_op jit(solution)/shard_map/ppermute | solution.py:21
  18.5 16.1 %collective-permute-start.3 = (bf16[14,32,256]{2,1,0:T(8,128)(2,1)S(1)}, bf16[14,32,256]{2,1,0:T(8,128)(2,1)S(1)}, u32[]{:S(2)}, u32[]{:S(2)}) collective-permute-start(bf16[14,32,256]{2,1,0:T(8,128)(2,1)S(1)} %get-tuple-element.11), channel_id=1, source_target_pairs={{16,0},{32,16},{48,32},{64,48},{80,64},{96,80},{112,96},{128,112},... | collective-permute-start | bytes 688136 | tf_op jit(solution)/shard_map/ppermute | solution.py:23
  36.9 31.8 %all-to-all-start.1 = ((bf16[16,14,16,128]{3,2,1,0:T(8,128)(2,1)}), bf16[16,14,16,128]{3,2,1,0:T(8,128)(2,1)}, u32[]{:S(2)}, u32[]{:S(2)}) async-start(bf16[16,14,16,128]{3,2,1,0:T(8,128)(2,1)} %copy.44), calls=%async_computation.1 | async-start | bytes 1835008 | tf_op jit(solution)/shard_map/all_to_all | solution.py:95
  44.5 23.6 %collective-permute-start = (f32[32,16,64]{2,1,0:T(8,128)S(1)}, f32[32,16,64]{2,1,0:T(8,128)S(1)}, u32[]{:S(2)}, u32[]{:S(2)}) collective-permute-start(f32[32,16,64]{2,1,0:T(8,128)S(1)} %get-tuple-element.14), channel_id=1, source_target_pairs={{0,16},{16,32},{32,48},{48,64},{64,80},{80,96},{96,112},{112,128},... | collective-permute-start | bytes 393224 | tf_op jit(solution)/shard_map/ppermute | solution.py:100
  50.2 17.9 %collective-permute-start.1 = (f32[32,16,64]{2,1,0:T(8,128)S(1)}, f32[32,16,64]{2,1,0:T(8,128)S(1)}, u32[]{:S(2)}, u32[]{:S(2)}) collective-permute-start(f32[32,16,64]{2,1,0:T(8,128)S(1)} %get-tuple-element.15), channel_id=1, source_target_pairs={{16,0},{32,16},{48,32},{64,48},{80,64},{96,80},{112,96},{128,112},... | collective-permute-start | bytes 393224 | tf_op jit(solution)/shard_map/ppermute | solution.py:105
  72.3 7.5 %copy-start.6 = (bf16[8,224]{1,0:T(8,128)(2,1)S(1)}, bf16[8,224]{1,0:T(8,128)(2,1)}, u32[]{:S(2)}) copy-start(bf16[8,224]{1,0:T(8,128)(2,1)} %param.7) | copy-start | bytes 10756
  74.2 13.5 %all-to-all-start.2 = ((bf16[16,2,4096]{2,1,0:T(2,128)(2,1)}), bf16[16,2,4096]{2,1,0:T(2,128)(2,1)S(1)}, u32[]{:S(2)}, u32[]{:S(2)}) async-start(bf16[16,2,4096]{2,1,0:T(2,128)(2,1)} %reshape.103), calls=%async_computation.2 | async-start | bytes 524288 | tf_op jit(solution)/shard_map/all_to_all | solution.py:119
  80.2 12.1 %copy-start.2 = (bf16[32,16,1024]{2,1,0:T(8,128)(2,1)S(1)}, bf16[32,16,1024]{2,1,0:T(8,128)(2,1)}, u32[]{:S(2)}) copy-start(bf16[32,16,1024]{2,1,0:T(8,128)(2,1)} %param.5) | copy-start | bytes 3145732
  80.2 12.1 %copy-start.5 = (bf16[8,16,1024]{2,1,0:T(8,128)(2,1)S(1)}, bf16[8,16,1024]{2,1,0:T(8,128)(2,1)}, u32[]{:S(2)}) copy-start(bf16[8,16,1024]{2,1,0:T(8,128)(2,1)} %param.9) | copy-start | bytes 786436
  87.8 14.4 %all-to-all-start.3 = ((bf16[16,2,7168]{2,1,0:T(2,128)(2,1)}), bf16[16,2,7168]{2,1,0:T(2,128)(2,1)}, u32[]{:S(2)}, u32[]{:S(2)}) async-start(bf16[16,2,7168]{2,1,0:T(2,128)(2,1)} %reshape.105), calls=%async_computation.3 | async-start | bytes 917504 | tf_op jit(solution)/shard_map/all_to_all | solution.py:125

commit v8 on v6

--- a/solution.py
+++ b/solution.py
@@ -70,18 +70,6 @@
     return high_wide.astype(jnp.bfloat16), (wide - high_wide).astype(jnp.bfloat16)
 
 
-def packed_swap(parts, axis):
-    count = parts[0].shape[0]
-    flat = jnp.concatenate([p.reshape(count, -1) for p in parts], axis=1)
-    got = lax.all_to_all(flat, axis, split_axis=0, concat_axis=0, tiled=True)
-    out, at = [], 0
-    for p in parts:
-        size = p.size // count
-        out.append(got[:, at : at + size].reshape(p.shape))
-        at += size
-    return out
-
-
 def shards(latent, basis, response, hyper_obs, multi_obs):
     highest = lax.Precision.HIGHEST
     f32 = jnp.float32
@@ -95,7 +83,6 @@
     subspace, rows_here, width_cols = latent.shape
     chunk = coarse_cols // n_spec
     wide_rows = coarse_rows + 2 * rim
-    half = wide_rows // 2
     basis_wide = basis.astype(f32)
     column_t = banded(coarse_cols, width_cols, DECIM, 0)
     own_rows = banded(wide_rows, rows_dev, DECIM, HALO)
@@ -106,12 +93,13 @@
         column_t.reshape(n_spec, chunk, width_cols),
         preferred_element_type=f32,
     ).astype(bf16)
+    tile_rows = lax.all_to_all(cols_done, "spec", split_axis=0, concat_axis=3, tiled=True)[0]
+
     obs_split = hyper_obs.reshape(group, coarse_rows, n_spec, chunk).transpose(2, 0, 3, 1)
-    rows_got, obs_got = packed_swap((cols_done, obs_split), "spec")
-    tile_rows = rows_got.transpose(1, 2, 0, 3).reshape(subspace, chunk, rows_dev)
-    obs_cols = obs_got.reshape(group * n_spec, chunk, coarse_rows)
+    obs_cols = lax.all_to_all(obs_split, "spec", split_axis=0, concat_axis=1, tiled=True)[0]
 
     own_part = jnp.einsum("qjr,er->qje", tile_rows, own_rows, preferred_element_type=f32)
+    half = wide_rows // 2
     ends = n_tile - 1
 
     def payload(part, obs_rim):
@@ -141,13 +129,15 @@
 
     coef_resid = jnp.einsum("bq,bji->qji", basis, resid_wide, preferred_element_type=f32)
     rows_back = split_dot("qjk,kr->qjr", coef_resid, own_rows).astype(bf16)
-    back_split = rows_back.reshape(subspace, chunk, n_spec, rows_here).transpose(2, 0, 1, 3)
+    back_split = rows_back.reshape(subspace, chunk, n_spec, rows_here).transpose(2, 0, 3, 1)
+    rows_pixel = lax.all_to_all(back_split, "spec", split_axis=0, concat_axis=3, tiled=True)[0]
+    grad_hs = jnp.einsum("qrj,jc->qrc", rows_pixel, column_t, preferred_element_type=f32)
+
     resid_cols = lax.slice_in_dim(resid_wide, rim, rim + coarse_rows, axis=2)
     resid_split = resid_cols.reshape(n_spec, group, chunk, coarse_rows)
-    back_got, resid_got = packed_swap((back_split, resid_split), "spec")
-    rows_pixel = back_got.transpose(1, 3, 0, 2).reshape(subspace, rows_here, coarse_cols)
-    hs_residual = resid_got.transpose(1, 3, 0, 2).reshape(group, coarse_rows, coarse_cols)
-    grad_hs = jnp.einsum("qrj,jc->qrc", rows_pixel, column_t, preferred_element_type=f32)
+    resid_split, _ = lax.optimization_barrier((resid_split, rows_pixel))
+    resid_bands = lax.all_to_all(resid_split, "spec", split_axis=0, concat_axis=2, tiled=True)[0]
+    hs_residual = resid_bands.transpose(0, 2, 1)
 
     resp_basis = jnp.dot(response.astype(f32), basis_wide, precision=highest)
     multi_pred = jnp.einsum("mq,qrc->mrc", resp_basis, latent.astype(f32), precision=highest)

time: 128 us -> 116 us (0.906); the launches traced: 127 us -> 113 us
  local copies, waits for them, and re-layouts: 51.6 us -> 38.4 us
  starting transfers between devices: 19.3 us -> 26.9 us
  waiting for transfers between devices: 36.9 us -> 32.1 us
  matrix products: 11.7 us -> 10 us
  other arithmetic: 5.81 us -> 4.36 us
    reshape x7 -> x0, local copies, waits for them, and re-layouts: 14.6 us -> none  [the longest x3 7.91 us: packed_swap(): flat = jnp.concatenate([p.reshape(count, -1) for p in parts], axis=1)]
    all_to_all x2 -> x4, starting transfers between devices: 9.63 us -> 17.3 us  [the longest x1 5.76 us: shards(): lax.all_to_all(cols_done, 'spec', split_axis=0, concat_axis=3, tiled=True)]
    transpose x4 -> x1, local copies, waits for them, and re-layouts: 8.57 us -> 1.25 us  [shards(): rows_back.reshape(subspace, chunk, n_spec, rows_here).transpose(2, 0, 3, 1)]
    unnamed x40 -> x34, local copies, waits for them, and re-layouts: 9.62 us -> 16.2 us
    all_to_all x2 -> x4, waiting for transfers between devices: 20.4 us -> 16.7 us  [the longest x1 5.9 us: shards(): lax.all_to_all(back_split, 'spec', split_axis=0, concat_axis=3, tiled=True)]
    squeeze x0 -> x3, local copies, waits for them, and re-layouts: none -> 3.72 us  [the longest x1 2.4 us: shards(): lax.all_to_all(back_split, 'spec', split_axis=0, concat_axis=3, tiled=True)]
    all_to_all x4 -> x0, other arithmetic: 2.64 us -> none  [packed_swap(): got = lax.all_to_all(flat, axis, split_axis=0, concat_axis=0, tiled=True)]
    convert_element_type x5 -> x0, local copies, waits for them, and re-layouts: 2.52 us -> none  [the longest x1 2.3 us: shards(): cols_done = jnp.einsum('qrc,sjc->sqjr', latent, column_t.reshape(n_spec,...]
  transfers between devices with their start and end apart: 4 -> 6, of which waited for: 4 -> 5; matrix products, arithmetic and copies ran while one was open for 5% -> 19% of each run, Pallas kernels for 0% -> 0%
where the time goes in v8:
time: 116 us; the launch traced here: 113 us
  local copies, waits for them, and re-layouts  38.4 us (33%)
  waiting for transfers between devices  32.1 us (28%)
  starting transfers between devices  26.9 us (23%)
  matrix products  10 us (9%)
  other arithmetic  4.36 us (4%)
  between operations  1.8 us (2%)
    unnamed x34, local copies, waits for them, and re-layouts  16.2 us
    ppermute x1, waiting for transfers between devices, shards(): lax.ppermute(to_prev, 'tile', [(i + 1, i) for i in range(ends)])  10.5 us
    all_to_all x1, waiting for transfers between devices, shards(): lax.all_to_all(back_split, 'spec', split_axis=0, concat_axis=3, tiled=True)  5.9 us
    all_to_all x1, starting transfers between devices, shards(): lax.all_to_all(cols_done, 'spec', split_axis=0, concat_axis=3, tiled=True)  5.76 us
    all_to_all x1, waiting for transfers between devices, shards(): lax.all_to_all(obs_split, 'spec', split_axis=0, concat_axis=1, tiled=True)  5.63 us
    ppermute x1, starting transfers between devices, shards(): lax.ppermute(to_next, 'tile', [(i, i + 1) for i in range(ends)])  5.17 us
    all_to_all x1, waiting for transfers between devices, shards(): lax.all_to_all(cols_done, 'spec', split_axis=0, concat_axis=3, tiled=True)  5.15 us
    ppermute x1, waiting for transfers between devices, shards(): lax.ppermute(to_next, 'tile', [(i, i + 1) for i in range(ends)])  4.84 us
  transfers between devices with their start and end apart: 6, of which 5 were waited for; matrix products, arithmetic and copies ran while one was open for 19% of the time, Pallas kernels for 0%

profile of v8, /device:TPU:24, one launch (start us, length us, event | category | flops | bytes accessed | tf_op | source)
XLA Modules:
  0.0 113.5 jit_solution(15872320496407077642)
XLA Ops:
  2.6 1.7 %reshape.166 = bf16[256,2044]{1,0:T(8,128)(2,1)S(1)} reshape(bf16[523264]{0:T(1024)(128)(2,1)S(1)} %slice.108) | data formatting | bytes 2093056 | tf_op jit(solution)/shard_map/reshape | solution.py:55
  5.8 1.7 %reshape.186 = bf16[16,2,4096]{2,1,0:T(2,128)(2,1)} reshape(bf16[16,16,16,32]{3,2,1,0:T(8,128)(2,1)S(1)} %fusion.49) | data formatting | bytes 524288
  7.4 5.8 %all-to-all-start = ((bf16[16,2,4096]{2,1,0:T(2,128)(2,1)}), bf16[16,2,4096]{2,1,0:T(2,128)(2,1)S(1)}, u32[]{:S(2)}, u32[]{:S(2)}) async-start(bf16[16,2,4096]{2,1,0:T(2,128)(2,1)} %reshape.186), calls=%async_computation | async-start | bytes 524288 | tf_op jit(solution)/shard_map/all_to_all | solution.py:96
  16.1 5.2 %all-to-all-done = bf16[16,2,4096]{2,1,0:T(2,128)(2,1)S(1)} async-done(((bf16[16,2,4096]{2,1,0:T(2,128)(2,1)}), bf16[16,2,4096]{2,1,0:T(2,128)(2,1)S(1)}, u32[]{:S(2)}, u32[]{:S(2)}) %all-to-all-start) | async-done | bytes 262176 | tf_op jit(solution)/shard_map/all_to_all | solution.py:96
  21.3 3.6 %all-to-all-start.1 = ((bf16[16,2,7168]{2,1,0:T(2,128)(2,1)}), bf16[16,2,7168]{2,1,0:T(2,128)(2,1)S(1)}, u32[]{:S(2)}, u32[]{:S(2)}) async-start(bf16[16,2,7168]{2,1,0:T(2,128)(2,1)} %reshape.188), calls=%async_computation.1 | async-start | bytes 917504 | tf_op jit(solution)/shard_map/all_to_all | solution.py:99
  29.3 5.6 %all-to-all-done.1 = bf16[16,2,7168]{2,1,0:T(2,128)(2,1)S(1)} async-done(((bf16[16,2,7168]{2,1,0:T(2,128)(2,1)}), bf16[16,2,7168]{2,1,0:T(2,128)(2,1)S(1)}, u32[]{:S(2)}, u32[]{:S(2)}) %all-to-all-start.1) | async-done | bytes 458784 | tf_op jit(solution)/shard_map/all_to_all | solution.py:99
  36.8 1.9 %reshape.172 = bf16[114688]{0:T(1024)(128)(2,1)S(1)} reshape(bf16[224,16,32]{2,1,0:T(8,128)(2,1)} %get-tuple-element.8) | data formatting | bytes 458752 | tf_op jit(solution)/shard_map/reshape | solution.py:107
  38.7 1.6 %pad_maximum_fusion = bf16[180224]{0:T(1024)(128)(2,1)} fusion(bf16[114688]{0:T(1024)(128)(2,1)S(1)} %reshape.172, bf16[32768]{0:T(1024)(128)(2,1)} %reshape.170, bf16[32768]{0:T(1024)(128)(2,1)} %reshape.169), kind=kLoop, calls=%fused_computation.28 | loop fusion | flops 1081344 | bytes 720896 | tf_op jit(solution)/shard_map/concatenate | solution.py:107
  40.3 5.2 %collective-permute-start = (bf16[180224]{0:T(1024)(128)(2,1)}, bf16[180224]{0:T(1024)(128)(2,1)}, u32[]{:S(2)}, u32[]{:S(2)}) collective-permute-start(bf16[180224]{0:T(1024)(128)(2,1)} %pad_maximum_fusion), channel_id=1, source_target_pairs={{0,16},{16,32},{32,48},{48,64},{64,80},{80,96},{96,112},{112,128},... | collective-permute-start | bytes 1081352 | tf_op jit(solution)/shard_map/ppermute | solution.py:121
  47.0 4.4 %collective-permute-start.1 = (bf16[180224]{0:T(1024)(128)(2,1)}, bf16[180224]{0:T(1024)(128)(2,1)S(1)}, u32[]{:S(2)}, u32[]{:S(2)}) collective-permute-start(bf16[180224]{0:T(1024)(128)(2,1)} %pad_maximum_fusion.1), channel_id=1, source_target_pairs={{16,0},{32,16},{48,32},{64,48},{80,64},{96,80},{112,96},{128,112},... | collective-permute-start | bytes 1081352 | tf_op jit(solution)/shard_map/ppermute | solution.py:122
  51.4 4.8 %collective-permute-done = bf16[180224]{0:T(1024)(128)(2,1)} collective-permute-done((bf16[180224]{0:T(1024)(128)(2,1)}, bf16[180224]{0:T(1024)(128)(2,1)}, u32[]{:S(2)}, u32[]{:S(2)}) %collective-permute-start) | collective-permute-done | bytes 360480 | tf_op jit(solution)/shard_map/ppermute | solution.py:121
  57.2 10.5 %collective-permute-done.1 = bf16[180224]{0:T(1024)(128)(2,1)S(1)} collective-permute-done((bf16[180224]{0:T(1024)(128)(2,1)}, bf16[180224]{0:T(1024)(128)(2,1)S(1)}, u32[]{:S(2)}, u32[]{:S(2)}) %collective-permute-start.1) | collective-permute-done | bytes 360480 | tf_op jit(solution)/shard_map/ppermute | solution.py:122
  68.6 1.6 %slice.120 = bf16[114688]{0:T(1024)(128)(2,1)} slice(bf16[180224]{0:T(1024)(128)(2,1)} %collective-permute-done), slice={[65536:180224]} | slice | bytes 458752 | tf_op jit(solution)/shard_map/slice | solution.py:112
  70.2 1.6 %reshape.176 = bf16[224,16,32]{2,1,0:T(8,128)(2,1)S(1)} reshape(bf16[114688]{0:T(1024)(128)(2,1)} %slice.120) | data formatting | bytes 458752 | tf_op jit(solution)/shard_map/reshape | solution.py:112
  73.7 1.6 %reshape.177 = bf16[224,16,32]{2,1,0:T(8,128)(2,1)S(1)} reshape(bf16[114688]{0:T(1024)(128)(2,1)} %slice.121) | data formatting | bytes 458752 | tf_op jit(solution)/shard_map/reshape | solution.py:112
  81.1 3.1 %reshape.190 = bf16[16,2,4096]{2,1,0:T(2,128)(2,1)} reshape(bf16[16,16,16,32]{3,2,1,0:T(8,128)(2,1)} %bitcast.91) | data formatting | bytes 524288
  84.1 3.5 %all-to-all-start.2 = ((bf16[16,2,4096]{2,1,0:T(2,128)(2,1)}), bf16[16,2,4096]{2,1,0:T(2,128)(2,1)S(1)}, u32[]{:S(2)}, u32[]{:S(2)}) async-start(bf16[16,2,4096]{2,1,0:T(2,128)(2,1)} %reshape.190), calls=%async_computation.2 | async-start | bytes 524288 | tf_op jit(solution)/shard_map/all_to_all | solution.py:133
  89.8 5.9 %all-to-all-done.2 = bf16[16,2,4096]{2,1,0:T(2,128)(2,1)S(1)} async-done(((bf16[16,2,4096]{2,1,0:T(2,128)(2,1)}), bf16[16,2,4096]{2,1,0:T(2,128)(2,1)S(1)}, u32[]{:S(2)}, u32[]{:S(2)}) %all-to-all-start.2) | async-done | bytes 262176 | tf_op jit(solution)/shard_map/all_to_all | solution.py:133
  95.7 4.4 %all-to-all-start.3 = ((bf16[16,2,7168]{2,1,0:T(2,128)(2,1)}), bf16[16,2,7168]{2,1,0:T(2,128)(2,1)}, u32[]{:S(2)}, u32[]{:S(2)}) async-start(bf16[16,2,7168]{2,1,0:T(2,128)(2,1)} %reshape.192), calls=%async_computation.3 | async-start | bytes 917504 | tf_op jit(solution)/shard_map/all_to_all | solution.py:139
  100.2 1.6 %fusion.7 = bf16[8,16,1024]{2,0,1:T(8,128)(2,1)S(1)} fusion(f32[8,32,1]{1,0,2:T(8,128)S(1)} %convolution_bitcast_fusion.1, bf16[32,16,1024]{2,1,0:T(8,128)(2,1)S(1)} %copy-done.1, bf16[8,16,1024]{2,1,0:T(8,128)(2,1)S(1)} %copy-done.9), kind=kOutput, calls=%fused_computation.12 | convolution fusion | flops 50724864 | bytes 1573888 | tf_op jit(solution)/shard_map/mq,qrc->mrc/dot_general | solution.py:143
  102.7 1.5 %reshape.191 = bf16[16,16,16,32]{3,2,1,0:T(8,128)(2,1)} reshape(bf16[16,2,4096]{2,1,0:T(2,128)(2,1)S(1)} %all-to-all-done.2) | data formatting | bytes 524288
  104.2 2.4 %copy.51 = bf16[32,16,256]{2,1,0:T(8,128)(2,1)S(1)} copy(bf16[32,16,256]{0,1,2:T(8,128)(2,1)} %bitcast.89) | data formatting | bytes 524288 | tf_op jit(solution)/shard_map/squeeze | solution.py:133
  106.6 3.4 %fusion.2 = bf16[32,16,1024]{2,1,0:T(8,128)(2,1)} fusion(f32[32,16,1024]{2,0,1:T(8,128)S(1)} %fusion.52, bf16[32,16,1024]{2,1,0:T(8,128)(2,1)S(1)} %copy-done.1, bf16[32,16,256]{2,1,0:T(8,128)(2,1)S(1)} %copy.51, bf16[256,2044]{1,0:T(8,128)(2,1)} %copy-done.2), kind=kOutput, calls=%fused_computation.3 | convolution fusion | flops 271056896 | bytes 4980736 | tf_op jit(solution)/shard_map/qrj,jc->qrc/dot_general | solution.py:134
  110.1 2.1 %reshape.193 = bf16[16,14,16,64]{3,2,1,0:T(8,128)(2,1)S(1)} reshape(bf16[16,2,7168]{2,1,0:T(2,128)(2,1)} %all-to-all-done.3) | data formatting | bytes 917504
  (73 shorter events, 27.1 us)
Async XLA Ops:
  0.6 75.8 %copy-start = (bf16[224,32]{0,1:T(8,128)(2,1)S(1)}, bf16[224,32]{0,1:T(8,128)(2,1)}, u32[]{:S(2)}) copy-start(bf16[224,32]{0,1:T(8,128)(2,1)} %param.6) | copy-start | bytes 43012
  2.6 1.7 %copy-start.1 = (bf16[32,16,1024]{2,1,0:T(8,128)(2,1)S(1)}, bf16[32,16,1024]{2,1,0:T(8,128)(2,1)}, u32[]{:S(2)}) copy-start(bf16[32,16,1024]{2,1,0:T(8,128)(2,1)} %param.5) | copy-start | bytes 3145732
  4.3 1.5 %copy-start.2 = (bf16[256,2044]{1,0:T(8,128)(2,1)}, bf16[256,2044]{1,0:T(8,128)(2,1)S(1)}, u32[]{:S(2)}) copy-start(bf16[256,2044]{1,0:T(8,128)(2,1)S(1)} %reshape.166) | copy-start | bytes 3139588
  7.4 13.8 %all-to-all-start = ((bf16[16,2,4096]{2,1,0:T(2,128)(2,1)}), bf16[16,2,4096]{2,1,0:T(2,128)(2,1)S(1)}, u32[]{:S(2)}, u32[]{:S(2)}) async-start(bf16[16,2,4096]{2,1,0:T(2,128)(2,1)} %reshape.186), calls=%async_computation | async-start | bytes 524288 | tf_op jit(solution)/shard_map/all_to_all | solution.py:96
  21.3 13.7 %all-to-all-start.1 = ((bf16[16,2,7168]{2,1,0:T(2,128)(2,1)}), bf16[16,2,7168]{2,1,0:T(2,128)(2,1)S(1)}, u32[]{:S(2)}, u32[]{:S(2)}) async-start(bf16[16,2,7168]{2,1,0:T(2,128)(2,1)} %reshape.188), calls=%async_computation.1 | async-start | bytes 917504 | tf_op jit(solution)/shard_map/all_to_all | solution.py:99
  25.6 2.0 %copy-start.5 = (bf16[128,764]{1,0:T(8,128)(2,1)}, bf16[128,764]{1,0:T(8,128)(2,1)S(1)}, u32[]{:S(2)}) copy-start(bf16[128,764]{1,0:T(8,128)(2,1)S(1)} %reshape.168) | copy-start | bytes 586756
  40.3 15.9 %collective-permute-start = (bf16[180224]{0:T(1024)(128)(2,1)}, bf16[180224]{0:T(1024)(128)(2,1)}, u32[]{:S(2)}, u32[]{:S(2)}) collective-permute-start(bf16[180224]{0:T(1024)(128)(2,1)} %pad_maximum_fusion), channel_id=1, source_target_pairs={{0,16},{16,32},{32,48},{48,64},{64,80},{80,96},{96,112},{112,128},... | collective-permute-start | bytes 1081352 | tf_op jit(solution)/shard_map/ppermute | solution.py:121
  47.0 20.8 %collective-permute-start.1 = (bf16[180224]{0:T(1024)(128)(2,1)}, bf16[180224]{0:T(1024)(128)(2,1)S(1)}, u32[]{:S(2)}, u32[]{:S(2)}) collective-permute-start(bf16[180224]{0:T(1024)(128)(2,1)} %pad_maximum_fusion.1), channel_id=1, source_target_pairs={{16,0},{32,16},{48,32},{64,48},{80,64},{96,80},{112,96},{128,112},... | collective-permute-start | bytes 1081352 | tf_op jit(solution)/shard_map/ppermute | solution.py:122
  67.7 0.8 copy-start.7
  71.8 1.2 %copy-start.8 = (bf16[180224]{0:T(1024)(128)(2,1)S(1)}, bf16[180224]{0:T(1024)(128)(2,1)}, u32[]{:S(2)}) copy-start(bf16[180224]{0:T(1024)(128)(2,1)} %copy-done.7) | copy-start | bytes 1081348
  75.3 1.0 copy-start.4
  76.2 1.2 %copy-start.3 = (bf16[224,16,32]{2,0,1:T(8,128)(2,1)S(1)}, bf16[224,16,32]{2,0,1:T(8,128)(2,1)}, u32[]{:S(2)}) copy-start(bf16[224,16,32]{2,0,1:T(8,128)(2,1)} %copy.43) | copy-start | bytes 688132
  77.4 1.4 %copy-start.6 = (bf16[128,764]{1,0:T(8,128)(2,1)S(1)}, bf16[128,764]{1,0:T(8,128)(2,1)}, u32[]{:S(2)}) copy-start(bf16[128,764]{1,0:T(8,128)(2,1)} %copy-done.5) | copy-start | bytes 586756
  79.8 7.9 %copy-start.10 = (bf16[8,224]{1,0:T(8,128)(2,1)S(1)}, bf16[8,224]{1,0:T(8,128)(2,1)}, u32[]{:S(2)}) copy-start(bf16[8,224]{1,0:T(8,128)(2,1)} %param.7) | copy-start | bytes 10756
  84.1 11.6 %all-to-all-start.2 = ((bf16[16,2,4096]{2,1,0:T(2,128)(2,1)}), bf16[16,2,4096]{2,1,0:T(2,128)(2,1)S(1)}, u32[]{:S(2)}, u32[]{:S(2)}) async-start(bf16[16,2,4096]{2,1,0:T(2,128)(2,1)} %reshape.190), calls=%async_computation.2 | async-start | bytes 524288 | tf_op jit(solution)/shard_map/all_to_all | solution.py:133
  88.1 12.0 %copy-start.9 = (bf16[8,16,1024]{2,1,0:T(8,128)(2,1)S(1)}, bf16[8,16,1024]{2,1,0:T(8,128)(2,1)}, u32[]{:S(2)}) copy-start(bf16[8,16,1024]{2,1,0:T(8,128)(2,1)} %param.9) | copy-start | bytes 786436
  95.7 14.4 %all-to-all-start.3 = ((bf16[16,2,7168]{2,1,0:T(2,128)(2,1)}), bf16[16,2,7168]{2,1,0:T(2,128)(2,1)}, u32[]{:S(2)}, u32[]{:S(2)}) async-start(bf16[16,2,7168]{2,1,0:T(2,128)(2,1)} %reshape.192), calls=%async_computation.3 | async-start | bytes 917504 | tf_op jit(solution)/shard_map/all_to_all | solution.py:139

commit v9 on v7

--- a/solution.py
+++ b/solution.py
@@ -90,40 +90,40 @@
     ).astype(bf16)
     tile_rows = lax.all_to_all(cols_done, "spec", split_axis=0, concat_axis=3, tiled=True)[0]
 
-    obs_wide_bands = with_halo(hyper_obs, (("tile", 1),), rim)
-    obs_split = obs_wide_bands.reshape(group, wide_rows, n_spec, chunk).transpose(2, 0, 3, 1)
-    obs_wide = lax.all_to_all(obs_split, "spec", split_axis=0, concat_axis=1, tiled=True)[0]
+    own_part = jnp.einsum("qjr,er->qje", tile_rows, own_rows, preferred_element_type=f32)
+    ends = n_tile - 1
+    to_next = lax.slice_in_dim(own_part, wide_rows - rim, wide_rows, axis=2)
+    to_prev = lax.slice_in_dim(own_part, 0, rim, axis=2)
 
-    own_part = jnp.einsum("qjr,er->qje", tile_rows, own_rows, preferred_element_type=f32)
-    half = wide_rows // 2
-    ends = n_tile - 1
-    from_prev = lax.ppermute(
-        lax.slice_in_dim(own_part, half, wide_rows, axis=2),
+    obs_split = hyper_obs.reshape(group, coarse_rows, n_spec, chunk).transpose(2, 0, 3, 1)
+    obs_split, to_next, to_prev = lax.optimization_barrier((obs_split, to_next, to_prev))
+    part_prev = lax.ppermute(to_next, "tile", [(i, i + 1) for i in range(ends)])
+    part_next = lax.ppermute(to_prev, "tile", [(i + 1, i) for i in range(ends)])
+    obs_cols = lax.all_to_all(obs_split, "spec", split_axis=0, concat_axis=1, tiled=True)[0]
+    coef_blurred = lax.slice_in_dim(own_part, rim, rim + coarse_rows, axis=2) + jnp.concatenate(
+        [part_prev, part_next], axis=2
+    )
+    blurred = split_dot("qji,bq->bji", coef_blurred, basis)
+    resid_cols = (blurred - obs_cols.astype(f32)).astype(bf16)
+
+    resid_split = resid_cols.reshape(n_spec, group, chunk, coarse_rows)
+    resid_bands = lax.all_to_all(resid_split, "spec", split_axis=0, concat_axis=2, tiled=True)[0]
+    hs_residual = resid_bands.transpose(0, 2, 1)
+
+    coef_resid = jnp.einsum("bq,bji->qji", basis, resid_cols, preferred_element_type=f32)
+    rim_prev = lax.ppermute(
+        lax.slice_in_dim(coef_resid, coarse_rows - rim, coarse_rows, axis=2),
         "tile",
         [(i, i + 1) for i in range(ends)],
     )
-    from_next = lax.ppermute(
-        lax.slice_in_dim(own_part, 0, half, axis=2),
-        "tile",
-        [(i + 1, i) for i in range(ends)],
+    rim_next = lax.ppermute(
+        lax.slice_in_dim(coef_resid, 0, rim, axis=2), "tile", [(i + 1, i) for i in range(ends)]
     )
-    coef_blurred = own_part + jnp.concatenate([from_prev, from_next], axis=2)
-    blurred = split_dot("qji,bq->bji", coef_blurred, basis)
-    coarse_at = jnp.arange(wide_rows) + tile_index * coarse_rows - rim
-    inside = (coarse_at >= 0) & (coarse_at < n_tile * coarse_rows)
-    resid_wide = jnp.where(inside, blurred - obs_wide.astype(f32), 0.0).astype(bf16)
-
-    coef_resid = jnp.einsum("bq,bji->qji", basis, resid_wide, preferred_element_type=f32)
-    rows_back = split_dot("qjk,kr->qjr", coef_resid, own_rows).astype(bf16)
+    coef_wide = jnp.concatenate([rim_prev, coef_resid, rim_next], axis=2)
+    rows_back = split_dot("qjk,kr->qjr", coef_wide, own_rows).astype(bf16)
     back_split = rows_back.reshape(subspace, chunk, n_spec, rows_here).transpose(2, 0, 3, 1)
     rows_pixel = lax.all_to_all(back_split, "spec", split_axis=0, concat_axis=3, tiled=True)[0]
     grad_hs = jnp.einsum("qrj,jc->qrc", rows_pixel, column_t, preferred_element_type=f32)
-
-    resid_cols = lax.slice_in_dim(resid_wide, rim, rim + coarse_rows, axis=2)
-    resid_split = resid_cols.reshape(n_spec, group, chunk, coarse_rows)
-    resid_split, _ = lax.optimization_barrier((resid_split, rows_pixel))
-    resid_bands = lax.all_to_all(resid_split, "spec", split_axis=0, concat_axis=2, tiled=True)[0]
-    hs_residual = resid_bands.transpose(0, 2, 1)
 
     resp_basis = jnp.dot(response.astype(f32), basis_wide, precision=highest)
     multi_pred = jnp.einsum("mq,qrc->mrc", resp_basis, latent.astype(f32), precision=highest)

time: 107 us -> 120 us (1.12)
  local copies, waits for them, and re-layouts: 20.4 us -> 29.3 us
  waiting for transfers between devices: 31.4 us -> 36.3 us
  matrix products: 9.9 us -> 11.7 us
  starting transfers between devices: 39 us -> 37.4 us
    unnamed x24 -> x22, local copies, waits for them, and re-layouts: 10.7 us -> 17.4 us
    all_to_all x1, waiting for transfers between devices: 0.01 us -> 5.85 us  [shards(): lax.all_to_all(cols_done, 'spec', split_axis=0, concat_axis=3, tiled=True)]
    convert_element_type x1 -> x3, local copies, waits for them, and re-layouts: 0.51 us -> 3.15 us  [the longest x2 2.64 us: shards(): resid_cols = (blurred - obs_cols.astype(f32)).astype(bf16)]
    all_to_all x1, starting transfers between devices: 4.88 us -> 3.56 us  [shards(): lax.all_to_all(obs_split, 'spec', split_axis=0, concat_axis=1, tiled=True)]
  transfers between devices with their start and end apart: 8 -> 8, of which waited for: 4 -> 6; matrix products, arithmetic and copies ran while one was open for 17% -> 13% of each run, Pallas kernels for 0% -> 0%
where the time goes in v9:
time: 120 us; the launch traced here: 119 us
  starting transfers between devices  37.4 us (31%)
  waiting for transfers between devices  36.3 us (30%)
  local copies, waits for them, and re-layouts  29.3 us (24%)
  matrix products  11.7 us (10%)
  other arithmetic  2.49 us (2%)
  between operations  1.67 us (1%)
    unnamed x22, local copies, waits for them, and re-layouts  17.4 us
    ppermute x1, waiting for transfers between devices, shards(): part_prev = lax.ppermute(to_next, 'tile', [(i, i + 1) for i in range(ends)])  13.6 us
    ppermute x1, waiting for transfers between devices, shards(): lax.ppermute(lax.slice_in_dim(coef_resid, coarse_rows - rim, coarse_rows,...  9.53 us
    all_to_all x1, waiting for transfers between devices, shards(): lax.all_to_all(back_split, 'spec', split_axis=0, concat_axis=3, tiled=True)  5.85 us
    all_to_all x1, waiting for transfers between devices, shards(): lax.all_to_all(cols_done, 'spec', split_axis=0, concat_axis=3, tiled=True)  5.85 us
    all_to_all x1, starting transfers between devices, shards(): lax.all_to_all(cols_done, 'spec', split_axis=0, concat_axis=3, tiled=True)  5.76 us
    ppermute x1, starting transfers between devices, shards(): lax.ppermute(lax.slice_in_dim(coef_resid, coarse_rows - rim, coarse_rows,...  5.47 us
    all_to_all x1, starting transfers between devices, shards(): lax.all_to_all(back_split, 'spec', split_axis=0, concat_axis=3, tiled=True)  5.41 us
  transfers between devices with their start and end apart: 8, of which 6 were waited for; matrix products, arithmetic and copies ran while one was open for 13% of the time, Pallas kernels for 0%

profile of v9, /device:TPU:24, one launch (start us, length us, event | category | flops | bytes accessed | tf_op | source)
XLA Modules:
  0.0 118.9 jit_solution(5251975621357832353)
XLA Ops:
  2.6 1.7 %reshape.88 = bf16[256,2044]{1,0:T(8,128)(2,1)S(1)} reshape(bf16[523264]{0:T(1024)(128)(2,1)S(1)} %slice.36) | data formatting | bytes 2093056 | tf_op jit(solution)/shard_map/reshape | solution.py:55
  5.8 1.7 %reshape.101 = bf16[16,2,4096]{2,1,0:T(2,128)(2,1)} reshape(bf16[16,16,16,32]{3,2,1,0:T(8,128)(2,1)S(1)} %fusion.46) | data formatting | bytes 524288
  7.4 5.8 %all-to-all-start = ((bf16[16,2,4096]{2,1,0:T(2,128)(2,1)}), bf16[16,2,4096]{2,1,0:T(2,128)(2,1)S(1)}, u32[]{:S(2)}, u32[]{:S(2)}) async-start(bf16[16,2,4096]{2,1,0:T(2,128)(2,1)} %reshape.101), calls=%async_computation | async-start | bytes 524288 | tf_op jit(solution)/shard_map/all_to_all | solution.py:91
  15.4 5.9 %all-to-all-done = bf16[16,2,4096]{2,1,0:T(2,128)(2,1)S(1)} async-done(((bf16[16,2,4096]{2,1,0:T(2,128)(2,1)}), bf16[16,2,4096]{2,1,0:T(2,128)(2,1)S(1)}, u32[]{:S(2)}, u32[]{:S(2)}) %all-to-all-start) | async-done | bytes 262176 | tf_op jit(solution)/shard_map/all_to_all | solution.py:91
  24.3 2.8 %reshape.103 = bf16[16,2,7168]{2,1,0:T(2,128)(2,1)} reshape(bf16[16,14,16,64]{3,2,1,0:T(8,128)(2,1)} %copy.40) | data formatting | bytes 917504
  27.1 3.6 %all-to-all-start.1 = ((bf16[16,2,7168]{2,1,0:T(2,128)(2,1)}), bf16[16,2,7168]{2,1,0:T(2,128)(2,1)S(1)}, u32[]{:S(2)}, u32[]{:S(2)}) async-start(bf16[16,2,7168]{2,1,0:T(2,128)(2,1)} %reshape.103), calls=%async_computation.1 | async-start | bytes 917504 | tf_op jit(solution)/shard_map/all_to_all | solution.py:102
  30.7 5.2 %collective-permute-start = (f32[32,16,32]{2,1,0:T(8,128)S(1)}, f32[32,16,32]{2,1,0:T(8,128)S(1)}, u32[]{:S(2)}, u32[]{:S(2)}) collective-permute-start(f32[32,16,32]{2,1,0:T(8,128)S(1)} %get-tuple-element.5), channel_id=1, source_target_pairs={{0,16},{16,32},{32,48},{48,64},{64,80},{80,96},{96,112},{112,128},... | collective-permute-start | bytes 196616 | tf_op jit(solution)/shard_map/ppermute | solution.py:100
  35.9 4.2 %collective-permute-start.1 = (f32[32,16,32]{2,1,0:T(8,128)S(1)}, f32[32,16,32]{2,1,0:T(8,128)S(1)}, u32[]{:S(2)}, u32[]{:S(2)}) collective-permute-start(f32[32,16,32]{2,1,0:T(8,128)S(1)} %get-tuple-element.6), channel_id=1, source_target_pairs={{16,0},{32,16},{48,32},{64,48},{80,64},{96,80},{112,96},{128,112},... | collective-permute-start | bytes 196616 | tf_op jit(solution)/shard_map/ppermute | solution.py:101
  40.1 13.6 %collective-permute-done = f32[32,16,32]{2,1,0:T(8,128)S(1)} collective-permute-done((f32[32,16,32]{2,1,0:T(8,128)S(1)}, f32[32,16,32]{2,1,0:T(8,128)S(1)}, u32[]{:S(2)}, u32[]{:S(2)}) %collective-permute-start) | collective-permute-done | bytes 65568 | tf_op jit(solution)/shard_map/ppermute | solution.py:100
  55.4 1.5 %reshape.104 = bf16[16,14,16,64]{3,2,1,0:T(8,128)(2,1)} reshape(bf16[16,2,7168]{2,1,0:T(2,128)(2,1)S(1)} %all-to-all-done.1) | data formatting | bytes 917504
  58.1 1.9 %copy.41 = f32[224,16,64]{0,2,1:T(8,128)} copy(f32[224,16,64]{2,1,0:T(8,128)S(1)} %bitcast_convert_fusion) | data formatting | bytes 1835008 | tf_op jit(solution)/shard_map/convert_element_type | solution.py:107
  60.0 1.9 %fusion.6 = bf16[224,16,64]{0,2,1:T(8,128)(2,1)S(1)} fusion(f32[224,16,64]{0,2,1:T(8,128)} %copy.41, f32[16,64,224]{2,1,0:T(8,128)} %fusion.19, bf16[32,16,64]{2,1,0:T(8,128)(2,1)S(1)} %get-tuple-element.14, bf16[224,32]{0,1:T(8,128)(2,1)S(1)} %copy-done), kind=kOutput, calls=%fused_computation.9 | convolution fusion | flops 15368192 | bytes 2373632 | tf_op jit(solution)/shard_map/qji,bq->bji/dot_general | solution.py:63
  62.4 5.5 %collective-permute-start.2 = (f32[32,16,32]{2,0,1:T(8,128)S(1)}, f32[32,16,32]{2,0,1:T(8,128)S(1)}, u32[]{:S(2)}, u32[]{:S(2)}) collective-permute-start(f32[32,16,32]{2,0,1:T(8,128)S(1)} %get-tuple-element.16), channel_id=1, source_target_pairs={{0,16},{16,32},{32,48},{48,64},{64,80},{80,96},{96,112},{112,128},... | collective-permute-start | bytes 196616 | tf_op jit(solution)/shard_map/ppermute | solution.py:114
  67.9 3.6 %collective-permute-start.3 = (f32[32,16,32]{2,0,1:T(8,128)S(1)}, f32[32,16,32]{2,0,1:T(8,128)S(1)}, u32[]{:S(2)}, u32[]{:S(2)}) collective-permute-start(f32[32,16,32]{2,0,1:T(8,128)S(1)} %get-tuple-element.17), channel_id=1, source_target_pairs={{16,0},{32,16},{48,32},{64,48},{80,64},{96,80},{112,96},{128,112},... | collective-permute-start | bytes 196616 | tf_op jit(solution)/shard_map/ppermute | solution.py:119
  71.4 9.5 %collective-permute-done.2 = f32[32,16,32]{2,0,1:T(8,128)S(1)} collective-permute-done((f32[32,16,32]{2,0,1:T(8,128)S(1)}, f32[32,16,32]{2,0,1:T(8,128)S(1)}, u32[]{:S(2)}, u32[]{:S(2)}) %collective-permute-start.2) | collective-permute-done | bytes 65568 | tf_op jit(solution)/shard_map/ppermute | solution.py:114
  84.5 3.1 %reshape.105 = bf16[16,2,4096]{2,1,0:T(2,128)(2,1)} reshape(bf16[16,16,16,32]{3,2,1,0:T(8,128)(2,1)} %bitcast.88) | data formatting | bytes 524288
  87.6 5.4 %all-to-all-start.2 = ((bf16[16,2,4096]{2,1,0:T(2,128)(2,1)}), bf16[16,2,4096]{2,1,0:T(2,128)(2,1)S(1)}, u32[]{:S(2)}, u32[]{:S(2)}) async-start(bf16[16,2,4096]{2,1,0:T(2,128)(2,1)} %reshape.105), calls=%async_computation.2 | async-start | bytes 524288 | tf_op jit(solution)/shard_map/all_to_all | solution.py:125
  95.2 5.9 %all-to-all-done.2 = bf16[16,2,4096]{2,1,0:T(2,128)(2,1)S(1)} async-done(((bf16[16,2,4096]{2,1,0:T(2,128)(2,1)}), bf16[16,2,4096]{2,1,0:T(2,128)(2,1)S(1)}, u32[]{:S(2)}, u32[]{:S(2)}) %all-to-all-start.2) | async-done | bytes 262176 | tf_op jit(solution)/shard_map/all_to_all | solution.py:125
  101.1 4.2 %all-to-all-start.3 = ((bf16[16,2,7168]{2,1,0:T(2,128)(2,1)}), bf16[16,2,7168]{2,1,0:T(2,128)(2,1)}, u32[]{:S(2)}, u32[]{:S(2)}) async-start(bf16[16,2,7168]{2,1,0:T(2,128)(2,1)} %reshape.107), calls=%async_computation.3 | async-start | bytes 917504 | tf_op jit(solution)/shard_map/all_to_all | solution.py:110
  105.3 1.6 %fusion.8 = bf16[8,16,1024]{2,0,1:T(8,128)(2,1)S(1)} fusion(f32[8,32,1]{1,0,2:T(8,128)S(1)} %convolution_bitcast_fusion.1, bf16[32,16,1024]{2,1,0:T(8,128)(2,1)S(1)} %copy-done.1, bf16[8,16,1024]{2,1,0:T(8,128)(2,1)S(1)} %copy-done.3), kind=kOutput, calls=%fused_computation.13 | convolution fusion | flops 50724864 | bytes 1573888 | tf_op jit(solution)/shard_map/mq,qrc->mrc/dot_general | solution.py:129
  107.9 1.5 %reshape.106 = bf16[16,16,16,32]{3,2,1,0:T(8,128)(2,1)} reshape(bf16[16,2,4096]{2,1,0:T(2,128)(2,1)S(1)} %all-to-all-done.2) | data formatting | bytes 524288
  109.4 2.4 %copy.47 = bf16[32,16,256]{2,1,0:T(8,128)(2,1)S(1)} copy(bf16[32,16,256]{0,1,2:T(8,128)(2,1)} %bitcast.86) | data formatting | bytes 524288 | tf_op jit(solution)/shard_map/squeeze | solution.py:125
  111.8 3.4 %fusion.2 = bf16[32,16,1024]{2,1,0:T(8,128)(2,1)} fusion(f32[32,16,1024]{2,0,1:T(8,128)S(1)} %fusion.49, bf16[32,16,1024]{2,1,0:T(8,128)(2,1)S(1)} %copy-done.1, bf16[32,16,256]{2,1,0:T(8,128)(2,1)S(1)} %copy.47, bf16[256,2044]{1,0:T(8,128)(2,1)} %copy-done.2), kind=kOutput, calls=%fused_computation.3 | convolution fusion | flops 271056896 | bytes 4980736 | tf_op jit(solution)/shard_map/qrj,jc->qrc/dot_general | solution.py:126
  115.5 2.1 %reshape.108 = bf16[16,14,16,64]{3,2,1,0:T(8,128)(2,1)S(1)} reshape(bf16[16,2,7168]{2,1,0:T(2,128)(2,1)} %all-to-all-done.3) | data formatting | bytes 917504
  (47 shorter events, 19.5 us)
Async XLA Ops:
  0.6 53.4 %copy-start = (bf16[224,32]{0,1:T(8,128)(2,1)S(1)}, bf16[224,32]{0,1:T(8,128)(2,1)}, u32[]{:S(2)}) copy-start(bf16[224,32]{0,1:T(8,128)(2,1)} %param.6) | copy-start | bytes 43012
  2.5 1.8 %copy-start.1 = (bf16[32,16,1024]{2,1,0:T(8,128)(2,1)S(1)}, bf16[32,16,1024]{2,1,0:T(8,128)(2,1)}, u32[]{:S(2)}) copy-start(bf16[32,16,1024]{2,1,0:T(8,128)(2,1)} %param.5) | copy-start | bytes 3145732
  4.3 1.5 %copy-start.2 = (bf16[256,2044]{1,0:T(8,128)(2,1)}, bf16[256,2044]{1,0:T(8,128)(2,1)S(1)}, u32[]{:S(2)}) copy-start(bf16[256,2044]{1,0:T(8,128)(2,1)S(1)} %reshape.88) | copy-start | bytes 3139588
  7.4 13.8 %all-to-all-start = ((bf16[16,2,4096]{2,1,0:T(2,128)(2,1)}), bf16[16,2,4096]{2,1,0:T(2,128)(2,1)S(1)}, u32[]{:S(2)}, u32[]{:S(2)}) async-start(bf16[16,2,4096]{2,1,0:T(2,128)(2,1)} %reshape.101), calls=%async_computation | async-start | bytes 524288 | tf_op jit(solution)/shard_map/all_to_all | solution.py:91
  27.1 28.2 %all-to-all-start.1 = ((bf16[16,2,7168]{2,1,0:T(2,128)(2,1)}), bf16[16,2,7168]{2,1,0:T(2,128)(2,1)S(1)}, u32[]{:S(2)}, u32[]{:S(2)}) async-start(bf16[16,2,7168]{2,1,0:T(2,128)(2,1)} %reshape.103), calls=%async_computation.1 | async-start | bytes 917504 | tf_op jit(solution)/shard_map/all_to_all | solution.py:102
  30.7 23.1 %collective-permute-start = (f32[32,16,32]{2,1,0:T(8,128)S(1)}, f32[32,16,32]{2,1,0:T(8,128)S(1)}, u32[]{:S(2)}, u32[]{:S(2)}) collective-permute-start(f32[32,16,32]{2,1,0:T(8,128)S(1)} %get-tuple-element.5), channel_id=1, source_target_pairs={{0,16},{16,32},{32,48},{48,64},{64,80},{80,96},{96,112},{112,128},... | collective-permute-start | bytes 196616 | tf_op jit(solution)/shard_map/ppermute | solution.py:100
  35.9 17.9 %collective-permute-start.1 = (f32[32,16,32]{2,1,0:T(8,128)S(1)}, f32[32,16,32]{2,1,0:T(8,128)S(1)}, u32[]{:S(2)}, u32[]{:S(2)}) collective-permute-start(f32[32,16,32]{2,1,0:T(8,128)S(1)} %get-tuple-element.6), channel_id=1, source_target_pairs={{16,0},{32,16},{48,32},{64,48},{80,64},{96,80},{112,96},{128,112},... | collective-permute-start | bytes 196616 | tf_op jit(solution)/shard_map/ppermute | solution.py:101
  62.4 18.6 %collective-permute-start.2 = (f32[32,16,32]{2,0,1:T(8,128)S(1)}, f32[32,16,32]{2,0,1:T(8,128)S(1)}, u32[]{:S(2)}, u32[]{:S(2)}) collective-permute-start(f32[32,16,32]{2,0,1:T(8,128)S(1)} %get-tuple-element.16), channel_id=1, source_target_pairs={{0,16},{16,32},{32,48},{48,64},{64,80},{80,96},{96,112},{112,128},... | collective-permute-start | bytes 196616 | tf_op jit(solution)/shard_map/ppermute | solution.py:114
  67.9 14.3 %collective-permute-start.3 = (f32[32,16,32]{2,0,1:T(8,128)S(1)}, f32[32,16,32]{2,0,1:T(8,128)S(1)}, u32[]{:S(2)}, u32[]{:S(2)}) collective-permute-start(f32[32,16,32]{2,0,1:T(8,128)S(1)} %get-tuple-element.17), channel_id=1, source_target_pairs={{16,0},{32,16},{48,32},{64,48},{80,64},{96,80},{112,96},{128,112},... | collective-permute-start | bytes 196616 | tf_op jit(solution)/shard_map/ppermute | solution.py:119
  83.3 9.7 %copy-start.4 = (bf16[8,224]{1,0:T(8,128)(2,1)S(1)}, bf16[8,224]{1,0:T(8,128)(2,1)}, u32[]{:S(2)}) copy-start(bf16[8,224]{1,0:T(8,128)(2,1)} %param.7) | copy-start | bytes 10756
  87.6 17.7 %copy-start.3 = (bf16[8,16,1024]{2,1,0:T(8,128)(2,1)S(1)}, bf16[8,16,1024]{2,1,0:T(8,128)(2,1)}, u32[]{:S(2)}) copy-start(bf16[8,16,1024]{2,1,0:T(8,128)(2,1)} %param.9) | copy-start | bytes 786436
  87.6 13.5 %all-to-all-start.2 = ((bf16[16,2,4096]{2,1,0:T(2,128)(2,1)}), bf16[16,2,4096]{2,1,0:T(2,128)(2,1)S(1)}, u32[]{:S(2)}, u32[]{:S(2)}) async-start(bf16[16,2,4096]{2,1,0:T(2,128)(2,1)} %reshape.105), calls=%async_computation.2 | async-start | bytes 524288 | tf_op jit(solution)/shard_map/all_to_all | solution.py:125
  101.1 14.4 %all-to-all-start.3 = ((bf16[16,2,7168]{2,1,0:T(2,128)(2,1)}), bf16[16,2,7168]{2,1,0:T(2,128)(2,1)}, u32[]{:S(2)}, u32[]{:S(2)}) async-start(bf16[16,2,7168]{2,1,0:T(2,128)(2,1)} %reshape.107), calls=%async_computation.3 | async-start | bytes 917504 | tf_op jit(solution)/shard_map/all_to_all | solution.py:110

commit v10 on v7

--- a/solution.py
+++ b/solution.py
@@ -90,6 +90,14 @@
     ).astype(bf16)
     tile_rows = lax.all_to_all(cols_done, "spec", split_axis=0, concat_axis=3, tiled=True)[0]
 
+    resp_basis = jnp.dot(response.astype(f32), basis_wide, precision=highest)
+    multi_pred = jnp.einsum("mq,qrc->mrc", resp_basis, latent.astype(f32), precision=highest)
+    multi_resid = (multi_pred - multi_obs.astype(f32)).astype(bf16)
+    grad_ms = jnp.einsum(
+        "mq,mrc->qrc", resp_basis, multi_resid.astype(f32), precision=highest
+    )
+    z_base = latent.astype(f32) - step_size * grad_ms
+
     obs_wide_bands = with_halo(hyper_obs, (("tile", 1),), rim)
     obs_split = obs_wide_bands.reshape(group, wide_rows, n_spec, chunk).transpose(2, 0, 3, 1)
     obs_wide = lax.all_to_all(obs_split, "spec", split_axis=0, concat_axis=1, tiled=True)[0]
@@ -107,6 +115,7 @@
         "tile",
         [(i + 1, i) for i in range(ends)],
     )
+    from_prev, from_next, z_base = lax.optimization_barrier((from_prev, from_next, z_base))
     coef_blurred = own_part + jnp.concatenate([from_prev, from_next], axis=2)
     blurred = split_dot("qji,bq->bji", coef_blurred, basis)
     coarse_at = jnp.arange(wide_rows) + tile_index * coarse_rows - rim
@@ -125,14 +134,7 @@
     resid_bands = lax.all_to_all(resid_split, "spec", split_axis=0, concat_axis=2, tiled=True)[0]
     hs_residual = resid_bands.transpose(0, 2, 1)
 
-    resp_basis = jnp.dot(response.astype(f32), basis_wide, precision=highest)
-    multi_pred = jnp.einsum("mq,qrc->mrc", resp_basis, latent.astype(f32), precision=highest)
-    multi_resid = (multi_pred - multi_obs.astype(f32)).astype(bf16)
-    grad_ms = jnp.einsum(
-        "mq,mrc->qrc", resp_basis, multi_resid.astype(f32), precision=highest
-    )
-    gradient = grad_hs + grad_ms
-    z_next = (latent.astype(f32) - step_size * gradient).astype(bf16)
+    z_next = (z_base - step_size * grad_hs).astype(bf16)
     return (z_next, hs_residual)
 
 

time: 107 us -> 123 us (1.15)
  local copies, waits for them, and re-layouts: 20.4 us -> 28.2 us
  waiting for transfers between devices: 31.4 us -> 36.1 us
  matrix products: 9.9 us -> 13.1 us
  other arithmetic: 3.07 us -> 6.19 us
  starting transfers between devices: 39 us -> 36.4 us
    ppermute x1, waiting for transfers between devices: 14.5 us -> 3.98 us  [shards(): lax.ppermute(lax.slice_in_dim(own_part, half, wide_rows, axis=2), 'tile',...]
    ppermute x1, waiting for transfers between devices: 0.01 us -> 7.43 us  [shards(): lax.ppermute(lax.slice_in_dim(own_part, 0, half, axis=2), 'tile', [(i + 1...]
    all_to_all x1, waiting for transfers between devices: 0.02 us -> 5.9 us  [shards(): lax.all_to_all(resid_split, 'spec', split_axis=0, concat_axis=2, tiled=True)]
    unnamed x24 -> x29, local copies, waits for them, and re-layouts: 10.7 us -> 15.4 us
    ppermute x1, starting transfers between devices: 4.22 us -> 7.49 us  [with_halo(): lax.ppermute(head, axis, [((i + 1) % count, i) for i in range(ends)])]
    ppermute x1, starting transfers between devices: 5.18 us -> 1.92 us  [with_halo(): lax.ppermute(tail, axis, [(i, (i + 1) % count) for i in range(ends)])]
    squeeze x1 -> x0, local copies, waits for them, and re-layouts: 2.4 us -> none  [shards(): lax.all_to_all(back_split, 'spec', split_axis=0, concat_axis=3, tiled=True)]
    transpose x1, local copies, waits for them, and re-layouts: 0.27 us -> 2.5 us  [shards(): rows_back.reshape(subspace, chunk, n_spec, rows_here).transpose(2, 0, 3, 1)]
  transfers between devices with their start and end apart: 8 -> 8, of which waited for: 4 -> 6; matrix products, arithmetic and copies ran while one was open for 17% -> 21% of each run, Pallas kernels for 0% -> 0%
where the time goes in v10:
time: 123 us; the launch traced here: 122 us
  starting transfers between devices  36.4 us (30%)
  waiting for transfers between devices  36.1 us (29%)
  local copies, waits for them, and re-layouts  28.2 us (23%)
  matrix products  13.1 us (11%)
  other arithmetic  6.19 us (5%)
  between operations  1.68 us (1%)
    unnamed x29, local copies, waits for them, and re-layouts  15.4 us
    ppermute x1, starting transfers between devices, with_halo(): lax.ppermute(head, axis, [((i + 1) % count, i) for i in range(ends)])  7.49 us
    ppermute x1, waiting for transfers between devices, shards(): lax.ppermute(lax.slice_in_dim(own_part, 0, half, axis=2), 'tile', [(i + 1...  7.43 us
    ppermute x1, waiting for transfers between devices, with_halo(): lax.ppermute(head, axis, [((i + 1) % count, i) for i in range(ends)])  6.83 us
    all_to_all x1, waiting for transfers between devices, shards(): lax.all_to_all(back_split, 'spec', split_axis=0, concat_axis=3, tiled=True)  6.08 us
    all_to_all x1, waiting for transfers between devices, shards(): lax.all_to_all(resid_split, 'spec', split_axis=0, concat_axis=2, tiled=True)  5.9 us
    ppermute x1, waiting for transfers between devices, with_halo(): lax.ppermute(tail, axis, [(i, (i + 1) % count) for i in range(ends)])  5.89 us
    all_to_all x1, starting transfers between devices, shards(): lax.all_to_all(cols_done, 'spec', split_axis=0, concat_axis=3, tiled=True)  5.75 us
  transfers between devices with their start and end apart: 8, of which 6 were waited for; matrix products, arithmetic and copies ran while one was open for 21% of the time, Pallas kernels for 0%

profile of v10, /device:TPU:24, one launch (start us, length us, event | category | flops | bytes accessed | tf_op | source)
XLA Modules:
  0.0 121.7 jit_solution(8485038615290989016)
XLA Ops:
  4.3 2.4 %fusion.44 = bf16[16,16,16,32]{3,2,1,0:T(8,128)(2,1)} fusion(bf16[16,16,1024,1]{2,1,3,0:T(8,128)(2,1)S(1)} %bitcast.97, bf16[32,16,1024]{2,1,0:T(8,128)(2,1)S(1)} %copy-done.3), kind=kOutput, calls=%fused_computation.72 | convolution fusion | flops 268566528 | bytes 1835008 | tf_op jit(solution)/shard_map/qrc,sjc->sqjr/dot_general | solution.py:85
  6.7 3.1 %reshape.101 = bf16[16,2,4096]{2,1,0:T(2,128)(2,1)} reshape(bf16[16,16,16,32]{3,2,1,0:T(8,128)(2,1)} %fusion.44) | data formatting | bytes 524288
  9.9 5.8 %all-to-all-start = ((bf16[16,2,4096]{2,1,0:T(2,128)(2,1)}), bf16[16,2,4096]{2,1,0:T(2,128)(2,1)S(1)}, u32[]{:S(2)}, u32[]{:S(2)}) async-start(bf16[16,2,4096]{2,1,0:T(2,128)(2,1)} %reshape.101), calls=%async_computation | async-start | bytes 524288 | tf_op jit(solution)/shard_map/all_to_all | solution.py:91
  15.7 7.5 %collective-permute-start.3 = (bf16[14,32,256]{2,1,0:T(8,128)(2,1)S(1)}, bf16[14,32,256]{2,1,0:T(8,128)(2,1)S(1)}, u32[]{:S(2)}, u32[]{:S(2)}) collective-permute-start(bf16[14,32,256]{2,1,0:T(8,128)(2,1)S(1)} %get-tuple-element.19), channel_id=1, source_target_pairs={{16,0},{32,16},{48,32},{64,48},{80,64},{96,80},{112,96},{128,112},... | collective-permute-start | bytes 688136 | tf_op jit(solution)/shard_map/ppermute | solution.py:23
  23.2 1.9 %collective-permute-start.2 = (bf16[14,32,256]{2,1,0:T(8,128)(2,1)S(1)}, bf16[14,32,256]{2,1,0:T(8,128)(2,1)S(1)}, u32[]{:S(2)}, u32[]{:S(2)}) collective-permute-start(bf16[14,32,256]{2,1,0:T(8,128)(2,1)S(1)} %get-tuple-element.18), channel_id=1, source_target_pairs={{0,16},{16,32},{32,48},{48,64},{64,80},{80,96},{96,112},{112,128},... | collective-permute-start | bytes 688136 | tf_op jit(solution)/shard_map/ppermute | solution.py:21
  26.7 6.8 %collective-permute-done.3 = bf16[14,32,256]{2,1,0:T(8,128)(2,1)S(1)} collective-permute-done((bf16[14,32,256]{2,1,0:T(8,128)(2,1)S(1)}, bf16[14,32,256]{2,1,0:T(8,128)(2,1)S(1)}, u32[]{:S(2)}, u32[]{:S(2)}) %collective-permute-start.3) | collective-permute-done | bytes 229408 | tf_op jit(solution)/shard_map/ppermute | solution.py:23
  34.8 5.9 %collective-permute-done.2 = bf16[14,32,256]{2,1,0:T(8,128)(2,1)S(1)} collective-permute-done((bf16[14,32,256]{2,1,0:T(8,128)(2,1)S(1)}, bf16[14,32,256]{2,1,0:T(8,128)(2,1)S(1)}, u32[]{:S(2)}, u32[]{:S(2)}) %collective-permute-start.2) | collective-permute-done | bytes 229408 | tf_op jit(solution)/shard_map/ppermute | solution.py:21
  41.9 2.3 %pad_maximum_fusion = bf16[14,128,256]{1,2,0:T(8,128)(2,1)S(1)} fusion(bf16[14,32,256]{1,2,0:T(8,128)(2,1)} %copy.50, bf16[14,64,256]{1,2,0:T(8,128)(2,1)S(1)} %copy.49, bf16[14,32,256]{1,2,0:T(8,128)(2,1)} %copy.48), kind=kLoop, calls=%fused_computation.16 | loop fusion | flops 2752512 | bytes 1835008 | tf_op jit(solution)/shard_map/concatenate | solution.py:19
  45.3 4.7 %all-to-all-start.1 = ((bf16[16,14,16,128]{3,2,1,0:T(8,128)(2,1)}), bf16[16,14,16,128]{3,2,1,0:T(8,128)(2,1)}, u32[]{:S(2)}, u32[]{:S(2)}) async-start(bf16[16,14,16,128]{3,2,1,0:T(8,128)(2,1)} %copy.51), calls=%async_computation.1 | async-start | bytes 1835008 | tf_op jit(solution)/shard_map/all_to_all | solution.py:103
  50.8 2.3 %fusion.3 = bf16[8,16,1024]{2,0,1:T(8,128)(2,1)} fusion(f32[8,32,1]{1,0,2:T(8,128)S(1)} %convolution_bitcast_fusion.1, bf16[32,16,1024]{2,1,0:T(8,128)(2,1)S(1)} %copy-done.3, bf16[8,16,1024]{2,1,0:T(8,128)(2,1)S(1)} %copy-done.7), kind=kOutput, calls=%fused_computation.9 | convolution fusion | flops 50724864 | bytes 1573888 | tf_op jit(solution)/shard_map/mq,qrc->mrc/dot_general | solution.py:94
  55.8 2.2 %collective-permute-start.1 = (f32[32,16,64]{2,1,0:T(8,128)}, f32[32,16,64]{2,1,0:T(8,128)}, u32[]{:S(2)}, u32[]{:S(2)}) collective-permute-start(f32[32,16,64]{2,1,0:T(8,128)} %get-tuple-element.22), channel_id=1, source_target_pairs={{16,0},{32,16},{48,32},{64,48},{80,64},{96,80},{112,96},{128,112},... | collective-permute-start | bytes 393224 | tf_op jit(solution)/shard_map/ppermute | solution.py:113
  58.0 4.7 %collective-permute-start = (f32[32,16,64]{2,1,0:T(8,128)}, f32[32,16,64]{2,1,0:T(8,128)}, u32[]{:S(2)}, u32[]{:S(2)}) collective-permute-start(f32[32,16,64]{2,1,0:T(8,128)} %get-tuple-element.23), channel_id=1, source_target_pairs={{0,16},{16,32},{32,48},{48,64},{64,80},{80,96},{96,112},{112,128},... | collective-permute-start | bytes 393224 | tf_op jit(solution)/shard_map/ppermute | solution.py:108
  62.7 3.0 %multiply_subtract_fusion = f32[32,16,1024]{2,0,1:T(8,128)S(1)} fusion(f32[8,32,1]{1,0,2:T(8,128)S(1)} %convolution_bitcast_fusion.1, bf16[8,16,1024]{2,0,1:T(8,128)(2,1)} %fusion.3, bf16[32,16,1024]{2,1,0:T(8,128)(2,1)S(1)} %copy-done.3), kind=kOutput, calls=%fused_computation.1 | convolution fusion | flops 51904512 | bytes 3408896 | tf_op jit(solution)/shard_map/mq,mrc->qrc/dot_general | solution.py:96
  65.8 7.4 %collective-permute-done.1 = f32[32,16,64]{2,1,0:T(8,128)} collective-permute-done((f32[32,16,64]{2,1,0:T(8,128)}, f32[32,16,64]{2,1,0:T(8,128)}, u32[]{:S(2)}, u32[]{:S(2)}) %collective-permute-start.1) | collective-permute-done | bytes 131104 | tf_op jit(solution)/shard_map/ppermute | solution.py:113
  73.2 4.0 %collective-permute-done = f32[32,16,64]{2,1,0:T(8,128)} collective-permute-done((f32[32,16,64]{2,1,0:T(8,128)}, f32[32,16,64]{2,1,0:T(8,128)}, u32[]{:S(2)}, u32[]{:S(2)}) %collective-permute-start) | collective-permute-done | bytes 131104 | tf_op jit(solution)/shard_map/ppermute | solution.py:108
  78.3 1.7 %fusion.17 = f32[16,128,224]{1,2,0:T(8,128)} fusion(bf16[32,16,128]{2,1,0:T(8,128)(2,1)S(1)} %get-tuple-element.17, bf16[224,32]{0,1:T(8,128)(2,1)S(1)} %copy-done), kind=kOutput, calls=%fused_computation.33 | convolution fusion | flops 29360128 | bytes 1980416 | tf_op jit(solution)/shard_map/qji,bq->bji/dot_general | solution.py:63
  84.9 2.5 %copy.92 = bf16[16,32,16,16]{1,2,3,0:T(8,128)(2,1)} copy(bf16[16,32,16,16]{1,2,0,3:T(8,128)(2,1)} %bitcast.89) | data formatting | bytes 524288 | tf_op jit(solution)/shard_map/transpose | solution.py:127
  87.4 3.1 %reshape.103 = bf16[16,2,4096]{2,1,0:T(2,128)(2,1)} reshape(bf16[16,16,16,32]{3,2,1,0:T(8,128)(2,1)} %bitcast.90) | data formatting | bytes 524288
  90.5 5.4 %all-to-all-start.2 = ((bf16[16,2,4096]{2,1,0:T(2,128)(2,1)}), bf16[16,2,4096]{2,1,0:T(2,128)(2,1)S(1)}, u32[]{:S(2)}, u32[]{:S(2)}) async-start(bf16[16,2,4096]{2,1,0:T(2,128)(2,1)} %reshape.103), calls=%async_computation.2 | async-start | bytes 524288 | tf_op jit(solution)/shard_map/all_to_all | solution.py:128
  97.9 6.1 %all-to-all-done.2 = bf16[16,2,4096]{2,1,0:T(2,128)(2,1)S(1)} async-done(((bf16[16,2,4096]{2,1,0:T(2,128)(2,1)}), bf16[16,2,4096]{2,1,0:T(2,128)(2,1)S(1)}, u32[]{:S(2)}, u32[]{:S(2)}) %all-to-all-start.2) | async-done | bytes 262176 | tf_op jit(solution)/shard_map/all_to_all | solution.py:128
  104.0 4.2 %all-to-all-start.3 = ((bf16[16,2,7168]{2,1,0:T(2,128)(2,1)}), bf16[16,2,7168]{2,1,0:T(2,128)(2,1)}, u32[]{:S(2)}, u32[]{:S(2)}) async-start(bf16[16,2,7168]{2,1,0:T(2,128)(2,1)} %reshape.105), calls=%async_computation.3 | async-start | bytes 917504 | tf_op jit(solution)/shard_map/all_to_all | solution.py:134
  108.7 1.7 %fusion.5 = f32[32,16,1024]{2,0,1:T(8,128)S(1)} fusion(bf16[32,16,256]{0,1,2:T(8,128)(2,1)S(1)} %bitcast.87, bf16[256,2044]{1,0:T(8,128)(2,1)} %copy-done.2), kind=kOutput, calls=%fused_computation.13 | convolution fusion | flops 268435456 | bytes 2883584 | tf_op jit(solution)/shard_map/qrj,jc->qrc/dot_general | solution.py:129
  112.5 5.9 %all-to-all-done.3 = bf16[16,2,7168]{2,1,0:T(2,128)(2,1)} async-done(((bf16[16,2,7168]{2,1,0:T(2,128)(2,1)}), bf16[16,2,7168]{2,1,0:T(2,128)(2,1)}, u32[]{:S(2)}, u32[]{:S(2)}) %all-to-all-start.3) | async-done | bytes 458784 | tf_op jit(solution)/shard_map/all_to_all | solution.py:134
  118.4 2.1 %reshape.106 = bf16[16,14,16,64]{3,2,1,0:T(8,128)(2,1)S(1)} reshape(bf16[16,2,7168]{2,1,0:T(2,128)(2,1)} %all-to-all-done.3) | data formatting | bytes 917504
  (57 shorter events, 23.3 us)
Async XLA Ops:
  0.6 25.9 %copy-start = (bf16[224,32]{0,1:T(8,128)(2,1)S(1)}, bf16[224,32]{0,1:T(8,128)(2,1)}, u32[]{:S(2)}) copy-start(bf16[224,32]{0,1:T(8,128)(2,1)} %param.6) | copy-start | bytes 43012
  2.6 1.7 %copy-start.3 = (bf16[32,16,1024]{2,1,0:T(8,128)(2,1)S(1)}, bf16[32,16,1024]{2,1,0:T(8,128)(2,1)}, u32[]{:S(2)}) copy-start(bf16[32,16,1024]{2,1,0:T(8,128)(2,1)} %param.5) | copy-start | bytes 3145732
  4.3 2.5 %copy-start.2 = (bf16[256,2044]{1,0:T(8,128)(2,1)}, bf16[256,2044]{1,0:T(8,128)(2,1)S(1)}, u32[]{:S(2)}) copy-start(bf16[256,2044]{1,0:T(8,128)(2,1)S(1)} %reshape.88) | copy-start | bytes 3139588
  6.7 8.9 %copy-start.4 = (bf16[14,64,256]{2,1,0:T(8,128)(2,1)S(1)}, bf16[14,64,256]{2,1,0:T(8,128)(2,1)}, u32[]{:S(2)}) copy-start(bf16[14,64,256]{2,1,0:T(8,128)(2,1)} %param.8) | copy-start | bytes 1376260
  6.7 19.8 %copy-start.8 = (bf16[8,224]{1,0:T(8,128)(2,1)S(1)}, bf16[8,224]{1,0:T(8,128)(2,1)}, u32[]{:S(2)}) copy-start(bf16[8,224]{1,0:T(8,128)(2,1)} %param.7) | copy-start | bytes 10756
  9.9 35.4 %all-to-all-start = ((bf16[16,2,4096]{2,1,0:T(2,128)(2,1)}), bf16[16,2,4096]{2,1,0:T(2,128)(2,1)S(1)}, u32[]{:S(2)}, u32[]{:S(2)}) async-start(bf16[16,2,4096]{2,1,0:T(2,128)(2,1)} %reshape.101), calls=%async_computation | async-start | bytes 524288 | tf_op jit(solution)/shard_map/all_to_all | solution.py:91
  15.7 17.8 %collective-permute-start.3 = (bf16[14,32,256]{2,1,0:T(8,128)(2,1)S(1)}, bf16[14,32,256]{2,1,0:T(8,128)(2,1)S(1)}, u32[]{:S(2)}, u32[]{:S(2)}) collective-permute-start(bf16[14,32,256]{2,1,0:T(8,128)(2,1)S(1)} %get-tuple-element.19), channel_id=1, source_target_pairs={{16,0},{32,16},{48,32},{64,48},{80,64},{96,80},{112,96},{128,112},... | collective-permute-start | bytes 688136 | tf_op jit(solution)/shard_map/ppermute | solution.py:23
  23.2 17.5 %collective-permute-start.2 = (bf16[14,32,256]{2,1,0:T(8,128)(2,1)S(1)}, bf16[14,32,256]{2,1,0:T(8,128)(2,1)S(1)}, u32[]{:S(2)}, u32[]{:S(2)}) collective-permute-start(bf16[14,32,256]{2,1,0:T(8,128)(2,1)S(1)} %get-tuple-element.18), channel_id=1, source_target_pairs={{0,16},{16,32},{32,48},{48,64},{64,80},{80,96},{96,112},{112,128},... | collective-permute-start | bytes 688136 | tf_op jit(solution)/shard_map/ppermute | solution.py:21
  45.3 5.5 %copy-start.7 = (bf16[8,16,1024]{2,1,0:T(8,128)(2,1)S(1)}, bf16[8,16,1024]{2,1,0:T(8,128)(2,1)}, u32[]{:S(2)}) copy-start(bf16[8,16,1024]{2,1,0:T(8,128)(2,1)} %param.9) | copy-start | bytes 786436
  45.3 34.8 %all-to-all-start.1 = ((bf16[16,14,16,128]{3,2,1,0:T(8,128)(2,1)}), bf16[16,14,16,128]{3,2,1,0:T(8,128)(2,1)}, u32[]{:S(2)}, u32[]{:S(2)}) async-start(bf16[16,14,16,128]{3,2,1,0:T(8,128)(2,1)} %copy.51), calls=%async_computation.1 | async-start | bytes 1835008 | tf_op jit(solution)/shard_map/all_to_all | solution.py:103
  50.8 3.9 %copy-start.5 = (bf16[128,764]{1,0:T(8,128)(2,1)}, bf16[128,764]{1,0:T(8,128)(2,1)S(1)}, u32[]{:S(2)}) copy-start(bf16[128,764]{1,0:T(8,128)(2,1)S(1)} %reshape.90) | copy-start | bytes 586756
  55.8 17.4 %collective-permute-start.1 = (f32[32,16,64]{2,1,0:T(8,128)}, f32[32,16,64]{2,1,0:T(8,128)}, u32[]{:S(2)}, u32[]{:S(2)}) collective-permute-start(f32[32,16,64]{2,1,0:T(8,128)} %get-tuple-element.22), channel_id=1, source_target_pairs={{16,0},{32,16},{48,32},{64,48},{80,64},{96,80},{112,96},{128,112},... | collective-permute-start | bytes 393224 | tf_op jit(solution)/shard_map/ppermute | solution.py:113
  58.0 19.1 %collective-permute-start = (f32[32,16,64]{2,1,0:T(8,128)}, f32[32,16,64]{2,1,0:T(8,128)}, u32[]{:S(2)}, u32[]{:S(2)}) collective-permute-start(f32[32,16,64]{2,1,0:T(8,128)} %get-tuple-element.23), channel_id=1, source_target_pairs={{0,16},{16,32},{32,48},{48,64},{64,80},{80,96},{96,112},{112,128},... | collective-permute-start | bytes 393224 | tf_op jit(solution)/shard_map/ppermute | solution.py:108
  80.1 1.8 %copy-start.1 = (f32[16,128,224]{1,2,0:T(8,128)S(1)}, f32[16,128,224]{1,2,0:T(8,128)}, u32[]{:S(2)}) copy-start(f32[16,128,224]{1,2,0:T(8,128)} %fusion.17) | copy-start | bytes 5505028
  81.8 1.2 %copy-start.6 = (bf16[128,764]{1,0:T(8,128)(2,1)S(1)}, bf16[128,764]{1,0:T(8,128)(2,1)}, u32[]{:S(2)}) copy-start(bf16[128,764]{1,0:T(8,128)(2,1)} %copy-done.5) | copy-start | bytes 586756
  90.5 13.5 %all-to-all-start.2 = ((bf16[16,2,4096]{2,1,0:T(2,128)(2,1)}), bf16[16,2,4096]{2,1,0:T(2,128)(2,1)S(1)}, u32[]{:S(2)}, u32[]{:S(2)}) async-start(bf16[16,2,4096]{2,1,0:T(2,128)(2,1)} %reshape.103), calls=%async_computation.2 | async-start | bytes 524288 | tf_op jit(solution)/shard_map/all_to_all | solution.py:128
  104.0 14.4 %all-to-all-start.3 = ((bf16[16,2,7168]{2,1,0:T(2,128)(2,1)}), bf16[16,2,7168]{2,1,0:T(2,128)(2,1)}, u32[]{:S(2)}, u32[]{:S(2)}) async-start(bf16[16,2,7168]{2,1,0:T(2,128)(2,1)} %reshape.105), calls=%async_computation.3 | async-start | bytes 917504 | tf_op jit(solution)/shard_map/all_to_all | solution.py:134

commit v11 on v7

--- a/solution.py
+++ b/solution.py
@@ -90,36 +90,60 @@
     ).astype(bf16)
     tile_rows = lax.all_to_all(cols_done, "spec", split_axis=0, concat_axis=3, tiled=True)[0]
 
-    obs_wide_bands = with_halo(hyper_obs, (("tile", 1),), rim)
-    obs_split = obs_wide_bands.reshape(group, wide_rows, n_spec, chunk).transpose(2, 0, 3, 1)
-    obs_wide = lax.all_to_all(obs_split, "spec", split_axis=0, concat_axis=1, tiled=True)[0]
+    obs_split = hyper_obs.reshape(group, coarse_rows, n_spec, chunk).transpose(2, 0, 3, 1)
+    obs_cols = lax.all_to_all(obs_split, "spec", split_axis=0, concat_axis=1, tiled=True)[0]
+    obs_proj = jnp.einsum("bq,bji->qji", basis, obs_cols, preferred_element_type=f32)
 
     own_part = jnp.einsum("qjr,er->qje", tile_rows, own_rows, preferred_element_type=f32)
     half = wide_rows // 2
     ends = n_tile - 1
-    from_prev = lax.ppermute(
-        lax.slice_in_dim(own_part, half, wide_rows, axis=2),
-        "tile",
-        [(i, i + 1) for i in range(ends)],
+    to_next = jnp.concatenate(
+        [
+            lax.slice_in_dim(own_part, half, wide_rows, axis=2),
+            lax.slice_in_dim(obs_proj, coarse_rows - rim, coarse_rows, axis=2),
+        ],
+        axis=2,
     )
-    from_next = lax.ppermute(
-        lax.slice_in_dim(own_part, 0, half, axis=2),
-        "tile",
-        [(i + 1, i) for i in range(ends)],
+    to_prev = jnp.concatenate(
+        [lax.slice_in_dim(own_part, 0, half, axis=2), lax.slice_in_dim(obs_proj, 0, rim, axis=2)],
+        axis=2,
     )
-    coef_blurred = own_part + jnp.concatenate([from_prev, from_next], axis=2)
-    blurred = split_dot("qji,bq->bji", coef_blurred, basis)
-    coarse_at = jnp.arange(wide_rows) + tile_index * coarse_rows - rim
-    inside = (coarse_at >= 0) & (coarse_at < n_tile * coarse_rows)
-    resid_wide = jnp.where(inside, blurred - obs_wide.astype(f32), 0.0).astype(bf16)
+    got_prev = lax.ppermute(to_next, "tile", [(i, i + 1) for i in range(ends)])
+    got_next = lax.ppermute(to_prev, "tile", [(i + 1, i) for i in range(ends)])
+    coef_blurred = own_part + jnp.concatenate(
+        [lax.slice_in_dim(got_prev, 0, half, axis=2), lax.slice_in_dim(got_next, 0, half, axis=2)],
+        axis=2,
+    )
 
-    coef_resid = jnp.einsum("bq,bji->qji", basis, resid_wide, preferred_element_type=f32)
-    rows_back = split_dot("qjk,kr->qjr", coef_resid, own_rows).astype(bf16)
+    coef_own = lax.slice_in_dim(coef_blurred, rim, rim + coarse_rows, axis=2)
+    blurred = split_dot("qji,bq->bji", coef_own, basis)
+    resid_cols = (blurred - obs_cols.astype(f32)).astype(bf16)
+    coef_resid = jnp.einsum("bq,bji->qji", basis, resid_cols, preferred_element_type=f32)
+
+    gram = jnp.einsum("bq,bp->qp", basis, basis, preferred_element_type=f32)
+    coef_rim = jnp.concatenate(
+        [
+            lax.slice_in_dim(coef_blurred, 0, rim, axis=2),
+            lax.slice_in_dim(coef_blurred, wide_rows - rim, wide_rows, axis=2),
+        ],
+        axis=2,
+    )
+    proj_rim = jnp.concatenate(
+        [lax.slice_in_dim(got_prev, half, half + rim, axis=2),
+         lax.slice_in_dim(got_next, half, half + rim, axis=2)],
+        axis=2,
+    )
+    resid_rim = jnp.einsum("qp,pji->qji", gram, coef_rim, precision=highest) - proj_rim
+    rim_prev = jnp.where(tile_index > 0, lax.slice_in_dim(resid_rim, 0, rim, axis=2), 0.0)
+    rim_next = jnp.where(
+        tile_index < ends, lax.slice_in_dim(resid_rim, rim, 2 * rim, axis=2), 0.0
+    )
+    coef_wide = jnp.concatenate([rim_prev, coef_resid, rim_next], axis=2)
+    rows_back = split_dot("qjk,kr->qjr", coef_wide, own_rows).astype(bf16)
     back_split = rows_back.reshape(subspace, chunk, n_spec, rows_here).transpose(2, 0, 3, 1)
     rows_pixel = lax.all_to_all(back_split, "spec", split_axis=0, concat_axis=3, tiled=True)[0]
     grad_hs = jnp.einsum("qrj,jc->qrc", rows_pixel, column_t, preferred_element_type=f32)
 
-    resid_cols = lax.slice_in_dim(resid_wide, rim, rim + coarse_rows, axis=2)
     resid_split = resid_cols.reshape(n_spec, group, chunk, coarse_rows)
     resid_split, _ = lax.optimization_barrier((resid_split, rows_pixel))
     resid_bands = lax.all_to_all(resid_split, "spec", split_axis=0, concat_axis=2, tiled=True)[0]

time: 107 us -> 102 us (0.953)
  starting transfers between devices: 39 us -> 27 us
  local copies, waits for them, and re-layouts: 20.4 us -> 26.3 us
  waiting for transfers between devices: 31.4 us -> 33.3 us
    ppermute x4 -> x2, waiting for transfers between devices: 25.5 us -> 15.6 us  [the longest x1 8.32 us: shards(): got_next = lax.ppermute(to_prev, 'tile', [(i + 1, i) for i in range(ends)])]
    ppermute x4 -> x2, starting transfers between devices: 18.5 us -> 9.59 us  [the longest x1 7.49 us: shards(): got_next = lax.ppermute(to_prev, 'tile', [(i + 1, i) for i in range(ends)])]
    all_to_all x1, waiting for transfers between devices: 0.01 us -> 6.76 us  [shards(): lax.all_to_all(obs_split, 'spec', split_axis=0, concat_axis=1, tiled=True)]
    all_to_all x1, waiting for transfers between devices: 0.01 us -> 5.15 us  [shards(): lax.all_to_all(cols_done, 'spec', split_axis=0, concat_axis=3, tiled=True)]
    unnamed x24 -> x30, local copies, waits for them, and re-layouts: 10.7 us -> 15.2 us
    all_to_all x1, starting transfers between devices: 5.48 us -> 3.66 us  [shards(): lax.all_to_all(back_split, 'spec', split_axis=0, concat_axis=3, tiled=True)]
    all_to_all x1, starting transfers between devices: 4.88 us -> 3.56 us  [shards(): lax.all_to_all(obs_split, 'spec', split_axis=0, concat_axis=1, tiled=True)]
    convert_element_type x1 -> x0, other arithmetic: 1.31 us -> none  [shards(): obs_wide.astype(f32)]
  transfers between devices with their start and end apart: 8 -> 6, of which waited for: 4 -> 5; matrix products, arithmetic and copies ran while one was open for 17% -> 18% of each run, Pallas kernels for 0% -> 0%
where the time goes in v11:
time: 102 us; the launch traced here: 101 us
  waiting for transfers between devices  33.3 us (33%)
  starting transfers between devices  27 us (26%)
  local copies, waits for them, and re-layouts  26.3 us (26%)
  matrix products  10.1 us (10%)
  other arithmetic  2.03 us (2%)
  between operations  1.8 us (2%)
    unnamed x30, local copies, waits for them, and re-layouts  15.2 us
    ppermute x1, waiting for transfers between devices, shards(): got_next = lax.ppermute(to_prev, 'tile', [(i + 1, i) for i in range(ends)])  8.32 us
    ppermute x1, starting transfers between devices, shards(): got_next = lax.ppermute(to_prev, 'tile', [(i + 1, i) for i in range(ends)])  7.49 us
    ppermute x1, waiting for transfers between devices, shards(): got_prev = lax.ppermute(to_next, 'tile', [(i, i + 1) for i in range(ends)])  7.23 us
    all_to_all x1, waiting for transfers between devices, shards(): lax.all_to_all(obs_split, 'spec', split_axis=0, concat_axis=1, tiled=True)  6.76 us
    all_to_all x1, waiting for transfers between devices, shards(): lax.all_to_all(back_split, 'spec', split_axis=0, concat_axis=3, tiled=True)  5.81 us
    all_to_all x1, starting transfers between devices, shards(): lax.all_to_all(cols_done, 'spec', split_axis=0, concat_axis=3, tiled=True)  5.76 us
    all_to_all x1, waiting for transfers between devices, shards(): lax.all_to_all(cols_done, 'spec', split_axis=0, concat_axis=3, tiled=True)  5.15 us
  transfers between devices with their start and end apart: 6, of which 5 were waited for; matrix products, arithmetic and copies ran while one was open for 18% of the time, Pallas kernels for 0%

profile of v11, /device:TPU:24, one launch (start us, length us, event | category | flops | bytes accessed | tf_op | source)
XLA Modules:
  0.0 100.5 jit_solution(8238537607765705140)
XLA Ops:
  2.6 1.7 %reshape.86 = bf16[256,2044]{1,0:T(8,128)(2,1)S(1)} reshape(bf16[523264]{0:T(1024)(128)(2,1)S(1)} %slice.68) | data formatting | bytes 2093056 | tf_op jit(solution)/shard_map/reshape | solution.py:55
  4.3 1.4 %fusion.51 = bf16[16,16,16,32]{3,2,1,0:T(8,128)(2,1)S(1)} fusion(bf16[16,16,1024,1]{2,1,3,0:T(8,128)(2,1)S(1)} %bitcast.107, bf16[32,16,1024]{2,1,0:T(8,128)(2,1)S(1)} %copy-done.1), kind=kOutput, calls=%fused_computation.83 | convolution fusion | flops 268566528 | bytes 1835008 | tf_op jit(solution)/shard_map/qrc,sjc->sqjr/dot_general | solution.py:85
  5.8 1.7 %reshape.101 = bf16[16,2,4096]{2,1,0:T(2,128)(2,1)} reshape(bf16[16,16,16,32]{3,2,1,0:T(8,128)(2,1)S(1)} %fusion.51) | data formatting | bytes 524288
  7.4 5.8 %all-to-all-start = ((bf16[16,2,4096]{2,1,0:T(2,128)(2,1)}), bf16[16,2,4096]{2,1,0:T(2,128)(2,1)S(1)}, u32[]{:S(2)}, u32[]{:S(2)}) async-start(bf16[16,2,4096]{2,1,0:T(2,128)(2,1)} %reshape.101), calls=%async_computation | async-start | bytes 524288 | tf_op jit(solution)/shard_map/all_to_all | solution.py:91
  13.2 1.4 %copy.50 = bf16[14,64,256]{1,2,0:T(8,128)(2,1)S(1)} copy(bf16[14,64,256]{2,1,0:T(8,128)(2,1)} %param.8) | data formatting | bytes 917504 | tf_op args[3]
  14.8 1.3 %reshape.99 = bf16[16,2,7168]{2,1,0:T(2,128)(2,1)} reshape(bf16[16,14,16,64]{3,2,1,0:T(8,128)(2,1)S(1)} %copy.51) | data formatting | bytes 917504
  16.1 5.2 %all-to-all-done = bf16[16,2,4096]{2,1,0:T(2,128)(2,1)S(1)} async-done(((bf16[16,2,4096]{2,1,0:T(2,128)(2,1)}), bf16[16,2,4096]{2,1,0:T(2,128)(2,1)S(1)}, u32[]{:S(2)}, u32[]{:S(2)}) %all-to-all-start) | async-done | bytes 262176 | tf_op jit(solution)/shard_map/all_to_all | solution.py:91
  21.3 3.6 %all-to-all-start.1 = ((bf16[16,2,7168]{2,1,0:T(2,128)(2,1)}), bf16[16,2,7168]{2,1,0:T(2,128)(2,1)S(1)}, u32[]{:S(2)}, u32[]{:S(2)}) async-start(bf16[16,2,7168]{2,1,0:T(2,128)(2,1)} %reshape.99), calls=%async_computation.1 | async-start | bytes 917504 | tf_op jit(solution)/shard_map/all_to_all | solution.py:94
  28.2 6.8 %all-to-all-done.1 = bf16[16,2,7168]{2,1,0:T(2,128)(2,1)S(1)} async-done(((bf16[16,2,7168]{2,1,0:T(2,128)(2,1)}), bf16[16,2,7168]{2,1,0:T(2,128)(2,1)S(1)}, u32[]{:S(2)}, u32[]{:S(2)}) %all-to-all-start.1) | async-done | bytes 458784 | tf_op jit(solution)/shard_map/all_to_all | solution.py:94
  37.2 7.5 %collective-permute-start.1 = (f32[32,16,96]{2,1,0:T(8,128)S(1)}, f32[32,16,96]{2,1,0:T(8,128)S(1)}, u32[]{:S(2)}, u32[]{:S(2)}) collective-permute-start(f32[32,16,96]{2,1,0:T(8,128)S(1)} %pad_maximum_fusion.1), channel_id=1, source_target_pairs={{16,0},{32,16},{48,32},{64,48},{80,64},{96,80},{112,96},{128,112},... | collective-permute-start | bytes 589832 | tf_op jit(solution)/shard_map/ppermute | solution.py:112
  44.9 2.1 %collective-permute-start = (f32[32,16,96]{2,1,0:T(8,128)S(1)}, f32[32,16,96]{2,1,0:T(8,128)S(1)}, u32[]{:S(2)}, u32[]{:S(2)}) collective-permute-start(f32[32,16,96]{2,1,0:T(8,128)S(1)} %pad_maximum_fusion), channel_id=1, source_target_pairs={{0,16},{16,32},{32,48},{48,64},{64,80},{80,96},{96,112},{112,128},... | collective-permute-start | bytes 589832 | tf_op jit(solution)/shard_map/ppermute | solution.py:111
  47.1 8.3 %collective-permute-done.1 = f32[32,16,96]{2,1,0:T(8,128)S(1)} collective-permute-done((f32[32,16,96]{2,1,0:T(8,128)S(1)}, f32[32,16,96]{2,1,0:T(8,128)S(1)}, u32[]{:S(2)}, u32[]{:S(2)}) %collective-permute-start.1) | collective-permute-done | bytes 196640 | tf_op jit(solution)/shard_map/ppermute | solution.py:112
  55.4 7.2 %collective-permute-done = f32[32,16,96]{2,1,0:T(8,128)S(1)} collective-permute-done((f32[32,16,96]{2,1,0:T(8,128)S(1)}, f32[32,16,96]{2,1,0:T(8,128)S(1)}, u32[]{:S(2)}, u32[]{:S(2)}) %collective-permute-start) | collective-permute-done | bytes 196640 | tf_op jit(solution)/shard_map/ppermute | solution.py:111
  66.7 1.2 %copy.107 = bf16[16,32,16,16]{1,2,3,0:T(8,128)(2,1)} copy(bf16[16,32,16,16]{1,2,0,3:T(8,128)(2,1)S(1)} %bitcast.96) | data formatting | bytes 524288 | tf_op jit(solution)/shard_map/transpose | solution.py:143
  68.0 3.1 %reshape.103 = bf16[16,2,4096]{2,1,0:T(2,128)(2,1)} reshape(bf16[16,16,16,32]{3,2,1,0:T(8,128)(2,1)} %bitcast.97) | data formatting | bytes 524288
  71.0 3.7 %all-to-all-start.2 = ((bf16[16,2,4096]{2,1,0:T(2,128)(2,1)}), bf16[16,2,4096]{2,1,0:T(2,128)(2,1)S(1)}, u32[]{:S(2)}, u32[]{:S(2)}) async-start(bf16[16,2,4096]{2,1,0:T(2,128)(2,1)} %reshape.103), calls=%async_computation.2 | async-start | bytes 524288 | tf_op jit(solution)/shard_map/all_to_all | solution.py:144
  75.6 1.3 %reshape.105 = bf16[16,2,7168]{2,1,0:T(2,128)(2,1)} reshape(bf16[16,14,16,64]{3,2,1,0:T(8,128)(2,1)S(1)} %bitcast.103) | data formatting | bytes 917504
  76.9 5.8 %all-to-all-done.2 = bf16[16,2,4096]{2,1,0:T(2,128)(2,1)S(1)} async-done(((bf16[16,2,4096]{2,1,0:T(2,128)(2,1)}), bf16[16,2,4096]{2,1,0:T(2,128)(2,1)S(1)}, u32[]{:S(2)}, u32[]{:S(2)}) %all-to-all-start.2) | async-done | bytes 262176 | tf_op jit(solution)/shard_map/all_to_all | solution.py:144
  82.7 4.4 %all-to-all-start.3 = ((bf16[16,2,7168]{2,1,0:T(2,128)(2,1)}), bf16[16,2,7168]{2,1,0:T(2,128)(2,1)}, u32[]{:S(2)}, u32[]{:S(2)}) async-start(bf16[16,2,7168]{2,1,0:T(2,128)(2,1)} %reshape.105), calls=%async_computation.3 | async-start | bytes 917504 | tf_op jit(solution)/shard_map/all_to_all | solution.py:149
  87.2 1.6 %fusion.8 = bf16[8,16,1024]{2,0,1:T(8,128)(2,1)S(1)} fusion(f32[8,32,1]{1,0,2:T(8,128)S(1)} %convolution_bitcast_fusion.2, bf16[32,16,1024]{2,1,0:T(8,128)(2,1)S(1)} %copy-done.1, bf16[8,16,1024]{2,1,0:T(8,128)(2,1)S(1)} %copy-done.6), kind=kOutput, calls=%fused_computation.13 | convolution fusion | flops 50724864 | bytes 1573888 | tf_op jit(solution)/shard_map/mq,qrc->mrc/dot_general | solution.py:153
  89.8 1.5 %reshape.104 = bf16[16,16,16,32]{3,2,1,0:T(8,128)(2,1)} reshape(bf16[16,2,4096]{2,1,0:T(2,128)(2,1)S(1)} %all-to-all-done.2) | data formatting | bytes 524288
  91.2 2.4 %copy.67 = bf16[32,16,256]{2,1,0:T(8,128)(2,1)S(1)} copy(bf16[32,16,256]{0,1,2:T(8,128)(2,1)} %bitcast.95) | data formatting | bytes 524288 | tf_op jit(solution)/shard_map/squeeze | solution.py:144
  93.7 3.4 %fusion.2 = bf16[32,16,1024]{2,1,0:T(8,128)(2,1)} fusion(f32[32,16,1024]{2,0,1:T(8,128)S(1)} %fusion.54, bf16[32,16,1024]{2,1,0:T(8,128)(2,1)S(1)} %copy-done.1, bf16[32,16,256]{2,1,0:T(8,128)(2,1)S(1)} %copy.67, bf16[256,2044]{1,0:T(8,128)(2,1)} %copy-done.2), kind=kOutput, calls=%fused_computation.3 | convolution fusion | flops 271056896 | bytes 4980736 | tf_op jit(solution)/shard_map/qrj,jc->qrc/dot_general | solution.py:145
  97.1 2.1 %reshape.106 = bf16[16,14,16,64]{3,2,1,0:T(8,128)(2,1)S(1)} reshape(bf16[16,2,7168]{2,1,0:T(2,128)(2,1)} %all-to-all-done.3) | data formatting | bytes 917504
  (64 shorter events, 14.4 us)
Async XLA Ops:
  0.6 35.6 %copy-start = (bf16[224,32]{0,1:T(8,128)(2,1)S(1)}, bf16[224,32]{0,1:T(8,128)(2,1)}, u32[]{:S(2)}) copy-start(bf16[224,32]{0,1:T(8,128)(2,1)} %param.6) | copy-start | bytes 43012
  2.5 1.8 %copy-start.1 = (bf16[32,16,1024]{2,1,0:T(8,128)(2,1)S(1)}, bf16[32,16,1024]{2,1,0:T(8,128)(2,1)}, u32[]{:S(2)}) copy-start(bf16[32,16,1024]{2,1,0:T(8,128)(2,1)} %param.5) | copy-start | bytes 3145732
  4.3 1.5 %copy-start.2 = (bf16[256,2044]{1,0:T(8,128)(2,1)}, bf16[256,2044]{1,0:T(8,128)(2,1)S(1)}, u32[]{:S(2)}) copy-start(bf16[256,2044]{1,0:T(8,128)(2,1)S(1)} %reshape.86) | copy-start | bytes 3139588
  7.4 13.8 %all-to-all-start = ((bf16[16,2,4096]{2,1,0:T(2,128)(2,1)}), bf16[16,2,4096]{2,1,0:T(2,128)(2,1)S(1)}, u32[]{:S(2)}, u32[]{:S(2)}) async-start(bf16[16,2,4096]{2,1,0:T(2,128)(2,1)} %reshape.101), calls=%async_computation | async-start | bytes 524288 | tf_op jit(solution)/shard_map/all_to_all | solution.py:91
  21.3 13.7 %all-to-all-start.1 = ((bf16[16,2,7168]{2,1,0:T(2,128)(2,1)}), bf16[16,2,7168]{2,1,0:T(2,128)(2,1)S(1)}, u32[]{:S(2)}, u32[]{:S(2)}) async-start(bf16[16,2,7168]{2,1,0:T(2,128)(2,1)} %reshape.99), calls=%async_computation.1 | async-start | bytes 917504 | tf_op jit(solution)/shard_map/all_to_all | solution.py:94
  25.6 2.6 %copy-start.4 = (bf16[128,764]{1,0:T(8,128)(2,1)}, bf16[128,764]{1,0:T(8,128)(2,1)S(1)}, u32[]{:S(2)}) copy-start(bf16[128,764]{1,0:T(8,128)(2,1)S(1)} %reshape.88) | copy-start | bytes 586756
  35.5 1.6 %copy-start.3 = (f32[32,16,64]{2,1,0:T(8,128)S(1)}, f32[32,16,64]{2,1,0:T(8,128)}, u32[]{:S(2)}) copy-start(f32[32,16,64]{2,1,0:T(8,128)} %get-tuple-element.17) | copy-start | bytes 393220
  37.2 18.2 %collective-permute-start.1 = (f32[32,16,96]{2,1,0:T(8,128)S(1)}, f32[32,16,96]{2,1,0:T(8,128)S(1)}, u32[]{:S(2)}, u32[]{:S(2)}) collective-permute-start(f32[32,16,96]{2,1,0:T(8,128)S(1)} %pad_maximum_fusion.1), channel_id=1, source_target_pairs={{16,0},{32,16},{48,32},{64,48},{80,64},{96,80},{112,96},{128,112},... | collective-permute-start | bytes 589832 | tf_op jit(solution)/shard_map/ppermute | solution.py:112
  44.9 17.8 %collective-permute-start = (f32[32,16,96]{2,1,0:T(8,128)S(1)}, f32[32,16,96]{2,1,0:T(8,128)S(1)}, u32[]{:S(2)}, u32[]{:S(2)}) collective-permute-start(f32[32,16,96]{2,1,0:T(8,128)S(1)} %pad_maximum_fusion), channel_id=1, source_target_pairs={{0,16},{16,32},{32,48},{48,64},{64,80},{80,96},{96,112},{112,128},... | collective-permute-start | bytes 589832 | tf_op jit(solution)/shard_map/ppermute | solution.py:111
  64.8 0.9 copy-start.5
  66.7 8.0 %copy-start.7 = (bf16[8,224]{1,0:T(8,128)(2,1)S(1)}, bf16[8,224]{1,0:T(8,128)(2,1)}, u32[]{:S(2)}) copy-start(bf16[8,224]{1,0:T(8,128)(2,1)} %param.7) | copy-start | bytes 10756
  71.0 16.1 %copy-start.6 = (bf16[8,16,1024]{2,1,0:T(8,128)(2,1)S(1)}, bf16[8,16,1024]{2,1,0:T(8,128)(2,1)}, u32[]{:S(2)}) copy-start(bf16[8,16,1024]{2,1,0:T(8,128)(2,1)} %param.9) | copy-start | bytes 786436
  71.0 11.7 %all-to-all-start.2 = ((bf16[16,2,4096]{2,1,0:T(2,128)(2,1)}), bf16[16,2,4096]{2,1,0:T(2,128)(2,1)S(1)}, u32[]{:S(2)}, u32[]{:S(2)}) async-start(bf16[16,2,4096]{2,1,0:T(2,128)(2,1)} %reshape.103), calls=%async_computation.2 | async-start | bytes 524288 | tf_op jit(solution)/shard_map/all_to_all | solution.py:144
  82.7 14.4 %all-to-all-start.3 = ((bf16[16,2,7168]{2,1,0:T(2,128)(2,1)}), bf16[16,2,7168]{2,1,0:T(2,128)(2,1)}, u32[]{:S(2)}, u32[]{:S(2)}) async-start(bf16[16,2,7168]{2,1,0:T(2,128)(2,1)} %reshape.105), calls=%async_computation.3 | async-start | bytes 917504 | tf_op jit(solution)/shard_map/all_to_all | solution.py:149

commit v12 on v11

--- a/solution.py
+++ b/solution.py
@@ -82,17 +82,19 @@
     column_t = banded(coarse_cols, width_cols, DECIM, 0)
     own_rows = banded(wide_rows, rows_dev, DECIM, HALO)
 
+    obs_split = hyper_obs.reshape(group, coarse_rows, n_spec, chunk).transpose(2, 0, 3, 1)
+    obs_cols = lax.all_to_all(obs_split, "spec", split_axis=0, concat_axis=1, tiled=True)[0]
+    obs_proj = jnp.einsum("bq,bji->qji", basis, obs_cols, preferred_element_type=f32)
+
+    latent_now, obs_cols = lax.optimization_barrier((latent, obs_cols))
+
     cols_done = jnp.einsum(
         "qrc,sjc->sqjr",
-        latent,
+        latent_now,
         column_t.reshape(n_spec, chunk, width_cols),
         preferred_element_type=f32,
     ).astype(bf16)
     tile_rows = lax.all_to_all(cols_done, "spec", split_axis=0, concat_axis=3, tiled=True)[0]
-
-    obs_split = hyper_obs.reshape(group, coarse_rows, n_spec, chunk).transpose(2, 0, 3, 1)
-    obs_cols = lax.all_to_all(obs_split, "spec", split_axis=0, concat_axis=1, tiled=True)[0]
-    obs_proj = jnp.einsum("bq,bji->qji", basis, obs_cols, preferred_element_type=f32)
 
     own_part = jnp.einsum("qjr,er->qje", tile_rows, own_rows, preferred_element_type=f32)
     half = wide_rows // 2

time: 102 us -> 105 us (1.029)
  local copies, waits for them, and re-layouts: 26.3 us -> 30.2 us
  waiting for transfers between devices: 33.3 us -> 30.6 us
  matrix products: 10.1 us -> 11.6 us
    unnamed x30, local copies, waits for them, and re-layouts: 15.2 us -> 18.4 us
    ppermute x1, waiting for transfers between devices: 8.32 us -> 5.72 us  [shards(): got_next = lax.ppermute(to_prev, 'tile', [(i + 1, i) for i in range(ends)])]
    all_to_all x1, waiting for transfers between devices: 6.76 us -> 4.17 us  [shards(): lax.all_to_all(obs_split, 'spec', split_axis=0, concat_axis=1, tiled=True)]
    all_to_all x1, starting transfers between devices: 3.56 us -> 5.8 us  [shards(): lax.all_to_all(obs_split, 'spec', split_axis=0, concat_axis=1, tiled=True)]
    all_to_all x1, starting transfers between devices: 5.76 us -> 3.53 us  [shards(): lax.all_to_all(cols_done, 'spec', split_axis=0, concat_axis=3, tiled=True)]
    all_to_all x1, waiting for transfers between devices: 5.15 us -> 6.58 us  [shards(): lax.all_to_all(cols_done, 'spec', split_axis=0, concat_axis=3, tiled=True)]
    ppermute x1, waiting for transfers between devices: 7.23 us -> 8.33 us  [shards(): got_prev = lax.ppermute(to_next, 'tile', [(i, i + 1) for i in range(ends)])]
  transfers between devices with their start and end apart: 6 -> 6, of which waited for: 5 -> 5; matrix products, arithmetic and copies ran while one was open for 18% -> 19% of each run, Pallas kernels for 0% -> 0%
where the time goes in v12:
time: 105 us; the launch traced here: 104 us
  waiting for transfers between devices  30.6 us (29%)
  local copies, waits for them, and re-layouts  30.2 us (29%)
  starting transfers between devices  27 us (26%)
  matrix products  11.6 us (11%)
  other arithmetic  2.74 us (3%)
  between operations  1.79 us (2%)
    unnamed x30, local copies, waits for them, and re-layouts  18.4 us
    ppermute x1, waiting for transfers between devices, shards(): got_prev = lax.ppermute(to_next, 'tile', [(i, i + 1) for i in range(ends)])  8.33 us
    ppermute x1, starting transfers between devices, shards(): got_next = lax.ppermute(to_prev, 'tile', [(i + 1, i) for i in range(ends)])  7.48 us
    all_to_all x1, waiting for transfers between devices, shards(): lax.all_to_all(cols_done, 'spec', split_axis=0, concat_axis=3, tiled=True)  6.58 us
    all_to_all x1, waiting for transfers between devices, shards(): lax.all_to_all(back_split, 'spec', split_axis=0, concat_axis=3, tiled=True)  5.81 us
    all_to_all x1, starting transfers between devices, shards(): lax.all_to_all(obs_split, 'spec', split_axis=0, concat_axis=1, tiled=True)  5.8 us
    ppermute x1, waiting for transfers between devices, shards(): got_next = lax.ppermute(to_prev, 'tile', [(i + 1, i) for i in range(ends)])  5.72 us
    all_to_all x1, starting transfers between devices, shards(): lax.all_to_all(resid_split, 'spec', split_axis=0, concat_axis=2, tiled=True)  4.44 us
  transfers between devices with their start and end apart: 6, of which 5 were waited for; matrix products, arithmetic and copies ran while one was open for 19% of the time, Pallas kernels for 0%

profile of v12, /device:TPU:24, one launch (start us, length us, event | category | flops | bytes accessed | tf_op | source)
XLA Modules:
  0.0 104.0 jit_solution(8457848861975211774)
XLA Ops:
  0.6 1.4 %copy.48 = bf16[14,64,256]{1,2,0:T(8,128)(2,1)S(1)} copy(bf16[14,64,256]{2,1,0:T(8,128)(2,1)} %param.8) | data formatting | bytes 917504 | tf_op args[3]
  2.3 1.3 %reshape.99 = bf16[16,2,7168]{2,1,0:T(2,128)(2,1)} reshape(bf16[16,14,16,64]{3,2,1,0:T(8,128)(2,1)S(1)} %copy.49) | data formatting | bytes 917504
  3.5 5.8 %all-to-all-start = ((bf16[16,2,7168]{2,1,0:T(2,128)(2,1)}), bf16[16,2,7168]{2,1,0:T(2,128)(2,1)}, u32[]{:S(2)}, u32[]{:S(2)}) async-start(bf16[16,2,7168]{2,1,0:T(2,128)(2,1)} %reshape.99), calls=%async_computation | async-start | bytes 917504 | tf_op jit(solution)/shard_map/all_to_all | solution.py:86
  12.8 1.7 %reshape.86 = bf16[256,2044]{1,0:T(8,128)(2,1)S(1)} reshape(bf16[523264]{0:T(1024)(128)(2,1)S(1)} %slice.68) | data formatting | bytes 2093056 | tf_op jit(solution)/shard_map/reshape | solution.py:55
  15.4 4.2 %all-to-all-done = bf16[16,2,7168]{2,1,0:T(2,128)(2,1)} async-done(((bf16[16,2,7168]{2,1,0:T(2,128)(2,1)}), bf16[16,2,7168]{2,1,0:T(2,128)(2,1)}, u32[]{:S(2)}, u32[]{:S(2)}) %all-to-all-start) | async-done | bytes 458784 | tf_op jit(solution)/shard_map/all_to_all | solution.py:86
  19.6 2.1 %reshape.100 = bf16[16,14,16,64]{3,2,1,0:T(8,128)(2,1)S(1)} reshape(bf16[16,2,7168]{2,1,0:T(2,128)(2,1)} %all-to-all-done) | data formatting | bytes 917504
  21.7 1.4 %fusion.52 = bf16[16,16,16,32]{3,2,1,0:T(8,128)(2,1)S(1)} fusion(bf16[16,16,1024,1]{2,1,3,0:T(8,128)(2,1)S(1)} %bitcast.107, bf16[32,16,1024]{2,1,0:T(8,128)(2,1)S(1)} %copy-done.1), kind=kOutput, calls=%fused_computation.84 | convolution fusion | flops 268566528 | bytes 1835008 | tf_op jit(solution)/shard_map/qrc,sjc->sqjr/dot_general | solution.py:91
  23.1 1.7 %reshape.101 = bf16[16,2,4096]{2,1,0:T(2,128)(2,1)} reshape(bf16[16,16,16,32]{3,2,1,0:T(8,128)(2,1)S(1)} %fusion.52) | data formatting | bytes 524288
  24.8 3.5 %all-to-all-start.1 = ((bf16[16,2,4096]{2,1,0:T(2,128)(2,1)}), bf16[16,2,4096]{2,1,0:T(2,128)(2,1)S(1)}, u32[]{:S(2)}, u32[]{:S(2)}) async-start(bf16[16,2,4096]{2,1,0:T(2,128)(2,1)} %reshape.101), calls=%async_computation.1 | async-start | bytes 524288 | tf_op jit(solution)/shard_map/all_to_all | solution.py:97
  29.8 6.6 %all-to-all-done.1 = bf16[16,2,4096]{2,1,0:T(2,128)(2,1)S(1)} async-done(((bf16[16,2,4096]{2,1,0:T(2,128)(2,1)}), bf16[16,2,4096]{2,1,0:T(2,128)(2,1)S(1)}, u32[]{:S(2)}, u32[]{:S(2)}) %all-to-all-start.1) | async-done | bytes 262176 | tf_op jit(solution)/shard_map/all_to_all | solution.py:97
  36.8 1.8 %copy.51 = bf16[32,16,256]{2,1,0:T(8,128)(2,1)} copy(bf16[32,16,256]{0,1,2:T(8,128)(2,1)S(1)} %bitcast.95) | data formatting | bytes 524288 | tf_op jit(solution)/shard_map/squeeze | solution.py:97
  40.8 7.5 %collective-permute-start.1 = (f32[32,16,96]{2,1,0:T(8,128)}, f32[32,16,96]{2,1,0:T(8,128)S(1)}, u32[]{:S(2)}, u32[]{:S(2)}) collective-permute-start(f32[32,16,96]{2,1,0:T(8,128)} %pad_maximum_fusion.1), channel_id=1, source_target_pairs={{16,0},{32,16},{48,32},{64,48},{80,64},{96,80},{112,96},{128,112},... | collective-permute-start | bytes 589832 | tf_op jit(solution)/shard_map/ppermute | solution.py:114
  48.4 2.1 %collective-permute-start = (f32[32,16,96]{2,1,0:T(8,128)S(1)}, f32[32,16,96]{2,1,0:T(8,128)S(1)}, u32[]{:S(2)}, u32[]{:S(2)}) collective-permute-start(f32[32,16,96]{2,1,0:T(8,128)S(1)} %pad_maximum_fusion), channel_id=1, source_target_pairs={{0,16},{16,32},{32,48},{48,64},{64,80},{80,96},{96,112},{112,128},... | collective-permute-start | bytes 589832 | tf_op jit(solution)/shard_map/ppermute | solution.py:113
  52.1 5.7 %collective-permute-done.1 = f32[32,16,96]{2,1,0:T(8,128)S(1)} collective-permute-done((f32[32,16,96]{2,1,0:T(8,128)}, f32[32,16,96]{2,1,0:T(8,128)S(1)}, u32[]{:S(2)}, u32[]{:S(2)}) %collective-permute-start.1) | collective-permute-done | bytes 196640 | tf_op jit(solution)/shard_map/ppermute | solution.py:114
  57.8 8.3 %collective-permute-done = f32[32,16,96]{2,1,0:T(8,128)S(1)} collective-permute-done((f32[32,16,96]{2,1,0:T(8,128)S(1)}, f32[32,16,96]{2,1,0:T(8,128)S(1)}, u32[]{:S(2)}, u32[]{:S(2)}) %collective-permute-start) | collective-permute-done | bytes 196640 | tf_op jit(solution)/shard_map/ppermute | solution.py:113
  71.4 3.1 %reshape.103 = bf16[16,2,4096]{2,1,0:T(2,128)(2,1)} reshape(bf16[16,16,16,32]{3,2,1,0:T(8,128)(2,1)} %bitcast.98) | data formatting | bytes 524288
  74.5 3.7 %all-to-all-start.2 = ((bf16[16,2,4096]{2,1,0:T(2,128)(2,1)}), bf16[16,2,4096]{2,1,0:T(2,128)(2,1)S(1)}, u32[]{:S(2)}, u32[]{:S(2)}) async-start(bf16[16,2,4096]{2,1,0:T(2,128)(2,1)} %reshape.103), calls=%async_computation.2 | async-start | bytes 524288 | tf_op jit(solution)/shard_map/all_to_all | solution.py:146
  80.4 5.8 %all-to-all-done.2 = bf16[16,2,4096]{2,1,0:T(2,128)(2,1)S(1)} async-done(((bf16[16,2,4096]{2,1,0:T(2,128)(2,1)}), bf16[16,2,4096]{2,1,0:T(2,128)(2,1)S(1)}, u32[]{:S(2)}, u32[]{:S(2)}) %all-to-all-start.2) | async-done | bytes 262176 | tf_op jit(solution)/shard_map/all_to_all | solution.py:146
  86.2 4.4 %all-to-all-start.3 = ((bf16[16,2,7168]{2,1,0:T(2,128)(2,1)}), bf16[16,2,7168]{2,1,0:T(2,128)(2,1)}, u32[]{:S(2)}, u32[]{:S(2)}) async-start(bf16[16,2,7168]{2,1,0:T(2,128)(2,1)} %reshape.105), calls=%async_computation.3 | async-start | bytes 917504 | tf_op jit(solution)/shard_map/all_to_all | solution.py:151
  90.6 1.6 %fusion.8 = bf16[8,16,1024]{2,0,1:T(8,128)(2,1)S(1)} fusion(f32[8,32,1]{1,0,2:T(8,128)S(1)} %convolution_bitcast_fusion.2, bf16[32,16,1024]{2,1,0:T(8,128)(2,1)S(1)} %copy-done.1, bf16[8,16,1024]{2,1,0:T(8,128)(2,1)S(1)} %copy-done.5), kind=kOutput, calls=%fused_computation.13 | convolution fusion | flops 50724864 | bytes 1573888 | tf_op jit(solution)/shard_map/mq,qrc->mrc/dot_general | solution.py:155
  93.2 1.5 %reshape.104 = bf16[16,16,16,32]{3,2,1,0:T(8,128)(2,1)} reshape(bf16[16,2,4096]{2,1,0:T(2,128)(2,1)S(1)} %all-to-all-done.2) | data formatting | bytes 524288
  94.7 2.4 %copy.67 = bf16[32,16,256]{2,1,0:T(8,128)(2,1)S(1)} copy(bf16[32,16,256]{0,1,2:T(8,128)(2,1)} %bitcast.96) | data formatting | bytes 524288 | tf_op jit(solution)/shard_map/squeeze | solution.py:146
  97.1 3.4 %fusion.2 = bf16[32,16,1024]{2,1,0:T(8,128)(2,1)} fusion(f32[32,16,1024]{2,0,1:T(8,128)S(1)} %fusion.55, bf16[32,16,1024]{2,1,0:T(8,128)(2,1)S(1)} %copy-done.1, bf16[32,16,256]{2,1,0:T(8,128)(2,1)S(1)} %copy.67, bf16[256,2044]{1,0:T(8,128)(2,1)} %copy-done.2), kind=kOutput, calls=%fused_computation.3 | convolution fusion | flops 271056896 | bytes 4980736 | tf_op jit(solution)/shard_map/qrj,jc->qrc/dot_general | solution.py:147
  100.6 2.1 %reshape.106 = bf16[16,14,16,64]{3,2,1,0:T(8,128)(2,1)S(1)} reshape(bf16[16,2,7168]{2,1,0:T(2,128)(2,1)} %all-to-all-done.3) | data formatting | bytes 917504
  (64 shorter events, 19.2 us)
Async XLA Ops:
  0.6 27.7 %copy-start = (bf16[224,32]{0,1:T(8,128)(2,1)S(1)}, bf16[224,32]{0,1:T(8,128)(2,1)}, u32[]{:S(2)}) copy-start(bf16[224,32]{0,1:T(8,128)(2,1)} %param.6) | copy-start | bytes 43012
  3.5 16.0 %all-to-all-start = ((bf16[16,2,7168]{2,1,0:T(2,128)(2,1)}), bf16[16,2,7168]{2,1,0:T(2,128)(2,1)}, u32[]{:S(2)}, u32[]{:S(2)}) async-start(bf16[16,2,7168]{2,1,0:T(2,128)(2,1)} %reshape.99), calls=%async_computation | async-start | bytes 917504 | tf_op jit(solution)/shard_map/all_to_all | solution.py:86
  12.7 8.9 %copy-start.1 = (bf16[32,16,1024]{2,1,0:T(8,128)(2,1)S(1)}, bf16[32,16,1024]{2,1,0:T(8,128)(2,1)}, u32[]{:S(2)}) copy-start(bf16[32,16,1024]{2,1,0:T(8,128)(2,1)} %param.5) | copy-start | bytes 3145732
  14.4 1.0 copy-start.2
  24.8 11.6 %all-to-all-start.1 = ((bf16[16,2,4096]{2,1,0:T(2,128)(2,1)}), bf16[16,2,4096]{2,1,0:T(2,128)(2,1)S(1)}, u32[]{:S(2)}, u32[]{:S(2)}) async-start(bf16[16,2,4096]{2,1,0:T(2,128)(2,1)} %reshape.101), calls=%async_computation.1 | async-start | bytes 524288 | tf_op jit(solution)/shard_map/all_to_all | solution.py:97
  36.8 3.1 %copy-start.3 = (f32[32,16,32]{2,1,0:T(8,128)S(1)}, f32[32,16,32]{2,1,0:T(8,128)}, u32[]{:S(2)}) copy-start(f32[32,16,32]{2,1,0:T(8,128)} %copy.77) | copy-start | bytes 196612
  40.8 17.0 %collective-permute-start.1 = (f32[32,16,96]{2,1,0:T(8,128)}, f32[32,16,96]{2,1,0:T(8,128)S(1)}, u32[]{:S(2)}, u32[]{:S(2)}) collective-permute-start(f32[32,16,96]{2,1,0:T(8,128)} %pad_maximum_fusion.1), channel_id=1, source_target_pairs={{16,0},{32,16},{48,32},{64,48},{80,64},{96,80},{112,96},{128,112},... | collective-permute-start | bytes 589832 | tf_op jit(solution)/shard_map/ppermute | solution.py:114
  48.4 17.7 %collective-permute-start = (f32[32,16,96]{2,1,0:T(8,128)S(1)}, f32[32,16,96]{2,1,0:T(8,128)S(1)}, u32[]{:S(2)}, u32[]{:S(2)}) collective-permute-start(f32[32,16,96]{2,1,0:T(8,128)S(1)} %pad_maximum_fusion), channel_id=1, source_target_pairs={{0,16},{16,32},{32,48},{48,64},{64,80},{80,96},{96,112},{112,128},... | collective-permute-start | bytes 589832 | tf_op jit(solution)/shard_map/ppermute | solution.py:113
  52.0 14.6 %copy-start.6 = (f32[32,32,1]{1,0,2:T(8,128)S(1)}, f32[32,32,1]{1,0,2:T(8,128)}, u32[]{:S(2)}) copy-start(f32[32,32,1]{1,0,2:T(8,128)} %convolution_bitcast_fusion.1) | copy-start | bytes 12292
  68.3 0.9 copy-start.4
  70.2 8.0 %copy-start.7 = (bf16[8,224]{1,0:T(8,128)(2,1)S(1)}, bf16[8,224]{1,0:T(8,128)(2,1)}, u32[]{:S(2)}) copy-start(bf16[8,224]{1,0:T(8,128)(2,1)} %param.7) | copy-start | bytes 10756
  74.5 16.1 %copy-start.5 = (bf16[8,16,1024]{2,1,0:T(8,128)(2,1)S(1)}, bf16[8,16,1024]{2,1,0:T(8,128)(2,1)}, u32[]{:S(2)}) copy-start(bf16[8,16,1024]{2,1,0:T(8,128)(2,1)} %param.9) | copy-start | bytes 786436
  74.5 11.7 %all-to-all-start.2 = ((bf16[16,2,4096]{2,1,0:T(2,128)(2,1)}), bf16[16,2,4096]{2,1,0:T(2,128)(2,1)S(1)}, u32[]{:S(2)}, u32[]{:S(2)}) async-start(bf16[16,2,4096]{2,1,0:T(2,128)(2,1)} %reshape.103), calls=%async_computation.2 | async-start | bytes 524288 | tf_op jit(solution)/shard_map/all_to_all | solution.py:146
  86.2 14.4 %all-to-all-start.3 = ((bf16[16,2,7168]{2,1,0:T(2,128)(2,1)}), bf16[16,2,7168]{2,1,0:T(2,128)(2,1)}, u32[]{:S(2)}, u32[]{:S(2)}) async-start(bf16[16,2,7168]{2,1,0:T(2,128)(2,1)} %reshape.105), calls=%async_computation.3 | async-start | bytes 917504 | tf_op jit(solution)/shard_map/all_to_all | solution.py:151

commit v13 on v11

--- a/solution.py
+++ b/solution.py
@@ -139,8 +139,9 @@
         tile_index < ends, lax.slice_in_dim(resid_rim, rim, 2 * rim, axis=2), 0.0
     )
     coef_wide = jnp.concatenate([rim_prev, coef_resid, rim_next], axis=2)
-    rows_back = split_dot("qjk,kr->qjr", coef_wide, own_rows).astype(bf16)
-    back_split = rows_back.reshape(subspace, chunk, n_spec, rows_here).transpose(2, 0, 3, 1)
+    back_split = split_dot(
+        "qjk,ksr->sqrj", coef_wide, own_rows.reshape(wide_rows, n_spec, rows_here)
+    ).astype(bf16)
     rows_pixel = lax.all_to_all(back_split, "spec", split_axis=0, concat_axis=3, tiled=True)[0]
     grad_hs = jnp.einsum("qrj,jc->qrc", rows_pixel, column_t, preferred_element_type=f32)
 

time: 102 us -> 101 us (level)
  local copies, waits for them, and re-layouts: 26.3 us -> 23.3 us
  waiting for transfers between devices: 33.3 us -> 35.9 us
    all_to_all x1, waiting for transfers between devices: 0.03 us -> 1.5 us  [shards(): lax.all_to_all(resid_split, 'spec', split_axis=0, concat_axis=2, tiled=True)]
    unnamed x30 -> x28, local copies, waits for them, and re-layouts: 15.2 us -> 13.9 us
    all_to_all x1, waiting for transfers between devices: 5.81 us -> 7.08 us  [shards(): lax.all_to_all(back_split, 'spec', split_axis=0, concat_axis=3, tiled=True)]
    transpose x1 -> x0, local copies, waits for them, and re-layouts: 1.25 us -> none  [shards(): rows_back.reshape(subspace, chunk, n_spec, rows_here).transpose(2, 0, 3, 1)]
  transfers between devices with their start and end apart: 6 -> 6, of which waited for: 5 -> 6; matrix products, arithmetic and copies ran while one was open for 18% -> 16% of each run, Pallas kernels for 0% -> 0%
where the time goes in v13:
time: 101 us; the launch traced here: 100 us
  waiting for transfers between devices  35.9 us (36%)
  starting transfers between devices  26.9 us (27%)
  local copies, waits for them, and re-layouts  23.3 us (23%)
  matrix products  10.7 us (11%)
  other arithmetic  1.81 us (2%)
  between operations  1.81 us (2%)
    unnamed x28, local copies, waits for them, and re-layouts  13.9 us
    ppermute x1, waiting for transfers between devices, shards(): got_next = lax.ppermute(to_prev, 'tile', [(i + 1, i) for i in range(ends)])  8.03 us
    ppermute x1, starting transfers between devices, shards(): got_next = lax.ppermute(to_prev, 'tile', [(i + 1, i) for i in range(ends)])  7.49 us
    ppermute x1, waiting for transfers between devices, shards(): got_prev = lax.ppermute(to_next, 'tile', [(i, i + 1) for i in range(ends)])  7.4 us
    all_to_all x1, waiting for transfers between devices, shards(): lax.all_to_all(back_split, 'spec', split_axis=0, concat_axis=3, tiled=True)  7.08 us
    all_to_all x1, waiting for transfers between devices, shards(): lax.all_to_all(obs_split, 'spec', split_axis=0, concat_axis=1, tiled=True)  6.76 us
    all_to_all x1, starting transfers between devices, shards(): lax.all_to_all(cols_done, 'spec', split_axis=0, concat_axis=3, tiled=True)  5.76 us
    all_to_all x1, waiting for transfers between devices, shards(): lax.all_to_all(cols_done, 'spec', split_axis=0, concat_axis=3, tiled=True)  5.15 us
  transfers between devices with their start and end apart: 6, of which 6 were waited for; matrix products, arithmetic and copies ran while one was open for 16% of the time, Pallas kernels for 0%

profile of v13, /device:TPU:24, one launch (start us, length us, event | category | flops | bytes accessed | tf_op | source)
XLA Modules:
  0.0 100.4 jit_solution(10893480399552089437)
XLA Ops:
  2.6 1.7 %reshape.88 = bf16[256,2044]{1,0:T(8,128)(2,1)S(1)} reshape(bf16[523264]{0:T(1024)(128)(2,1)S(1)} %slice.70) | data formatting | bytes 2093056 | tf_op jit(solution)/shard_map/reshape | solution.py:55
  4.3 1.4 %fusion.55 = bf16[16,16,16,32]{3,2,1,0:T(8,128)(2,1)S(1)} fusion(bf16[16,16,1024,1]{2,1,3,0:T(8,128)(2,1)S(1)} %bitcast.119, bf16[32,16,1024]{2,1,0:T(8,128)(2,1)S(1)} %copy-done.1), kind=kOutput, calls=%fused_computation.84 | convolution fusion | flops 268566528 | bytes 1835008 | tf_op jit(solution)/shard_map/qrc,sjc->sqjr/dot_general | solution.py:85
  5.8 1.7 %reshape.104 = bf16[16,2,4096]{2,1,0:T(2,128)(2,1)} reshape(bf16[16,16,16,32]{3,2,1,0:T(8,128)(2,1)S(1)} %fusion.55) | data formatting | bytes 524288
  7.4 5.8 %all-to-all-start = ((bf16[16,2,4096]{2,1,0:T(2,128)(2,1)}), bf16[16,2,4096]{2,1,0:T(2,128)(2,1)S(1)}, u32[]{:S(2)}, u32[]{:S(2)}) async-start(bf16[16,2,4096]{2,1,0:T(2,128)(2,1)} %reshape.104), calls=%async_computation | async-start | bytes 524288 | tf_op jit(solution)/shard_map/all_to_all | solution.py:91
  13.2 1.4 %copy.48 = bf16[14,64,256]{1,2,0:T(8,128)(2,1)S(1)} copy(bf16[14,64,256]{2,1,0:T(8,128)(2,1)} %param.8) | data formatting | bytes 917504 | tf_op args[3]
  14.8 1.3 %reshape.102 = bf16[16,2,7168]{2,1,0:T(2,128)(2,1)} reshape(bf16[16,14,16,64]{3,2,1,0:T(8,128)(2,1)S(1)} %copy.49) | data formatting | bytes 917504
  16.1 5.2 %all-to-all-done = bf16[16,2,4096]{2,1,0:T(2,128)(2,1)S(1)} async-done(((bf16[16,2,4096]{2,1,0:T(2,128)(2,1)}), bf16[16,2,4096]{2,1,0:T(2,128)(2,1)S(1)}, u32[]{:S(2)}, u32[]{:S(2)}) %all-to-all-start) | async-done | bytes 262176 | tf_op jit(solution)/shard_map/all_to_all | solution.py:91
  21.3 3.6 %all-to-all-start.1 = ((bf16[16,2,7168]{2,1,0:T(2,128)(2,1)}), bf16[16,2,7168]{2,1,0:T(2,128)(2,1)S(1)}, u32[]{:S(2)}, u32[]{:S(2)}) async-start(bf16[16,2,7168]{2,1,0:T(2,128)(2,1)} %reshape.102), calls=%async_computation.1 | async-start | bytes 917504 | tf_op jit(solution)/shard_map/all_to_all | solution.py:94
  28.2 6.8 %all-to-all-done.1 = bf16[16,2,7168]{2,1,0:T(2,128)(2,1)S(1)} async-done(((bf16[16,2,7168]{2,1,0:T(2,128)(2,1)}), bf16[16,2,7168]{2,1,0:T(2,128)(2,1)S(1)}, u32[]{:S(2)}, u32[]{:S(2)}) %all-to-all-start.1) | async-done | bytes 458784 | tf_op jit(solution)/shard_map/all_to_all | solution.py:94
  37.1 7.5 %collective-permute-start.1 = (f32[32,16,96]{2,1,0:T(8,128)S(1)}, f32[32,16,96]{2,1,0:T(8,128)S(1)}, u32[]{:S(2)}, u32[]{:S(2)}) collective-permute-start(f32[32,16,96]{2,1,0:T(8,128)S(1)} %pad_maximum_fusion.1), channel_id=1, source_target_pairs={{16,0},{32,16},{48,32},{64,48},{80,64},{96,80},{112,96},{128,112},... | collective-permute-start | bytes 589832 | tf_op jit(solution)/shard_map/ppermute | solution.py:112
  44.9 2.1 %collective-permute-start = (f32[32,16,96]{2,1,0:T(8,128)S(1)}, f32[32,16,96]{2,1,0:T(8,128)S(1)}, u32[]{:S(2)}, u32[]{:S(2)}) collective-permute-start(f32[32,16,96]{2,1,0:T(8,128)S(1)} %pad_maximum_fusion), channel_id=1, source_target_pairs={{0,16},{16,32},{32,48},{48,64},{64,80},{80,96},{96,112},{112,128},... | collective-permute-start | bytes 589832 | tf_op jit(solution)/shard_map/ppermute | solution.py:111
  47.2 8.0 %collective-permute-done.1 = f32[32,16,96]{2,1,0:T(8,128)S(1)} collective-permute-done((f32[32,16,96]{2,1,0:T(8,128)S(1)}, f32[32,16,96]{2,1,0:T(8,128)S(1)}, u32[]{:S(2)}, u32[]{:S(2)}) %collective-permute-start.1) | collective-permute-done | bytes 196640 | tf_op jit(solution)/shard_map/ppermute | solution.py:112
  55.3 7.4 %collective-permute-done = f32[32,16,96]{2,1,0:T(8,128)S(1)} collective-permute-done((f32[32,16,96]{2,1,0:T(8,128)S(1)}, f32[32,16,96]{2,1,0:T(8,128)S(1)}, u32[]{:S(2)}, u32[]{:S(2)}) %collective-permute-start) | collective-permute-done | bytes 196640 | tf_op jit(solution)/shard_map/ppermute | solution.py:111
  66.6 1.7 %reshape.106 = bf16[16,2,4096]{2,1,0:T(2,128)(2,1)} reshape(bf16[16,16,16,32]{3,2,1,0:T(8,128)(2,1)S(1)} %fusion.58) | data formatting | bytes 524288
  68.3 3.5 %all-to-all-start.2 = ((bf16[16,2,4096]{2,1,0:T(2,128)(2,1)}), bf16[16,2,4096]{2,1,0:T(2,128)(2,1)S(1)}, u32[]{:S(2)}, u32[]{:S(2)}) async-start(bf16[16,2,4096]{2,1,0:T(2,128)(2,1)} %reshape.106), calls=%async_computation.2 | async-start | bytes 524288 | tf_op jit(solution)/shard_map/all_to_all | solution.py:145
  72.8 7.1 %all-to-all-done.2 = bf16[16,2,4096]{2,1,0:T(2,128)(2,1)S(1)} async-done(((bf16[16,2,4096]{2,1,0:T(2,128)(2,1)}), bf16[16,2,4096]{2,1,0:T(2,128)(2,1)S(1)}, u32[]{:S(2)}, u32[]{:S(2)}) %all-to-all-start.2) | async-done | bytes 262176 | tf_op jit(solution)/shard_map/all_to_all | solution.py:145
  79.9 1.5 %reshape.107 = bf16[16,16,16,32]{3,2,1,0:T(8,128)(2,1)} reshape(bf16[16,2,4096]{2,1,0:T(2,128)(2,1)S(1)} %all-to-all-done.2) | data formatting | bytes 524288
  81.4 1.3 %reshape.108 = bf16[16,2,7168]{2,1,0:T(2,128)(2,1)} reshape(bf16[16,14,16,64]{3,2,1,0:T(8,128)(2,1)S(1)} %bitcast.112) | data formatting | bytes 917504
  82.6 4.4 %all-to-all-start.3 = ((bf16[16,2,7168]{2,1,0:T(2,128)(2,1)}), bf16[16,2,7168]{2,1,0:T(2,128)(2,1)}, u32[]{:S(2)}, u32[]{:S(2)}) async-start(bf16[16,2,7168]{2,1,0:T(2,128)(2,1)} %reshape.108), calls=%async_computation.3 | async-start | bytes 917504 | tf_op jit(solution)/shard_map/all_to_all | solution.py:150
  87.1 1.6 %fusion.8 = bf16[8,16,1024]{2,0,1:T(8,128)(2,1)S(1)} fusion(f32[8,32,1]{1,0,2:T(8,128)S(1)} %convolution_bitcast_fusion.2, bf16[32,16,1024]{2,1,0:T(8,128)(2,1)S(1)} %copy-done.1, bf16[8,16,1024]{2,1,0:T(8,128)(2,1)S(1)} %copy-done.5), kind=kOutput, calls=%fused_computation.13 | convolution fusion | flops 50724864 | bytes 1573888 | tf_op jit(solution)/shard_map/mq,qrc->mrc/dot_general | solution.py:154
  89.7 2.4 %copy.60 = bf16[32,16,256]{2,1,0:T(8,128)(2,1)S(1)} copy(bf16[32,16,256]{0,1,2:T(8,128)(2,1)} %bitcast.106) | data formatting | bytes 524288 | tf_op jit(solution)/shard_map/squeeze | solution.py:145
  92.1 3.4 %fusion.2 = bf16[32,16,1024]{2,1,0:T(8,128)(2,1)} fusion(f32[32,16,1024]{2,0,1:T(8,128)S(1)} %fusion.61, bf16[32,16,1024]{2,1,0:T(8,128)(2,1)S(1)} %copy-done.1, bf16[32,16,256]{2,1,0:T(8,128)(2,1)S(1)} %copy.60, bf16[256,2044]{1,0:T(8,128)(2,1)} %copy-done.2), kind=kOutput, calls=%fused_computation.3 | convolution fusion | flops 271056896 | bytes 4980736 | tf_op jit(solution)/shard_map/qrj,jc->qrc/dot_general | solution.py:146
  95.5 1.5 %all-to-all-done.3 = bf16[16,2,7168]{2,1,0:T(2,128)(2,1)} async-done(((bf16[16,2,7168]{2,1,0:T(2,128)(2,1)}), bf16[16,2,7168]{2,1,0:T(2,128)(2,1)}, u32[]{:S(2)}, u32[]{:S(2)}) %all-to-all-start.3) | async-done | bytes 458784 | tf_op jit(solution)/shard_map/all_to_all | solution.py:150
  97.0 2.1 %reshape.109 = bf16[16,14,16,64]{3,2,1,0:T(8,128)(2,1)S(1)} reshape(bf16[16,2,7168]{2,1,0:T(2,128)(2,1)} %all-to-all-done.3) | data formatting | bytes 917504
  (62 shorter events, 14.4 us)
Async XLA Ops:
  0.6 35.6 %copy-start = (bf16[224,32]{0,1:T(8,128)(2,1)S(1)}, bf16[224,32]{0,1:T(8,128)(2,1)}, u32[]{:S(2)}) copy-start(bf16[224,32]{0,1:T(8,128)(2,1)} %param.6) | copy-start | bytes 43012
  2.5 1.8 %copy-start.1 = (bf16[32,16,1024]{2,1,0:T(8,128)(2,1)S(1)}, bf16[32,16,1024]{2,1,0:T(8,128)(2,1)}, u32[]{:S(2)}) copy-start(bf16[32,16,1024]{2,1,0:T(8,128)(2,1)} %param.5) | copy-start | bytes 3145732
  4.3 1.5 %copy-start.2 = (bf16[256,2044]{1,0:T(8,128)(2,1)}, bf16[256,2044]{1,0:T(8,128)(2,1)S(1)}, u32[]{:S(2)}) copy-start(bf16[256,2044]{1,0:T(8,128)(2,1)S(1)} %reshape.88) | copy-start | bytes 3139588
  7.4 13.8 %all-to-all-start = ((bf16[16,2,4096]{2,1,0:T(2,128)(2,1)}), bf16[16,2,4096]{2,1,0:T(2,128)(2,1)S(1)}, u32[]{:S(2)}, u32[]{:S(2)}) async-start(bf16[16,2,4096]{2,1,0:T(2,128)(2,1)} %reshape.104), calls=%async_computation | async-start | bytes 524288 | tf_op jit(solution)/shard_map/all_to_all | solution.py:91
  21.3 13.7 %all-to-all-start.1 = ((bf16[16,2,7168]{2,1,0:T(2,128)(2,1)}), bf16[16,2,7168]{2,1,0:T(2,128)(2,1)S(1)}, u32[]{:S(2)}, u32[]{:S(2)}) async-start(bf16[16,2,7168]{2,1,0:T(2,128)(2,1)} %reshape.102), calls=%async_computation.1 | async-start | bytes 917504 | tf_op jit(solution)/shard_map/all_to_all | solution.py:94
  25.6 9.9 %copy-start.4 = (bf16[128,764]{1,0:T(8,128)(2,1)}, bf16[128,764]{1,0:T(8,128)(2,1)S(1)}, u32[]{:S(2)}) copy-start(bf16[128,764]{1,0:T(8,128)(2,1)S(1)} %reshape.86) | copy-start | bytes 586756
  35.5 1.4 %copy-start.3 = (f32[32,16,64]{2,1,0:T(8,128)S(1)}, f32[32,16,64]{2,1,0:T(8,128)}, u32[]{:S(2)}) copy-start(f32[32,16,64]{2,1,0:T(8,128)} %get-tuple-element.15) | copy-start | bytes 393220
  36.6 10.4 %slice-start = ((bf16[128,764]{1,0:T(8,128)(2,1)}), bf16[128,256]{1,0:T(8,128)(2,1)S(1)}, s32[]{:S(2)}) async-start(bf16[128,764]{1,0:T(8,128)(2,1)} %copy-done.4), calls=%async_computation.4 | async-start | bytes 131072 | tf_op jit(solution)/shard_map/slice | solution.py:55
  37.1 18.2 %collective-permute-start.1 = (f32[32,16,96]{2,1,0:T(8,128)S(1)}, f32[32,16,96]{2,1,0:T(8,128)S(1)}, u32[]{:S(2)}, u32[]{:S(2)}) collective-permute-start(f32[32,16,96]{2,1,0:T(8,128)S(1)} %pad_maximum_fusion.1), channel_id=1, source_target_pairs={{16,0},{32,16},{48,32},{64,48},{80,64},{96,80},{112,96},{128,112},... | collective-permute-start | bytes 589832 | tf_op jit(solution)/shard_map/ppermute | solution.py:112
  44.9 17.8 %collective-permute-start = (f32[32,16,96]{2,1,0:T(8,128)S(1)}, f32[32,16,96]{2,1,0:T(8,128)S(1)}, u32[]{:S(2)}, u32[]{:S(2)}) collective-permute-start(f32[32,16,96]{2,1,0:T(8,128)S(1)} %pad_maximum_fusion), channel_id=1, source_target_pairs={{0,16},{16,32},{32,48},{48,64},{64,80},{80,96},{96,112},{112,128},... | collective-permute-start | bytes 589832 | tf_op jit(solution)/shard_map/ppermute | solution.py:111
  66.1 5.8 %copy-start.6 = (bf16[8,224]{1,0:T(8,128)(2,1)S(1)}, bf16[8,224]{1,0:T(8,128)(2,1)}, u32[]{:S(2)}) copy-start(bf16[8,224]{1,0:T(8,128)(2,1)} %param.7) | copy-start | bytes 10756
  68.3 11.6 %all-to-all-start.2 = ((bf16[16,2,4096]{2,1,0:T(2,128)(2,1)}), bf16[16,2,4096]{2,1,0:T(2,128)(2,1)S(1)}, u32[]{:S(2)}, u32[]{:S(2)}) async-start(bf16[16,2,4096]{2,1,0:T(2,128)(2,1)} %reshape.106), calls=%async_computation.2 | async-start | bytes 524288 | tf_op jit(solution)/shard_map/all_to_all | solution.py:145
  72.8 14.3 %copy-start.5 = (bf16[8,16,1024]{2,1,0:T(8,128)(2,1)S(1)}, bf16[8,16,1024]{2,1,0:T(8,128)(2,1)}, u32[]{:S(2)}) copy-start(bf16[8,16,1024]{2,1,0:T(8,128)(2,1)} %param.9) | copy-start | bytes 786436
  82.6 14.4 %all-to-all-start.3 = ((bf16[16,2,7168]{2,1,0:T(2,128)(2,1)}), bf16[16,2,7168]{2,1,0:T(2,128)(2,1)}, u32[]{:S(2)}, u32[]{:S(2)}) async-start(bf16[16,2,7168]{2,1,0:T(2,128)(2,1)} %reshape.108), calls=%async_computation.3 | async-start | bytes 917504 | tf_op jit(solution)/shard_map/all_to_all | solution.py:150

commit v14 on v13

--- a/solution.py
+++ b/solution.py
@@ -92,6 +92,10 @@
 
     obs_split = hyper_obs.reshape(group, coarse_rows, n_spec, chunk).transpose(2, 0, 3, 1)
     obs_cols = lax.all_to_all(obs_split, "spec", split_axis=0, concat_axis=1, tiled=True)[0]
+    resp_basis = jnp.dot(response.astype(f32), basis_wide, precision=highest)
+    multi_pred = jnp.einsum("mq,qrc->mrc", resp_basis, latent.astype(f32), precision=highest)
+    multi_resid = (multi_pred - multi_obs.astype(f32)).astype(bf16)
+    multi_resid, obs_cols = lax.optimization_barrier((multi_resid, obs_cols))
     obs_proj = jnp.einsum("bq,bji->qji", basis, obs_cols, preferred_element_type=f32)
 
     own_part = jnp.einsum("qjr,er->qje", tile_rows, own_rows, preferred_element_type=f32)
@@ -150,9 +154,6 @@
     resid_bands = lax.all_to_all(resid_split, "spec", split_axis=0, concat_axis=2, tiled=True)[0]
     hs_residual = resid_bands.transpose(0, 2, 1)
 
-    resp_basis = jnp.dot(response.astype(f32), basis_wide, precision=highest)
-    multi_pred = jnp.einsum("mq,qrc->mrc", resp_basis, latent.astype(f32), precision=highest)
-    multi_resid = (multi_pred - multi_obs.astype(f32)).astype(bf16)
     grad_ms = jnp.einsum(
         "mq,mrc->qrc", resp_basis, multi_resid.astype(f32), precision=highest
     )

time: 101 us -> 101 us (level)
  matrix products: 10.7 us -> 12.4 us
  waiting for transfers between devices: 35.9 us -> 34.4 us
    all_to_all x1, waiting for transfers between devices: 6.76 us -> 4.14 us  [shards(): lax.all_to_all(obs_split, 'spec', split_axis=0, concat_axis=1, tiled=True)]
    all_to_all x1, waiting for transfers between devices: 1.5 us -> 3.28 us  [shards(): lax.all_to_all(resid_split, 'spec', split_axis=0, concat_axis=2, tiled=True)]
    dot_general x1, matrix products: 1.56 us -> 3.23 us  [shards(): jnp.einsum('mq,qrc->mrc', resp_basis, latent.astype(f32), precision=highest)]
    unnamed x28 -> x30, local copies, waits for them, and re-layouts: 13.9 us -> 13.6 us
  transfers between devices with their start and end apart: 6 -> 6, of which waited for: 6 -> 6; matrix products, arithmetic and copies ran while one was open for 16% -> 18% of each run, Pallas kernels for 0% -> 0%
where the time goes in v14:
time: 101 us; the launch traced here: 100 us
  waiting for transfers between devices  34.4 us (34%)
  starting transfers between devices  26.7 us (26%)
  local copies, waits for them, and re-layouts  23.2 us (23%)
  matrix products  12.4 us (12%)
  between operations  1.83 us (2%)
  other arithmetic  1.81 us (2%)
    unnamed x30, local copies, waits for them, and re-layouts  13.6 us
    ppermute x1, waiting for transfers between devices, shards(): got_next = lax.ppermute(to_prev, 'tile', [(i + 1, i) for i in range(ends)])  8.2 us
    ppermute x1, starting transfers between devices, shards(): got_next = lax.ppermute(to_prev, 'tile', [(i + 1, i) for i in range(ends)])  7.49 us
    ppermute x1, waiting for transfers between devices, shards(): got_prev = lax.ppermute(to_next, 'tile', [(i, i + 1) for i in range(ends)])  7.23 us
    all_to_all x1, waiting for transfers between devices, shards(): lax.all_to_all(back_split, 'spec', split_axis=0, concat_axis=3, tiled=True)  7.21 us
    all_to_all x1, starting transfers between devices, shards(): lax.all_to_all(cols_done, 'spec', split_axis=0, concat_axis=3, tiled=True)  5.76 us
    all_to_all x1, waiting for transfers between devices, shards(): lax.all_to_all(cols_done, 'spec', split_axis=0, concat_axis=3, tiled=True)  4.31 us
    all_to_all x1, starting transfers between devices, shards(): lax.all_to_all(resid_split, 'spec', split_axis=0, concat_axis=2, tiled=True)  4.22 us
  transfers between devices with their start and end apart: 6, of which 6 were waited for; matrix products, arithmetic and copies ran while one was open for 18% of the time, Pallas kernels for 0%

profile of v14, /device:TPU:24, one launch (start us, length us, event | category | flops | bytes accessed | tf_op | source)
XLA Modules:
  0.0 100.2 jit_solution(10661442841546105906)
XLA Ops:
  2.6 1.7 %reshape.88 = bf16[256,2044]{1,0:T(8,128)(2,1)S(1)} reshape(bf16[523264]{0:T(1024)(128)(2,1)S(1)} %slice.70) | data formatting | bytes 2093056 | tf_op jit(solution)/shard_map/reshape | solution.py:55
  4.3 1.4 %fusion.55 = bf16[16,16,16,32]{3,2,1,0:T(8,128)(2,1)S(1)} fusion(bf16[16,16,1024,1]{2,1,3,0:T(8,128)(2,1)S(1)} %bitcast.123, bf16[32,16,1024]{2,1,0:T(8,128)(2,1)S(1)} %copy-done.1), kind=kOutput, calls=%fused_computation.85 | convolution fusion | flops 268566528 | bytes 1835008 | tf_op jit(solution)/shard_map/qrc,sjc->sqjr/dot_general | solution.py:85
  5.8 1.7 %reshape.104 = bf16[16,2,4096]{2,1,0:T(2,128)(2,1)} reshape(bf16[16,16,16,32]{3,2,1,0:T(8,128)(2,1)S(1)} %fusion.55) | data formatting | bytes 524288
  7.4 5.8 %all-to-all-start = ((bf16[16,2,4096]{2,1,0:T(2,128)(2,1)}), bf16[16,2,4096]{2,1,0:T(2,128)(2,1)S(1)}, u32[]{:S(2)}, u32[]{:S(2)}) async-start(bf16[16,2,4096]{2,1,0:T(2,128)(2,1)} %reshape.104), calls=%async_computation | async-start | bytes 524288 | tf_op jit(solution)/shard_map/all_to_all | solution.py:91
  14.0 1.5 %copy.50 = bf16[14,64,256]{1,2,0:T(8,128)(2,1)S(1)} copy(bf16[14,64,256]{2,1,0:T(8,128)(2,1)} %param.8) | data formatting | bytes 917504 | tf_op args[3]
  15.7 1.3 %reshape.102 = bf16[16,2,7168]{2,1,0:T(2,128)(2,1)} reshape(bf16[16,14,16,64]{3,2,1,0:T(8,128)(2,1)S(1)} %copy.51) | data formatting | bytes 917504
  17.0 4.3 %all-to-all-done = bf16[16,2,4096]{2,1,0:T(2,128)(2,1)S(1)} async-done(((bf16[16,2,4096]{2,1,0:T(2,128)(2,1)}), bf16[16,2,4096]{2,1,0:T(2,128)(2,1)S(1)}, u32[]{:S(2)}, u32[]{:S(2)}) %all-to-all-start) | async-done | bytes 262176 | tf_op jit(solution)/shard_map/all_to_all | solution.py:91
  21.3 3.6 %all-to-all-start.1 = ((bf16[16,2,7168]{2,1,0:T(2,128)(2,1)}), bf16[16,2,7168]{2,1,0:T(2,128)(2,1)S(1)}, u32[]{:S(2)}, u32[]{:S(2)}) async-start(bf16[16,2,7168]{2,1,0:T(2,128)(2,1)} %reshape.102), calls=%async_computation.1 | async-start | bytes 917504 | tf_op jit(solution)/shard_map/all_to_all | solution.py:94
  25.0 3.2 %fusion.8 = bf16[8,16,1024]{2,0,1:T(8,128)(2,1)} fusion(f32[8,32,1]{1,0,2:T(8,128)S(1)} %convolution_bitcast_fusion.2, bf16[32,16,1024]{2,1,0:T(8,128)(2,1)S(1)} %copy-done.1, bf16[8,16,1024]{2,1,0:T(8,128)(2,1)} %param.9), kind=kOutput, calls=%fused_computation.13 | convolution fusion | flops 50724864 | bytes 1573888 | tf_op jit(solution)/shard_map/mq,qrc->mrc/dot_general | solution.py:96
  30.8 4.1 %all-to-all-done.1 = bf16[16,2,7168]{2,1,0:T(2,128)(2,1)S(1)} async-done(((bf16[16,2,7168]{2,1,0:T(2,128)(2,1)}), bf16[16,2,7168]{2,1,0:T(2,128)(2,1)S(1)}, u32[]{:S(2)}, u32[]{:S(2)}) %all-to-all-start.1) | async-done | bytes 458784 | tf_op jit(solution)/shard_map/all_to_all | solution.py:94
  37.1 7.5 %collective-permute-start.1 = (f32[32,16,96]{2,1,0:T(8,128)S(1)}, f32[32,16,96]{2,1,0:T(8,128)S(1)}, u32[]{:S(2)}, u32[]{:S(2)}) collective-permute-start(f32[32,16,96]{2,1,0:T(8,128)S(1)} %pad_maximum_fusion.1), channel_id=1, source_target_pairs={{16,0},{32,16},{48,32},{64,48},{80,64},{96,80},{112,96},{128,112},... | collective-permute-start | bytes 589832 | tf_op jit(solution)/shard_map/ppermute | solution.py:116
  44.7 2.1 %collective-permute-start = (f32[32,16,96]{2,1,0:T(8,128)S(1)}, f32[32,16,96]{2,1,0:T(8,128)S(1)}, u32[]{:S(2)}, u32[]{:S(2)}) collective-permute-start(f32[32,16,96]{2,1,0:T(8,128)S(1)} %pad_maximum_fusion), channel_id=1, source_target_pairs={{0,16},{16,32},{32,48},{48,64},{64,80},{80,96},{96,112},{112,128},... | collective-permute-start | bytes 589832 | tf_op jit(solution)/shard_map/ppermute | solution.py:115
  47.1 8.2 %collective-permute-done.1 = f32[32,16,96]{2,1,0:T(8,128)S(1)} collective-permute-done((f32[32,16,96]{2,1,0:T(8,128)S(1)}, f32[32,16,96]{2,1,0:T(8,128)S(1)}, u32[]{:S(2)}, u32[]{:S(2)}) %collective-permute-start.1) | collective-permute-done | bytes 196640 | tf_op jit(solution)/shard_map/ppermute | solution.py:116
  55.3 7.2 %collective-permute-done = f32[32,16,96]{2,1,0:T(8,128)S(1)} collective-permute-done((f32[32,16,96]{2,1,0:T(8,128)S(1)}, f32[32,16,96]{2,1,0:T(8,128)S(1)}, u32[]{:S(2)}, u32[]{:S(2)}) %collective-permute-start) | collective-permute-done | bytes 196640 | tf_op jit(solution)/shard_map/ppermute | solution.py:115
  66.5 1.7 %reshape.106 = bf16[16,2,4096]{2,1,0:T(2,128)(2,1)} reshape(bf16[16,16,16,32]{3,2,1,0:T(8,128)(2,1)S(1)} %fusion.58) | data formatting | bytes 524288
  68.1 3.5 %all-to-all-start.2 = ((bf16[16,2,4096]{2,1,0:T(2,128)(2,1)}), bf16[16,2,4096]{2,1,0:T(2,128)(2,1)S(1)}, u32[]{:S(2)}, u32[]{:S(2)}) async-start(bf16[16,2,4096]{2,1,0:T(2,128)(2,1)} %reshape.106), calls=%async_computation.2 | async-start | bytes 524288 | tf_op jit(solution)/shard_map/all_to_all | solution.py:149
  72.5 7.2 %all-to-all-done.2 = bf16[16,2,4096]{2,1,0:T(2,128)(2,1)S(1)} async-done(((bf16[16,2,4096]{2,1,0:T(2,128)(2,1)}), bf16[16,2,4096]{2,1,0:T(2,128)(2,1)S(1)}, u32[]{:S(2)}, u32[]{:S(2)}) %all-to-all-start.2) | async-done | bytes 262176 | tf_op jit(solution)/shard_map/all_to_all | solution.py:149
  79.7 1.5 %reshape.107 = bf16[16,16,16,32]{3,2,1,0:T(8,128)(2,1)} reshape(bf16[16,2,4096]{2,1,0:T(2,128)(2,1)S(1)} %all-to-all-done.2) | data formatting | bytes 524288
  81.2 1.3 %reshape.108 = bf16[16,2,7168]{2,1,0:T(2,128)(2,1)} reshape(bf16[16,14,16,64]{3,2,1,0:T(8,128)(2,1)S(1)} %bitcast.115) | data formatting | bytes 917504
  82.4 4.2 %all-to-all-start.3 = ((bf16[16,2,7168]{2,1,0:T(2,128)(2,1)}), bf16[16,2,7168]{2,1,0:T(2,128)(2,1)}, u32[]{:S(2)}, u32[]{:S(2)}) async-start(bf16[16,2,7168]{2,1,0:T(2,128)(2,1)} %reshape.108), calls=%async_computation.3 | async-start | bytes 917504 | tf_op jit(solution)/shard_map/all_to_all | solution.py:154
  87.7 2.4 %copy.61 = bf16[32,16,256]{2,1,0:T(8,128)(2,1)S(1)} copy(bf16[32,16,256]{0,1,2:T(8,128)(2,1)} %bitcast.109) | data formatting | bytes 524288 | tf_op jit(solution)/shard_map/squeeze | solution.py:149
  90.1 3.4 %fusion.2 = bf16[32,16,1024]{2,1,0:T(8,128)(2,1)} fusion(f32[32,16,1024]{2,0,1:T(8,128)S(1)} %fusion.61, bf16[32,16,1024]{2,1,0:T(8,128)(2,1)S(1)} %copy-done.1, bf16[32,16,256]{2,1,0:T(8,128)(2,1)S(1)} %copy.61, bf16[256,2044]{1,0:T(8,128)(2,1)} %copy-done.2), kind=kOutput, calls=%fused_computation.3 | convolution fusion | flops 271056896 | bytes 4980736 | tf_op jit(solution)/shard_map/qrj,jc->qrc/dot_general | solution.py:150
  93.6 3.3 %all-to-all-done.3 = bf16[16,2,7168]{2,1,0:T(2,128)(2,1)} async-done(((bf16[16,2,7168]{2,1,0:T(2,128)(2,1)}), bf16[16,2,7168]{2,1,0:T(2,128)(2,1)}, u32[]{:S(2)}, u32[]{:S(2)}) %all-to-all-start.3) | async-done | bytes 458784 | tf_op jit(solution)/shard_map/all_to_all | solution.py:154
  96.8 2.1 %reshape.109 = bf16[16,14,16,64]{3,2,1,0:T(8,128)(2,1)S(1)} reshape(bf16[16,2,7168]{2,1,0:T(2,128)(2,1)} %all-to-all-done.3) | data formatting | bytes 917504
  (65 shorter events, 14.2 us)
Async XLA Ops:
  0.6 24.2 %copy-start = (bf16[224,32]{0,1:T(8,128)(2,1)S(1)}, bf16[224,32]{0,1:T(8,128)(2,1)}, u32[]{:S(2)}) copy-start(bf16[224,32]{0,1:T(8,128)(2,1)} %param.6) | copy-start | bytes 43012
  2.5 1.8 %copy-start.1 = (bf16[32,16,1024]{2,1,0:T(8,128)(2,1)S(1)}, bf16[32,16,1024]{2,1,0:T(8,128)(2,1)}, u32[]{:S(2)}) copy-start(bf16[32,16,1024]{2,1,0:T(8,128)(2,1)} %param.5) | copy-start | bytes 3145732
  4.3 1.5 %copy-start.2 = (bf16[256,2044]{1,0:T(8,128)(2,1)}, bf16[256,2044]{1,0:T(8,128)(2,1)S(1)}, u32[]{:S(2)}) copy-start(bf16[256,2044]{1,0:T(8,128)(2,1)S(1)} %reshape.88) | copy-start | bytes 3139588
  7.4 13.8 %all-to-all-start = ((bf16[16,2,4096]{2,1,0:T(2,128)(2,1)}), bf16[16,2,4096]{2,1,0:T(2,128)(2,1)S(1)}, u32[]{:S(2)}, u32[]{:S(2)}) async-start(bf16[16,2,4096]{2,1,0:T(2,128)(2,1)} %reshape.104), calls=%async_computation | async-start | bytes 524288 | tf_op jit(solution)/shard_map/all_to_all | solution.py:91
  14.0 15.8 %copy-start.5 = (bf16[128,764]{1,0:T(8,128)(2,1)}, bf16[128,764]{1,0:T(8,128)(2,1)S(1)}, u32[]{:S(2)}) copy-start(bf16[128,764]{1,0:T(8,128)(2,1)S(1)} %reshape.86) | copy-start | bytes 586756
  15.5 9.4 %copy-start.8 = (bf16[8,224]{1,0:T(8,128)(2,1)S(1)}, bf16[8,224]{1,0:T(8,128)(2,1)}, u32[]{:S(2)}) copy-start(bf16[8,224]{1,0:T(8,128)(2,1)} %param.7) | copy-start | bytes 10756
  21.3 13.7 %all-to-all-start.1 = ((bf16[16,2,7168]{2,1,0:T(2,128)(2,1)}), bf16[16,2,7168]{2,1,0:T(2,128)(2,1)S(1)}, u32[]{:S(2)}, u32[]{:S(2)}) async-start(bf16[16,2,7168]{2,1,0:T(2,128)(2,1)} %reshape.102), calls=%async_computation.1 | async-start | bytes 917504 | tf_op jit(solution)/shard_map/all_to_all | solution.py:94
  25.0 4.8 %copy-start.6 = (f32[8,32,1]{1,0,2:T(8,128)}, f32[8,32,1]{1,0,2:T(8,128)S(1)}, u32[]{:S(2)}) copy-start(f32[8,32,1]{1,0,2:T(8,128)S(1)} %convolution_bitcast_fusion.2) | copy-start | bytes 3076
  35.5 1.4 %copy-start.4 = (f32[32,16,64]{2,1,0:T(8,128)S(1)}, f32[32,16,64]{2,1,0:T(8,128)}, u32[]{:S(2)}) copy-start(f32[32,16,64]{2,1,0:T(8,128)} %get-tuple-element.19) | copy-start | bytes 393220
  36.3 10.6 %slice-start = ((bf16[128,764]{1,0:T(8,128)(2,1)}), bf16[128,256]{1,0:T(8,128)(2,1)S(1)}, s32[]{:S(2)}) async-start(bf16[128,764]{1,0:T(8,128)(2,1)} %copy-done.5), calls=%async_computation.4 | async-start | bytes 131072 | tf_op jit(solution)/shard_map/slice | solution.py:55
  37.1 18.2 %collective-permute-start.1 = (f32[32,16,96]{2,1,0:T(8,128)S(1)}, f32[32,16,96]{2,1,0:T(8,128)S(1)}, u32[]{:S(2)}, u32[]{:S(2)}) collective-permute-start(f32[32,16,96]{2,1,0:T(8,128)S(1)} %pad_maximum_fusion.1), channel_id=1, source_target_pairs={{16,0},{32,16},{48,32},{64,48},{80,64},{96,80},{112,96},{128,112},... | collective-permute-start | bytes 589832 | tf_op jit(solution)/shard_map/ppermute | solution.py:116
  44.7 17.8 %collective-permute-start = (f32[32,16,96]{2,1,0:T(8,128)S(1)}, f32[32,16,96]{2,1,0:T(8,128)S(1)}, u32[]{:S(2)}, u32[]{:S(2)}) collective-permute-start(f32[32,16,96]{2,1,0:T(8,128)S(1)} %pad_maximum_fusion), channel_id=1, source_target_pairs={{0,16},{16,32},{32,48},{48,64},{64,80},{80,96},{96,112},{112,128},... | collective-permute-start | bytes 589832 | tf_op jit(solution)/shard_map/ppermute | solution.py:115
  68.1 11.6 %all-to-all-start.2 = ((bf16[16,2,4096]{2,1,0:T(2,128)(2,1)}), bf16[16,2,4096]{2,1,0:T(2,128)(2,1)S(1)}, u32[]{:S(2)}, u32[]{:S(2)}) async-start(bf16[16,2,4096]{2,1,0:T(2,128)(2,1)} %reshape.106), calls=%async_computation.2 | async-start | bytes 524288 | tf_op jit(solution)/shard_map/all_to_all | solution.py:149
  72.5 14.2 %copy-start.3 = (bf16[8,16,1024]{2,0,1:T(8,128)(2,1)S(1)}, bf16[8,16,1024]{2,0,1:T(8,128)(2,1)}, u32[]{:S(2)}) copy-start(bf16[8,16,1024]{2,0,1:T(8,128)(2,1)} %fusion.8) | copy-start | bytes 786436
  72.5 14.2 %copy-start.7 = (f32[8,32,1]{1,0,2:T(8,128)S(1)}, f32[8,32,1]{1,0,2:T(8,128)}, u32[]{:S(2)}) copy-start(f32[8,32,1]{1,0,2:T(8,128)} %copy-done.6) | copy-start | bytes 3076
  82.4 14.4 %all-to-all-start.3 = ((bf16[16,2,7168]{2,1,0:T(2,128)(2,1)}), bf16[16,2,7168]{2,1,0:T(2,128)(2,1)}, u32[]{:S(2)}, u32[]{:S(2)}) async-start(bf16[16,2,7168]{2,1,0:T(2,128)(2,1)} %reshape.108), calls=%async_computation.3 | async-start | bytes 917504 | tf_op jit(solution)/shard_map/all_to_all | solution.py:154

commit v15 on v14

--- a/solution.py
+++ b/solution.py
@@ -114,6 +114,10 @@
     )
     got_prev = lax.ppermute(to_next, "tile", [(i, i + 1) for i in range(ends)])
     got_next = lax.ppermute(to_prev, "tile", [(i + 1, i) for i in range(ends)])
+    grad_ms = jnp.einsum(
+        "mq,mrc->qrc", resp_basis, multi_resid.astype(f32), precision=highest
+    )
+    grad_ms, got_prev, got_next = lax.optimization_barrier((grad_ms, got_prev, got_next))
     coef_blurred = own_part + jnp.concatenate(
         [lax.slice_in_dim(got_prev, 0, half, axis=2), lax.slice_in_dim(got_next, 0, half, axis=2)],
         axis=2,
@@ -154,9 +158,6 @@
     resid_bands = lax.all_to_all(resid_split, "spec", split_axis=0, concat_axis=2, tiled=True)[0]
     hs_residual = resid_bands.transpose(0, 2, 1)
 
-    grad_ms = jnp.einsum(
-        "mq,mrc->qrc", resp_basis, multi_resid.astype(f32), precision=highest
-    )
     gradient = grad_hs + grad_ms
     z_next = (latent.astype(f32) - step_size * gradient).astype(bf16)
     return (z_next, hs_residual)

time: 101 us -> 101 us (level); the launches traced: 100 us -> 99.1 us
  waiting for transfers between devices: 34.4 us -> 32.4 us
  matrix products: 12.4 us -> 10.9 us
  local copies, waits for them, and re-layouts: 23.2 us -> 24.5 us
    ppermute x1, waiting for transfers between devices: 7.23 us -> 2.71 us  [shards(): got_prev = lax.ppermute(to_next, 'tile', [(i, i + 1) for i in range(ends)])]
    unnamed x30 -> x27, local copies, waits for them, and re-layouts: 13.6 us -> 17.1 us
    ppermute x1, starting transfers between devices: 2.1 us -> 5.18 us  [shards(): got_prev = lax.ppermute(to_next, 'tile', [(i, i + 1) for i in range(ends)])]
    ppermute x1, starting transfers between devices: 7.49 us -> 4.41 us  [shards(): got_next = lax.ppermute(to_prev, 'tile', [(i + 1, i) for i in range(ends)])]
    all_to_all x1, waiting for transfers between devices: 3.28 us -> 5.84 us  [shards(): lax.all_to_all(resid_split, 'spec', split_axis=0, concat_axis=2, tiled=True)]
    squeeze x1 -> x0, local copies, waits for them, and re-layouts: 2.41 us -> none  [shards(): lax.all_to_all(back_split, 'spec', split_axis=0, concat_axis=3, tiled=True)]
    dot_general x1, matrix products: 3.23 us -> 1.57 us  [shards(): jnp.einsum('mq,qrc->mrc', resp_basis, latent.astype(f32), precision=highest)]
    dot_general x1, matrix products: 3.43 us -> 1.78 us  [shards(): jnp.einsum('qrj,jc->qrc', rows_pixel, column_t, preferred_element_type=f32)]
  transfers between devices with their start and end apart: 6 -> 6, of which waited for: 6 -> 6; matrix products, arithmetic and copies ran while one was open for 18% -> 16% of each run, Pallas kernels for 0% -> 0%
where the time goes in v15:
time: 101 us; the launch traced here: 99.1 us
  waiting for transfers between devices  32.4 us (32%)
  starting transfers between devices  26.8 us (27%)
  local copies, waits for them, and re-layouts  24.5 us (24%)
  matrix products  10.9 us (11%)
  other arithmetic  2.77 us (3%)
  between operations  1.77 us (2%)
    unnamed x27, local copies, waits for them, and re-layouts  17.1 us
    ppermute x1, waiting for transfers between devices, shards(): got_next = lax.ppermute(to_prev, 'tile', [(i + 1, i) for i in range(ends)])  7.79 us
    all_to_all x1, waiting for transfers between devices, shards(): lax.all_to_all(back_split, 'spec', split_axis=0, concat_axis=3, tiled=True)  6.41 us
    all_to_all x1, waiting for transfers between devices, shards(): lax.all_to_all(resid_split, 'spec', split_axis=0, concat_axis=2, tiled=True)  5.84 us
    all_to_all x1, starting transfers between devices, shards(): lax.all_to_all(cols_done, 'spec', split_axis=0, concat_axis=3, tiled=True)  5.76 us
    all_to_all x1, waiting for transfers between devices, shards(): lax.all_to_all(obs_split, 'spec', split_axis=0, concat_axis=1, tiled=True)  5.61 us
    ppermute x1, starting transfers between devices, shards(): got_prev = lax.ppermute(to_next, 'tile', [(i, i + 1) for i in range(ends)])  5.18 us
    ppermute x1, starting transfers between devices, shards(): got_next = lax.ppermute(to_prev, 'tile', [(i + 1, i) for i in range(ends)])  4.41 us
  transfers between devices with their start and end apart: 6, of which 6 were waited for; matrix products, arithmetic and copies ran while one was open for 16% of the time, Pallas kernels for 0%

profile of v15, /device:TPU:24, one launch (start us, length us, event | category | flops | bytes accessed | tf_op | source)
XLA Modules:
  0.0 99.1 jit_solution(2215170727621795944)
XLA Ops:
  2.6 1.7 %reshape.88 = bf16[256,2044]{1,0:T(8,128)(2,1)S(1)} reshape(bf16[523264]{0:T(1024)(128)(2,1)S(1)} %slice.70) | data formatting | bytes 2093056 | tf_op jit(solution)/shard_map/reshape | solution.py:55
  4.3 1.4 %fusion.54 = bf16[16,16,16,32]{3,2,1,0:T(8,128)(2,1)S(1)} fusion(bf16[16,16,1024,1]{2,1,3,0:T(8,128)(2,1)S(1)} %bitcast.122, bf16[32,16,1024]{2,1,0:T(8,128)(2,1)S(1)} %copy-done.2), kind=kOutput, calls=%fused_computation.84 | convolution fusion | flops 268566528 | bytes 1835008 | tf_op jit(solution)/shard_map/qrc,sjc->sqjr/dot_general | solution.py:85
  5.8 1.7 %reshape.104 = bf16[16,2,4096]{2,1,0:T(2,128)(2,1)} reshape(bf16[16,16,16,32]{3,2,1,0:T(8,128)(2,1)S(1)} %fusion.54) | data formatting | bytes 524288
  7.4 5.8 %all-to-all-start = ((bf16[16,2,4096]{2,1,0:T(2,128)(2,1)}), bf16[16,2,4096]{2,1,0:T(2,128)(2,1)S(1)}, u32[]{:S(2)}, u32[]{:S(2)}) async-start(bf16[16,2,4096]{2,1,0:T(2,128)(2,1)} %reshape.104), calls=%async_computation | async-start | bytes 524288 | tf_op jit(solution)/shard_map/all_to_all | solution.py:91
  14.0 1.5 %copy.55 = bf16[14,64,256]{1,2,0:T(8,128)(2,1)S(1)} copy(bf16[14,64,256]{2,1,0:T(8,128)(2,1)} %param.8) | data formatting | bytes 917504 | tf_op args[3]
  17.2 4.0 %all-to-all-done = bf16[16,2,4096]{2,1,0:T(2,128)(2,1)S(1)} async-done(((bf16[16,2,4096]{2,1,0:T(2,128)(2,1)}), bf16[16,2,4096]{2,1,0:T(2,128)(2,1)S(1)}, u32[]{:S(2)}, u32[]{:S(2)}) %all-to-all-start) | async-done | bytes 262176 | tf_op jit(solution)/shard_map/all_to_all | solution.py:91
  21.3 3.6 %all-to-all-start.1 = ((bf16[16,2,7168]{2,1,0:T(2,128)(2,1)}), bf16[16,2,7168]{2,1,0:T(2,128)(2,1)S(1)}, u32[]{:S(2)}, u32[]{:S(2)}) async-start(bf16[16,2,7168]{2,1,0:T(2,128)(2,1)} %reshape.102), calls=%async_computation.1 | async-start | bytes 917504 | tf_op jit(solution)/shard_map/all_to_all | solution.py:94
  25.0 1.6 %fusion.5 = bf16[8,16,1024]{2,0,1:T(8,128)(2,1)S(1)} fusion(f32[8,32,1]{1,0,2:T(8,128)S(1)} %convolution_bitcast_fusion.2, bf16[32,16,1024]{2,1,0:T(8,128)(2,1)S(1)} %copy-done.2, bf16[8,16,1024]{2,1,0:T(8,128)(2,1)S(1)} %copy-done.5), kind=kOutput, calls=%fused_computation.10 | convolution fusion | flops 50724864 | bytes 1573888 | tf_op jit(solution)/shard_map/mq,qrc->mrc/dot_general | solution.py:96
  29.3 5.6 %all-to-all-done.1 = bf16[16,2,7168]{2,1,0:T(2,128)(2,1)S(1)} async-done(((bf16[16,2,7168]{2,1,0:T(2,128)(2,1)}), bf16[16,2,7168]{2,1,0:T(2,128)(2,1)S(1)}, u32[]{:S(2)}, u32[]{:S(2)}) %all-to-all-start.1) | async-done | bytes 458784 | tf_op jit(solution)/shard_map/all_to_all | solution.py:94
  37.0 5.2 %collective-permute-start = (f32[32,16,96]{2,1,0:T(8,128)S(1)}, f32[32,16,96]{2,1,0:T(8,128)S(1)}, u32[]{:S(2)}, u32[]{:S(2)}) collective-permute-start(f32[32,16,96]{2,1,0:T(8,128)S(1)} %pad_maximum_fusion), channel_id=1, source_target_pairs={{0,16},{16,32},{32,48},{48,64},{64,80},{80,96},{96,112},{112,128},... | collective-permute-start | bytes 589832 | tf_op jit(solution)/shard_map/ppermute | solution.py:115
  42.4 4.4 %collective-permute-start.1 = (f32[32,16,96]{2,1,0:T(8,128)S(1)}, f32[32,16,96]{2,1,0:T(8,128)S(1)}, u32[]{:S(2)}, u32[]{:S(2)}) collective-permute-start(f32[32,16,96]{2,1,0:T(8,128)S(1)} %pad_maximum_fusion.1), channel_id=1, source_target_pairs={{16,0},{32,16},{48,32},{64,48},{80,64},{96,80},{112,96},{128,112},... | collective-permute-start | bytes 589832 | tf_op jit(solution)/shard_map/ppermute | solution.py:116
  47.8 2.7 %collective-permute-done = f32[32,16,96]{2,1,0:T(8,128)S(1)} collective-permute-done((f32[32,16,96]{2,1,0:T(8,128)S(1)}, f32[32,16,96]{2,1,0:T(8,128)S(1)}, u32[]{:S(2)}, u32[]{:S(2)}) %collective-permute-start) | collective-permute-done | bytes 196640 | tf_op jit(solution)/shard_map/ppermute | solution.py:115
  50.5 7.8 %collective-permute-done.1 = f32[32,16,96]{2,1,0:T(8,128)S(1)} collective-permute-done((f32[32,16,96]{2,1,0:T(8,128)S(1)}, f32[32,16,96]{2,1,0:T(8,128)S(1)}, u32[]{:S(2)}, u32[]{:S(2)}) %collective-permute-start.1) | collective-permute-done | bytes 196640 | tf_op jit(solution)/shard_map/ppermute | solution.py:116
  61.7 1.5 %fusion.57 = bf16[16,16,16,32]{3,2,1,0:T(8,128)(2,1)} fusion(f32[16,16,32,16]{2,1,3,0:T(8,128)S(1)} %fusion.19, bf16[128,16,16,1]{0,2,3,1:T(8,128)(2,1)S(1)} %bitcast.121, f32[32,16,32]{2,0,1:T(8,128)S(1)} %copy.65, f32[32,16,64]{2,0,1:T(8,128)S(1)} %convolution_bitcast_fusion, f32[32,16,32]{2,0,1:T(8,128)S(1)} %copy.64), kind=kOutput, calls=%fused_computation.85 | convolution fusion | flops 34144256 | bytes 1114112 | tf_op jit(solution)/shard_map/qjk,ksr->sqrj/dot_general | solution.py:63
  63.2 3.1 %reshape.106 = bf16[16,2,4096]{2,1,0:T(2,128)(2,1)} reshape(bf16[16,16,16,32]{3,2,1,0:T(8,128)(2,1)} %fusion.57) | data formatting | bytes 524288
  66.3 3.7 %all-to-all-start.2 = ((bf16[16,2,4096]{2,1,0:T(2,128)(2,1)}), bf16[16,2,4096]{2,1,0:T(2,128)(2,1)S(1)}, u32[]{:S(2)}, u32[]{:S(2)}) async-start(bf16[16,2,4096]{2,1,0:T(2,128)(2,1)} %reshape.106), calls=%async_computation.2 | async-start | bytes 524288 | tf_op jit(solution)/shard_map/all_to_all | solution.py:153
  70.0 1.6 %copy.68 = bf16[224,16,64]{2,1,0:T(8,128)(2,1)} copy(bf16[224,16,64]{0,2,1:T(8,128)(2,1)S(1)} %fusion.4) | data formatting | bytes 917504 | tf_op jit(solution)/shard_map/convert_element_type | solution.py:128
  71.6 6.4 %all-to-all-done.2 = bf16[16,2,4096]{2,1,0:T(2,128)(2,1)S(1)} async-done(((bf16[16,2,4096]{2,1,0:T(2,128)(2,1)}), bf16[16,2,4096]{2,1,0:T(2,128)(2,1)S(1)}, u32[]{:S(2)}, u32[]{:S(2)}) %all-to-all-start.2) | async-done | bytes 262176 | tf_op jit(solution)/shard_map/all_to_all | solution.py:153
  78.5 2.8 %reshape.108 = bf16[16,2,7168]{2,1,0:T(2,128)(2,1)} reshape(bf16[16,14,16,64]{3,2,1,0:T(8,128)(2,1)} %bitcast.114) | data formatting | bytes 917504
  81.4 4.2 %all-to-all-start.3 = ((bf16[16,2,7168]{2,1,0:T(2,128)(2,1)}), bf16[16,2,7168]{2,1,0:T(2,128)(2,1)}, u32[]{:S(2)}, u32[]{:S(2)}) async-start(bf16[16,2,7168]{2,1,0:T(2,128)(2,1)} %reshape.108), calls=%async_computation.3 | async-start | bytes 917504 | tf_op jit(solution)/shard_map/all_to_all | solution.py:158
  85.6 1.8 %fusion.6 = f32[32,16,1024]{2,0,1:T(8,128)S(1)} fusion(bf16[32,16,256]{0,1,2:T(8,128)(2,1)S(1)} %bitcast.108, bf16[256,2044]{1,0:T(8,128)(2,1)} %copy-done.1), kind=kOutput, calls=%fused_computation.14 | convolution fusion | flops 268435456 | bytes 2883584 | tf_op jit(solution)/shard_map/qrj,jc->qrc/dot_general | solution.py:154
  88.4 1.5 %copy.70 = bf16[32,16,1024]{2,1,0:T(8,128)(2,1)} copy(bf16[32,16,1024]{2,0,1:T(8,128)(2,1)S(1)} %subtract_convert_fusion) | data formatting | bytes 2097152
  89.9 5.8 %all-to-all-done.3 = bf16[16,2,7168]{2,1,0:T(2,128)(2,1)} async-done(((bf16[16,2,7168]{2,1,0:T(2,128)(2,1)}), bf16[16,2,7168]{2,1,0:T(2,128)(2,1)}, u32[]{:S(2)}, u32[]{:S(2)}) %all-to-all-start.3) | async-done | bytes 458784 | tf_op jit(solution)/shard_map/all_to_all | solution.py:158
  95.8 2.1 %reshape.109 = bf16[16,14,16,64]{3,2,1,0:T(8,128)(2,1)S(1)} reshape(bf16[16,2,7168]{2,1,0:T(2,128)(2,1)} %all-to-all-done.3) | data formatting | bytes 917504
  (61 shorter events, 15.9 us)
Async XLA Ops:
  0.6 16.5 %copy-start = (bf16[224,32]{0,1:T(8,128)(2,1)S(1)}, bf16[224,32]{0,1:T(8,128)(2,1)}, u32[]{:S(2)}) copy-start(bf16[224,32]{0,1:T(8,128)(2,1)} %param.6) | copy-start | bytes 43012
  2.5 1.8 %copy-start.2 = (bf16[32,16,1024]{2,1,0:T(8,128)(2,1)S(1)}, bf16[32,16,1024]{2,1,0:T(8,128)(2,1)}, u32[]{:S(2)}) copy-start(bf16[32,16,1024]{2,1,0:T(8,128)(2,1)} %param.5) | copy-start | bytes 3145732
  4.3 1.5 %copy-start.1 = (bf16[256,2044]{1,0:T(8,128)(2,1)}, bf16[256,2044]{1,0:T(8,128)(2,1)S(1)}, u32[]{:S(2)}) copy-start(bf16[256,2044]{1,0:T(8,128)(2,1)S(1)} %reshape.88) | copy-start | bytes 3139588
  7.4 13.8 %all-to-all-start = ((bf16[16,2,4096]{2,1,0:T(2,128)(2,1)}), bf16[16,2,4096]{2,1,0:T(2,128)(2,1)S(1)}, u32[]{:S(2)}, u32[]{:S(2)}) async-start(bf16[16,2,4096]{2,1,0:T(2,128)(2,1)} %reshape.104), calls=%async_computation | async-start | bytes 524288 | tf_op jit(solution)/shard_map/all_to_all | solution.py:91
  14.0 3.0 %copy-start.4 = (bf16[128,764]{1,0:T(8,128)(2,1)}, bf16[128,764]{1,0:T(8,128)(2,1)S(1)}, u32[]{:S(2)}) copy-start(bf16[128,764]{1,0:T(8,128)(2,1)S(1)} %reshape.86) | copy-start | bytes 586756
  15.5 9.3 %copy-start.6 = (bf16[8,224]{1,0:T(8,128)(2,1)S(1)}, bf16[8,224]{1,0:T(8,128)(2,1)}, u32[]{:S(2)}) copy-start(bf16[8,224]{1,0:T(8,128)(2,1)} %param.7) | copy-start | bytes 10756
  15.7 9.3 %copy-start.5 = (bf16[8,16,1024]{2,1,0:T(8,128)(2,1)S(1)}, bf16[8,16,1024]{2,1,0:T(8,128)(2,1)}, u32[]{:S(2)}) copy-start(bf16[8,16,1024]{2,1,0:T(8,128)(2,1)} %param.9) | copy-start | bytes 786436
  21.3 13.7 %all-to-all-start.1 = ((bf16[16,2,7168]{2,1,0:T(2,128)(2,1)}), bf16[16,2,7168]{2,1,0:T(2,128)(2,1)S(1)}, u32[]{:S(2)}, u32[]{:S(2)}) async-start(bf16[16,2,7168]{2,1,0:T(2,128)(2,1)} %reshape.102), calls=%async_computation.1 | async-start | bytes 917504 | tf_op jit(solution)/shard_map/all_to_all | solution.py:94
  37.0 13.5 %collective-permute-start = (f32[32,16,96]{2,1,0:T(8,128)S(1)}, f32[32,16,96]{2,1,0:T(8,128)S(1)}, u32[]{:S(2)}, u32[]{:S(2)}) collective-permute-start(f32[32,16,96]{2,1,0:T(8,128)S(1)} %pad_maximum_fusion), channel_id=1, source_target_pairs={{0,16},{16,32},{32,48},{48,64},{64,80},{80,96},{96,112},{112,128},... | collective-permute-start | bytes 589832 | tf_op jit(solution)/shard_map/ppermute | solution.py:115
  42.4 15.9 %collective-permute-start.1 = (f32[32,16,96]{2,1,0:T(8,128)S(1)}, f32[32,16,96]{2,1,0:T(8,128)S(1)}, u32[]{:S(2)}, u32[]{:S(2)}) collective-permute-start(f32[32,16,96]{2,1,0:T(8,128)S(1)} %pad_maximum_fusion.1), channel_id=1, source_target_pairs={{16,0},{32,16},{48,32},{64,48},{80,64},{96,80},{112,96},{128,112},... | collective-permute-start | bytes 589832 | tf_op jit(solution)/shard_map/ppermute | solution.py:116
  66.3 11.7 %all-to-all-start.2 = ((bf16[16,2,4096]{2,1,0:T(2,128)(2,1)}), bf16[16,2,4096]{2,1,0:T(2,128)(2,1)S(1)}, u32[]{:S(2)}, u32[]{:S(2)}) async-start(bf16[16,2,4096]{2,1,0:T(2,128)(2,1)} %reshape.106), calls=%async_computation.2 | async-start | bytes 524288 | tf_op jit(solution)/shard_map/all_to_all | solution.py:153
  81.4 14.4 %all-to-all-start.3 = ((bf16[16,2,7168]{2,1,0:T(2,128)(2,1)}), bf16[16,2,7168]{2,1,0:T(2,128)(2,1)}, u32[]{:S(2)}, u32[]{:S(2)}) async-start(bf16[16,2,7168]{2,1,0:T(2,128)(2,1)} %reshape.108), calls=%async_computation.3 | async-start | bytes 917504 | tf_op jit(solution)/shard_map/all_to_all | solution.py:158
  85.6 1.8 %copy-start.3 = (bf16[32,16,1024]{2,1,0:T(8,128)(2,1)S(1)}, bf16[32,16,1024]{2,1,0:T(8,128)(2,1)}, u32[]{:S(2)}) copy-start(bf16[32,16,1024]{2,1,0:T(8,128)(2,1)} %param.5) | copy-start | bytes 3145732
